TPU v7x, 256 devices: a whole 4x4x8 slice. The times are simulated.
256 devices in a mesh: row: 16 (over z_lo, x, core), col: 16 (over z_hi, y).
Axes of the slice: x: 4, y: 4, z: 8 (z_hi: 4, z_lo: 2; z = z_hi * 2 + z_lo), core: 2. Of those that a mesh axis runs over, the one named last changes fastest.
Arguments:
- features: bfloat16 [65536, 512], P(('col', 'row')), may hold values from -6 to 6
- weight: bfloat16 [512, 512], replicated, may hold values from -0.25 to 0.25
- entry_values: bfloat16 [16, 16, 32, 128, 128], P('row', 'col'), may hold values from 0.0009994507 to 0.019897461
- block_rows: int32 [16, 16, 32], P('row', 'col'), may hold values from 0 to 31
- block_cols: int32 [16, 16, 32], P('row', 'col'), may hold values from 0 to 31
- entry_counts: int32 [16, 16], P('row', 'col'), may hold values from 8 to 32, as said below
- cotangent: bfloat16 [65536, 512], P(('row', 'col')), may hold values from -1.5 to 1.5
Outputs:
- output: bfloat16 [65536, 512], P(('row', 'col'))
- grad_features: bfloat16 [65536, 512], P(('col', 'row'))
- grad_weight: float32 [512, 512], replicated
Inputs may be any that keep to these rules, and one draw needn't show every extreme that they name: `entry_counts`: each grid cell has at least 8 live slots; at least one cell has all 32 live.
All inputs are finite; a program needn't handle non-finite values.
Results may differ from a plain program's by a relative error of at most 0.022.
Values may be sent and summed in bfloat16 or wider, within the bound.
No kernel may reach another device: no remote copies, remote signals or barrier semaphores. Data moves between devices by JAX's collectives and lax.ppermute only.
A program may use at most 128 MiB of HBM per device.

v0:
```python
import jax
import jax.numpy as jnp
from jax import lax
from jax.sharding import PartitionSpec as P


def block_terms(values, source_ids, target_ids, live_count, source, target_blocks, transpose):
    entry_total = values.shape[0]
    block_side = values.shape[1]
    feature_count = source.shape[1]
    group_size = min(32, entry_total)
    source_tiles = source.reshape(-1, block_side, feature_count)

    def one_group(group_index, running):
        first_entry = group_index * group_size
        tiles = jnp.take(source_tiles, source_ids, axis=0)
        if transpose:
            products = jnp.einsum("kba,kbf->kaf", values, tiles, preferred_element_type=jnp.float32)
        else:
            products = jnp.einsum("kab,kbf->kaf", values, tiles, preferred_element_type=jnp.float32)
        alive_mask = (first_entry + jnp.arange(group_size) < live_count).astype(jnp.float32)
        return running.at[target_ids].add(products * alive_mask[:, None, None])

    zero_sum = jnp.zeros((target_blocks, block_side, feature_count), jnp.float32)
    trip_count = entry_total // group_size
    running = lax.fori_loop(0, trip_count, one_group, zero_sum)
    return running.reshape(target_blocks * block_side, feature_count)


def silu_slope(summed):
    sigmoid_value = jax.nn.sigmoid(summed)
    return sigmoid_value * (1.0 + summed * (1.0 - sigmoid_value))


def shards(features, weight, entry_values, block_rows, block_cols, entry_counts, cotangent):
    values = entry_values[0, 0]
    row_ids = block_rows[0, 0]
    col_ids = block_cols[0, 0]
    live_count = entry_counts[0, 0]
    local_rows = features.shape[0]
    block_side = values.shape[1]
    row_span = lax.axis_size("col") * local_rows
    col_span = lax.axis_size("row") * local_rows
    projected = jnp.dot(features, weight, preferred_element_type=jnp.float32).astype(jnp.bfloat16)
    panel = lax.all_gather(projected, "row", axis=0, tiled=True)
    forward_terms = block_terms(
        values, col_ids, row_ids, live_count, panel, row_span // block_side, False
    )
    summed = lax.psum(forward_terms.astype(jnp.bfloat16), "col").astype(jnp.float32)
    position = lax.axis_index("col") * local_rows
    own_sum = lax.dynamic_slice_in_dim(summed, position, local_rows, 0)
    output = jax.nn.silu(own_sum).astype(jnp.bfloat16)
    incoming = lax.all_gather(cotangent, "col", axis=0, tiled=True)
    upstream = (incoming.astype(jnp.float32) * silu_slope(summed)).astype(jnp.bfloat16)
    backward_terms = block_terms(
        values, row_ids, col_ids, live_count, upstream, col_span // block_side, True
    )
    grad_projected = lax.psum_scatter(
        backward_terms.astype(jnp.bfloat16), "row", scatter_dimension=0, tiled=True
    )
    weight_term = lax.dot_general(
        features, grad_projected, (((0,), (0,)), ((), ())), preferred_element_type=jnp.float32
    )
    grad_weight = lax.psum(weight_term, ("row", "col"))
    grad_features = lax.dot_general(
        grad_projected, weight, (((1,), (1,)), ((), ())), preferred_element_type=jnp.float32
    ).astype(jnp.bfloat16)
    return (output, grad_features, grad_weight)


def solution(mesh):
    placed = (
        P(("col", "row"), None),
        P(),
        P("row", "col", None, None, None),
        P("row", "col", None),
        P("row", "col", None),
        P("row", "col"),
        P(("row", "col"), None),
    )
    return jax.shard_map(
        shards,
        mesh=mesh,
        in_specs=placed,
        out_specs=(P(("row", "col"), None), P(("col", "row"), None), P()),
        check_vma=False,
    )
```

profile of v0, /device:TPU:2, one launch (start us, length us, event | category | flops | bytes accessed | tf_op | source)
XLA Modules:
  0.0 751.4 jit_solution(11538004060448155654)
XLA Ops:
  7.2 0.0 copy-start
  7.2 0.0 all-gather.3.cloned.1.call-start
  7.2 2.2 convolution_convert_fusion.1
  9.4 0.0 all-gather.3.cloned.1.call-update
  9.5 0.0 all-gather.5.cloned.1.call-start
  9.5 0.7 all-gather.5.cloned.1.call-update
  10.2 0.0 all-reduce.3.cloned.1.call-start
  10.9 0.7 compare_select_fusion.1
  11.6 0.7 fusion.14
  12.2 0.7 compare_and_fusion.1
  12.9 39.9 %all-gather.3.cloned.1.call-done = bf16[4096,512]{1,0:T(8,128)(2,1)} async-done(((bf16[256,512]{1,0:T(8,128)(2,1)}), bf16[4096,512]{1,0:T(8,128)(2,1)}) %all-gather.3.cloned.1.call-update) | async-done | bytes 4194320 | tf_op jit(solution)/shard_map/all_gather | solution.py:45
  52.8 5.0 gather_fusion
  57.8 0.0 copy-done
  57.8 7.1 multiply_bitcast_fusion.1
  64.9 9.1 %copy.14 = f32[32,128,512]{2,1,0:T(8,128)} copy(f32[32,128,512]{1,2,0:T(8,128)} %multiply_bitcast_fusion.1) | data formatting | bytes 16777216 | tf_op jit(solution)/shard_map/while/body/eval_jaxpr/mul | solution.py:22
  74.0 4.3 broadcast.57.clone
  78.2 18.5 %scatter_fusion = f32[32,128,512]{2,1,0:T(8,128)} fusion(f32[32,128,512]{2,1,0:T(8,128)} %broadcast.57.clone, s32[32]{0:T(128)S(1)} %fusion.14, f32[32,128,512]{2,1,0:T(8,128)} %copy.14), kind=kCustom, calls=%fused_computation.2 | custom fusion | flops 2097152 | bytes 25165952 | tf_op jit(solution)/shard_map/while/body/eval_jaxpr/scatter-add | solution.py:22
  96.8 0.0 copy-start.5
  96.8 0.0 copy-start.4
  96.8 6.0 convert_element_type.42
  102.7 0.0 all-reduce.3.cloned.1.call-update
  102.8 0.0 reduce-scatter.2.cloned.1.call-start
  102.8 0.0 copy-done.5
  102.9 0.0 copy-done.4
  102.9 27.8 %all-gather.5.cloned.1.call-done = bf16[4096,512]{1,0:T(8,128)(2,1)} async-done(((bf16[256,512]{1,0:T(8,128)(2,1)}), bf16[4096,512]{1,0:T(8,128)(2,1)}) %all-gather.5.cloned.1.call-update) | async-done | bytes 4194320 | tf_op jit(solution)/shard_map/all_gather | solution.py:53
  130.6 224.6 %all-reduce.3.cloned.1.call-done = bf16[4096,512]{1,0:T(8,128)(2,1)} async-done(((bf16[4096,512]{1,0:T(8,128)(2,1)}), bf16[4096,512]{1,0:T(8,128)(2,1)}) %all-reduce.3.cloned.1.call-update) | async-done | bytes 4194320 | tf_op jit(solution)/shard_map/psum | solution.py:49
  355.2 7.0 multiply_convert_fusion
  362.2 5.0 gather_fusion.1
  367.1 7.1 multiply_bitcast_fusion
  374.3 9.0 %copy.16 = f32[32,128,512]{2,1,0:T(8,128)} copy(f32[32,128,512]{1,2,0:T(8,128)} %multiply_bitcast_fusion) | data formatting | bytes 16777216 | tf_op jit(solution)/shard_map/while/body/eval_jaxpr/mul | solution.py:22
  383.3 4.3 broadcast.57
  387.6 18.5 %scatter_fusion.1 = f32[32,128,512]{2,1,0:T(8,128)} fusion(f32[32,128,512]{2,1,0:T(8,128)} %broadcast.57, s32[32]{0:T(128)S(1)} %fusion.15, f32[32,128,512]{2,1,0:T(8,128)} %copy.16), kind=kCustom, calls=%fused_computation.3 | custom fusion | flops 2097152 | bytes 25165952 | tf_op jit(solution)/shard_map/while/body/eval_jaxpr/scatter-add | solution.py:22
  406.1 0.0 copy-start.2
  406.1 6.0 convert_element_type.48
  412.1 0.0 reduce-scatter.2.cloned.1.call-update
  412.1 0.0 copy-start.1
  412.1 0.0 all-reduce.5.cloned.1.call-start
  412.2 63.3 %reduce-scatter.2.cloned.1.call-done = bf16[256,512]{1,0:T(8,128)(2,1)} async-done(((bf16[4096,512]{1,0:T(8,128)(2,1)}), bf16[256,512]{1,0:T(8,128)(2,1)}) %reduce-scatter.2.cloned.1.call-update) | async-done | bytes 262160 | tf_op jit(solution)/shard_map/reduce_scatter | solution.py:58
  475.4 0.0 copy-done.2
  475.4 2.3 convolution_bitcast_fusion
  477.8 0.0 all-reduce.5.cloned.1.call-update
  477.8 3.4 convert_element_type.44
  481.2 0.9 multiply_convert_fusion.1
  482.0 0.0 copy-done.1
  482.0 0.0 copy-done.3
  482.0 1.0 convolution_convert_fusion
  483.1 259.2 %all-reduce.5.cloned.1.call-done = f32[512,512]{0,1:T(8,128)} async-done(((f32[512,512]{0,1:T(8,128)}), f32[512,512]{0,1:T(8,128)}) %all-reduce.5.cloned.1.call-update) | async-done | bytes 1048592 | tf_op jit(solution)/shard_map/psum | solution.py:64
  742.3 2.5 copy.17
  (6 shorter events, 0.0 us)
Async XLA Ops:
  7.2 50.6 %copy-start = (bf16[1,1,32,128,128]{4,3,2,1,0:T(8,128)(2,1)S(1)}, bf16[1,1,32,128,128]{4,3,2,1,0:T(8,128)(2,1)}, u32[]{:S(2)}) copy-start(bf16[1,1,32,128,128]{4,3,2,1,0:T(8,128)(2,1)} %param.11) | copy-start | bytes 3145732
  7.2 45.6 %all-gather.3.cloned.1.call-start = ((), (), s32[]{:S(2)}) async-start(), calls=%async_computation.1 | async-start | bytes 4456448 | tf_op jit(solution)/shard_map/all_gather | solution.py:45
  9.5 121.2 %all-gather.5.cloned.1.call-start = ((), (), s32[]{:S(2)}) async-start(), calls=%async_computation.3 | async-start | bytes 4456448 | tf_op jit(solution)/shard_map/all_gather | solution.py:53
  10.2 345.0 %all-reduce.3.cloned.1.call-start = ((), (), s32[]{:S(2)}) async-start(), calls=%async_computation.2 | async-start | bytes 8388608 | tf_op jit(solution)/shard_map/psum | solution.py:49
  96.8 6.1 copy-start.5
  96.8 6.1 copy-start.4
  102.8 372.7 %reduce-scatter.2.cloned.1.call-start = ((), (), s32[]{:S(2)}) async-start(), calls=%async_computation.4 | async-start | bytes 4456448 | tf_op jit(solution)/shard_map/reduce_scatter | solution.py:58
  406.1 69.3 %copy-start.2 = (bf16[256,512]{1,0:T(8,128)(2,1)S(1)}, bf16[256,512]{1,0:T(8,128)(2,1)}, u32[]{:S(2)}) copy-start(bf16[256,512]{1,0:T(8,128)(2,1)} %param.9) | copy-start | bytes 786436
  412.1 69.9 %copy-start.1 = (bf16[512,512]{1,0:T(8,128)(2,1)S(1)}, bf16[512,512]{1,0:T(8,128)(2,1)}, u32[]{:S(2)}) copy-start(bf16[512,512]{1,0:T(8,128)(2,1)} %param.10) | copy-start | bytes 1572868
  412.1 330.2 %all-reduce.5.cloned.1.call-start = ((), (), s32[]{:S(2)}) async-start(), calls=%async_computation.5 | async-start | bytes 2097152 | tf_op jit(solution)/shard_map/psum | solution.py:64
  475.4 6.6 copy-start.3
Sparse Core Ops, SparseCore 0:
  10.4 42.3 all-gather.2
  55.2 75.3 all-gather.4
  133.3 221.8 all-reduce.2
  412.2 63.1 reduce-scatter.1
  481.3 260.9 all-reduce.4
where the time goes:
time: 752 us; the launch traced here: 751 us
  waiting for transfers between devices  615 us (82%)
  other arithmetic  62.2 us (8%)
  local copies, waits for them, and re-layouts  39.2 us (5%)
  matrix products  19.8 us (3%)
  between operations  14.5 us (2%)
    psum x1, waiting for transfers between devices, shards(): grad_weight = lax.psum(weight_term, ('row', 'col'))  259 us
    psum x1, waiting for transfers between devices, shards(): lax.psum(forward_terms.astype(jnp.bfloat16), 'col').astype(jnp.float32)  225 us
    reduce_scatter x1, waiting for transfers between devices, shards(): lax.psum_scatter(backward_terms.astype(jnp.bfloat16), 'row', scatter_dime...  63.3 us
    all_gather x1, waiting for transfers between devices, shards(): panel = lax.all_gather(projected, 'row', axis=0, tiled=True)  39.9 us
    scatter-add x2, other arithmetic, one_group(): return running.at[target_ids].add(products * alive_mask[:, None, None])  37 us
    all_gather x1, waiting for transfers between devices, shards(): incoming = lax.all_gather(cotangent, 'col', axis=0, tiled=True)  27.8 us
    mul x2, local copies, waits for them, and re-layouts, one_group(): return running.at[target_ids].add(products * alive_mask[:, None, None])  18.1 us
  transfers between devices with their start and end apart: 5, of which 5 were waited for; matrix products, arithmetic and copies ran while one was open for 8% of the time, Pallas kernels for 0%

commit v1 on v0

--- a/solution.py
+++ b/solution.py
@@ -46,12 +46,12 @@
     forward_terms = block_terms(
         values, col_ids, row_ids, live_count, panel, row_span // block_side, False
     )
-    summed = lax.psum(forward_terms.astype(jnp.bfloat16), "col").astype(jnp.float32)
-    position = lax.axis_index("col") * local_rows
-    own_sum = lax.dynamic_slice_in_dim(summed, position, local_rows, 0)
+    own_sum = lax.psum_scatter(
+        forward_terms.astype(jnp.bfloat16), "col", scatter_dimension=0, tiled=True
+    ).astype(jnp.float32)
     output = jax.nn.silu(own_sum).astype(jnp.bfloat16)
-    incoming = lax.all_gather(cotangent, "col", axis=0, tiled=True)
-    upstream = (incoming.astype(jnp.float32) * silu_slope(summed)).astype(jnp.bfloat16)
+    own_upstream = (cotangent.astype(jnp.float32) * silu_slope(own_sum)).astype(jnp.bfloat16)
+    upstream = lax.all_gather(own_upstream, "col", axis=0, tiled=True)
     backward_terms = block_terms(
         values, row_ids, col_ids, live_count, upstream, col_span // block_side, True
     )
@@ -61,7 +61,9 @@
     weight_term = lax.dot_general(
         features, grad_projected, (((0,), (0,)), ((), ())), preferred_element_type=jnp.float32
     )
-    grad_weight = lax.psum(weight_term, ("row", "col"))
+    weight_part = lax.psum_scatter(weight_term, "row", scatter_dimension=0, tiled=True)
+    weight_part = lax.psum(weight_part, "col")
+    grad_weight = lax.all_gather(weight_part, "row", axis=0, tiled=True)
     grad_features = lax.dot_general(
         grad_projected, weight, (((1,), (1,)), ((), ())), preferred_element_type=jnp.float32
     ).astype(jnp.bfloat16)

time: 752 us -> 677 us (0.900)
  waiting for transfers between devices: 615 us -> 543 us
  other arithmetic: 62.2 us -> 53.2 us
    psum x2 -> x1, waiting for transfers between devices: 484 us -> 169 us  [shards(): weight_part = lax.psum(weight_part, 'col')]
    reduce_scatter x0 -> x1, waiting for transfers between devices: none -> 97.1 us  [shards(): lax.psum_scatter(forward_terms.astype(jnp.bfloat16), 'col', scatter_dimen...]
    all_gather x1 -> x2, waiting for transfers between devices: 27.8 us -> 106 us  [the longest x1 73.7 us: shards(): upstream = lax.all_gather(own_upstream, 'col', axis=0, tiled=True)]
    unnamed x5 -> x8, waiting for transfers between devices: 0.76 us -> 63.7 us
    convert_element_type x3 -> x1, other arithmetic: 11.2 us -> 1.99 us  [shards(): (cotangent.astype(jnp.float32) * silu_slope(own_sum)).astype(jnp.bfloat16)]
  transfers between devices with their start and end apart: 5 -> 7, of which waited for: 5 -> 7; matrix products, arithmetic and copies ran while one was open for 8% -> 0% of each run, Pallas kernels for 0% -> 0%
where the time goes in v1:
time: 677 us; the launch traced here: 674 us
  waiting for transfers between devices  543 us (80%)
  other arithmetic  53.2 us (8%)
  local copies, waits for them, and re-layouts  43.5 us (6%)
  matrix products  18.9 us (3%)
  between operations  14.9 us (2%)
    psum x1, waiting for transfers between devices, shards(): weight_part = lax.psum(weight_part, 'col')  169 us
    reduce_scatter x1, waiting for transfers between devices, shards(): lax.psum_scatter(forward_terms.astype(jnp.bfloat16), 'col', scatter_dimen...  97.1 us
    all_gather x1, waiting for transfers between devices, shards(): upstream = lax.all_gather(own_upstream, 'col', axis=0, tiled=True)  73.7 us
    reduce_scatter x1, waiting for transfers between devices, shards(): lax.psum_scatter(backward_terms.astype(jnp.bfloat16), 'row', scatter_dime...  66.4 us
    unnamed x8, waiting for transfers between devices  63.7 us
    all_gather x1, waiting for transfers between devices, shards(): panel = lax.all_gather(projected, 'row', axis=0, tiled=True)  40.6 us
    scatter-add x2, other arithmetic, one_group(): return running.at[target_ids].add(products * alive_mask[:, None, None])  37.3 us
    all_gather x1, waiting for transfers between devices, shards(): grad_weight = lax.all_gather(weight_part, 'row', axis=0, tiled=True)  32.7 us
  transfers between devices with their start and end apart: 7, of which 7 were waited for; matrix products, arithmetic and copies ran while one was open for 0% of the time, Pallas kernels for 0%

profile of v1, /device:TPU:2, one launch (start us, length us, event | category | flops | bytes accessed | tf_op | source)
XLA Modules:
  0.0 673.9 jit_solution(13709387366234247826)
XLA Ops:
  7.2 0.0 copy-start
  7.2 0.0 all-gather.4.cloned.1.call-start
  7.2 2.2 convolution_convert_fusion.1
  9.4 0.0 all-gather.4.cloned.1.call-update
  9.5 0.0 reduce-scatter.6.cloned.1.call-start
  10.2 0.7 compare_select_fusion.1
  10.8 0.7 fusion.22
  11.5 0.7 compare_and_fusion.1
  12.1 40.6 %all-gather.4.cloned.1.call-done = bf16[4096,512]{1,0:T(8,128)(2,1)} async-done(((bf16[256,512]{1,0:T(8,128)(2,1)}), bf16[4096,512]{1,0:T(8,128)(2,1)}) %all-gather.4.cloned.1.call-update) | async-done | bytes 4194320 | tf_op jit(solution)/shard_map/all_gather | solution.py:45
  52.8 4.9 gather_fusion
  57.7 7.1 %multiply_bitcast_fusion.1 = f32[32,128,512]{1,2,0:T(8,128)} fusion(f32[32]{0:T(128)S(1)} %get-tuple-element.53, bf16[32,128,512]{2,1,0:T(8,128)(2,1)} %gather_fusion, pred[32]{0:T(512)(128)(4,1)S(1)} %get-tuple-element.52, bf16[1,1,32,128,128]{4,3,2,1,0:T(8,128)(2,1)S(1)} %copy-done), kind=kOutput, calls=%fused_computation.5 | convolution fusion | flops 541065216 | bytes 13631648 | tf_op jit(solution)/shard_map/while/body/eval_jaxpr/kab,kbf->kaf/dot_general | solution.py:20
  64.9 9.0 %copy.19 = f32[32,128,512]{2,1,0:T(8,128)} copy(f32[32,128,512]{1,2,0:T(8,128)} %multiply_bitcast_fusion.1) | data formatting | bytes 16777216 | tf_op jit(solution)/shard_map/while/body/eval_jaxpr/mul | solution.py:22
  73.9 4.3 broadcast.55.clone
  78.2 18.8 %scatter_fusion = f32[32,128,512]{2,1,0:T(8,128)} fusion(f32[32,128,512]{2,1,0:T(8,128)} %broadcast.55.clone, s32[32]{0:T(128)S(1)} %fusion.22, f32[32,128,512]{2,1,0:T(8,128)} %copy.19), kind=kCustom, calls=%fused_computation.2 | custom fusion | flops 2097152 | bytes 25165952 | tf_op jit(solution)/shard_map/while/body/eval_jaxpr/scatter-add | solution.py:22
  97.0 6.0 convert_element_type.42
  103.0 0.0 reduce-scatter.6.cloned.1.call-update
  103.0 0.0 all-gather.6.cloned.1.call-start
  103.0 97.1 %reduce-scatter.6.cloned.1.call-done = bf16[256,512]{1,0:T(8,128)(2,1)} async-done(((bf16[4096,512]{1,0:T(8,128)(2,1)}), bf16[256,512]{1,0:T(8,128)(2,1)}) %reduce-scatter.6.cloned.1.call-update) | async-done | bytes 262160 | tf_op jit(solution)/shard_map/reduce_scatter | solution.py:49
  200.1 0.0 copy-done.5
  200.1 2.0 fusion.21
  202.1 0.0 all-gather.6.cloned.1.call-update
  202.1 0.0 reduce-scatter.8.cloned.1.call-start
  202.3 73.7 %all-gather.6.cloned.1.call-done = bf16[4096,512]{1,0:T(8,128)(2,1)} async-done(((bf16[256,512]{1,0:T(8,128)(2,1)}), bf16[4096,512]{1,0:T(8,128)(2,1)}) %all-gather.6.cloned.1.call-update) | async-done | bytes 4194320 | tf_op jit(solution)/shard_map/all_gather | solution.py:54
  276.0 4.9 gather_fusion.1
  280.9 7.1 %multiply_bitcast_fusion = f32[32,128,512]{1,2,0:T(8,128)} fusion(f32[32]{0:T(128)S(1)} %get-tuple-element.53, bf16[32,128,512]{2,1,0:T(8,128)(2,1)} %gather_fusion.1, pred[32]{0:T(512)(128)(4,1)S(1)} %compare_and_fusion, bf16[1,1,32,128,128]{4,3,2,1,0:T(8,128)(2,1)S(1)} %copy-done), kind=kOutput, calls=%fused_computation.4 | convolution fusion | flops 541065216 | bytes 13631648 | tf_op jit(solution)/shard_map/while/body/eval_jaxpr/kba,kbf->kaf/dot_general | solution.py:18
  288.1 9.0 %copy.21 = f32[32,128,512]{2,1,0:T(8,128)} copy(f32[32,128,512]{1,2,0:T(8,128)} %multiply_bitcast_fusion) | data formatting | bytes 16777216 | tf_op jit(solution)/shard_map/while/body/eval_jaxpr/mul | solution.py:22
  297.1 4.3 broadcast.55
  301.4 18.5 %scatter_fusion.1 = f32[32,128,512]{2,1,0:T(8,128)} fusion(f32[32,128,512]{2,1,0:T(8,128)} %broadcast.55, s32[32]{0:T(128)S(1)} %fusion.23, f32[32,128,512]{2,1,0:T(8,128)} %copy.21), kind=kCustom, calls=%fused_computation.3 | custom fusion | flops 2097152 | bytes 25165952 | tf_op jit(solution)/shard_map/while/body/eval_jaxpr/scatter-add | solution.py:22
  319.9 6.0 convert_element_type.48
  325.9 0.0 reduce-scatter.8.cloned.1.call-update
  325.9 0.0 copy-start.1
  325.9 0.0 reduce-scatter.10.cloned.1.call-start
  326.0 66.4 %reduce-scatter.8.cloned.1.call-done = bf16[256,512]{1,0:T(8,128)(2,1)} async-done(((bf16[4096,512]{1,0:T(8,128)(2,1)}), bf16[256,512]{1,0:T(8,128)(2,1)}) %reduce-scatter.8.cloned.1.call-update) | async-done | bytes 262160 | tf_op jit(solution)/shard_map/reduce_scatter | solution.py:58
  392.3 1.3 convolution_bitcast_fusion
  393.7 1.3 copy.25
  395.0 0.0 reduce-scatter.10.cloned.1.call-update
  395.0 0.0 all-reduce.2.cloned.1.call-start
  395.1 63.5 %reduce-scatter.10.cloned.1.call-done = f32[32,512]{1,0:T(8,128)} async-done(((f32[512,512]{1,0:T(8,128)}), f32[32,512]{1,0:T(8,128)}) %reduce-scatter.10.cloned.1.call-update) | async-done | bytes 65552
  458.6 1.7 copy.26
  460.3 0.0 all-reduce.2.cloned.1.call-update
  460.3 0.0 all-gather.8.cloned.1.call-start
  460.4 169.0 %all-reduce.2.cloned.1.call-done = f32[32,512]{0,1:T(8,128)} async-done(((f32[32,512]{0,1:T(8,128)}), f32[32,512]{0,1:T(8,128)}) %all-reduce.2.cloned.1.call-update) | async-done | bytes 65552 | tf_op jit(solution)/shard_map/psum | solution.py:65
  629.3 1.7 copy.22
  631.0 0.0 all-gather.8.cloned.1.call-update
  631.0 0.0 copy-done.2
  631.0 1.0 convolution_convert_fusion
  632.1 32.7 %all-gather.8.cloned.1.call-done = f32[512,512]{1,0:T(8,128)} async-done(((f32[32,512]{1,0:T(8,128)}), f32[512,512]{1,0:T(8,128)}) %all-gather.8.cloned.1.call-update) | async-done | bytes 1048592 | tf_op jit(solution)/shard_map/all_gather | solution.py:66
  664.8 2.3 copy.32
  (17 shorter events, 0.1 us)
Async XLA Ops:
  7.2 50.6 %copy-start = (bf16[1,1,32,128,128]{4,3,2,1,0:T(8,128)(2,1)S(1)}, bf16[1,1,32,128,128]{4,3,2,1,0:T(8,128)(2,1)}, u32[]{:S(2)}) copy-start(bf16[1,1,32,128,128]{4,3,2,1,0:T(8,128)(2,1)} %param.11) | copy-start | bytes 3145732
  7.2 45.6 %all-gather.4.cloned.1.call-start = ((), (), s32[]{:S(2)}) async-start(), calls=%async_computation.3 | async-start | bytes 4456448 | tf_op jit(solution)/shard_map/all_gather | solution.py:45
  9.5 190.7 %reduce-scatter.6.cloned.1.call-start = ((), (), s32[]{:S(2)}) async-start(), calls=%async_computation.4 | async-start | bytes 4456448 | tf_op jit(solution)/shard_map/reduce_scatter | solution.py:49
  103.0 97.2 %copy-start.5 = (bf16[256,512]{1,0:T(8,128)(2,1)S(1)}, bf16[256,512]{1,0:T(8,128)(2,1)}, u32[]{:S(2)}) copy-start(bf16[256,512]{1,0:T(8,128)(2,1)} %param.15) | copy-start | bytes 786436
  103.0 99.2 %copy-start.7 = (s32[1,1,32]{2,1,0:T(1,128)S(1)}, s32[1,1,32]{2,1,0:T(1,128)}, u32[]{:S(2)}) copy-start(s32[1,1,32]{2,1,0:T(1,128)} %param.12) | copy-start | bytes 388
  103.0 99.3 %copy-start.6 = (s32[1,1,32]{2,1,0:T(1,128)S(1)}, s32[1,1,32]{2,1,0:T(1,128)}, u32[]{:S(2)}) copy-start(s32[1,1,32]{2,1,0:T(1,128)} %param.13) | copy-start | bytes 388
  103.0 173.0 %all-gather.6.cloned.1.call-start = ((), (), s32[]{:S(2)}) async-start(), calls=%async_computation.5 | async-start | bytes 4456448 | tf_op jit(solution)/shard_map/all_gather | solution.py:54
  202.1 190.2 %reduce-scatter.8.cloned.1.call-start = ((), (), s32[]{:S(2)}) async-start(), calls=%async_computation.6 | async-start | bytes 4456448 | tf_op jit(solution)/shard_map/reduce_scatter | solution.py:58
  325.9 66.5 %copy-start.3 = (bf16[256,512]{1,0:T(8,128)(2,1)S(1)}, bf16[256,512]{1,0:T(8,128)(2,1)}, u32[]{:S(2)}) copy-start(bf16[256,512]{1,0:T(8,128)(2,1)} %param.9) | copy-start | bytes 786436
  325.9 305.2 %copy-start.2 = (bf16[512,512]{1,0:T(8,128)(2,1)S(1)}, bf16[512,512]{1,0:T(8,128)(2,1)}, u32[]{:S(2)}) copy-start(bf16[512,512]{1,0:T(8,128)(2,1)} %param.10) | copy-start | bytes 1572868
  325.9 341.2 %copy-start.1 = (bf16[1,1,32,128,128]{4,3,2,1,0:T(8,128)(2,1)S(1)}, bf16[1,1,32,128,128]{4,3,2,1,0:T(8,128)(2,1)}, u32[]{:S(2)}) copy-start(bf16[1,1,32,128,128]{4,3,2,1,0:T(8,128)(2,1)} %param.11) | copy-start | bytes 3145732
  325.9 132.7 %reduce-scatter.10.cloned.1.call-start = ((), (), s32[]{:S(2)}) async-start(), calls=%async_computation.9 | async-start | bytes 1114112
  392.3 238.7 %copy-start.4 = (bf16[256,512]{1,0:T(8,128)(2,1)S(1)}, bf16[256,512]{1,0:T(8,128)(2,1)}, u32[]{:S(2)}) copy-start(bf16[256,512]{1,0:T(8,128)(2,1)} %reduce-scatter.8.cloned.1.call-done) | copy-start | bytes 786436
  395.0 234.3 %all-reduce.2.cloned.1.call-start = ((), (), s32[]{:S(2)}) async-start(), calls=%async_computation.7 | async-start | bytes 524288 | tf_op jit(solution)/shard_map/psum | solution.py:65
  460.3 204.5 %all-gather.8.cloned.1.call-start = ((), (), s32[]{:S(2)}) async-start(), calls=%async_computation.8 | async-start | bytes 1114112 | tf_op jit(solution)/shard_map/all_gather | solution.py:66
Sparse Core Ops, SparseCore 0:
  10.4 42.3 all-gather.3
  103.1 96.9 reduce-scatter.5
  203.1 72.7 all-gather.5
  326.0 66.2 reduce-scatter.7
  395.3 63.2 reduce-scatter.9
  461.6 167.6 all-reduce.1
  631.7 33.0 all-gather.7

commit v2 on v1

--- a/solution.py
+++ b/solution.py
@@ -27,6 +27,20 @@
     return running.reshape(target_blocks * block_side, feature_count)
 
 
+def exchange_sum(parts, axis_name):
+    count = lax.axis_size(axis_name)
+    pieces = parts.reshape((count, -1) + parts.shape[1:])
+    pieces = lax.all_to_all(pieces, axis_name, 0, 0, tiled=False)
+    return pieces.astype(jnp.float32).sum(0)
+
+
+def exchange_gather(part, axis_name):
+    count = lax.axis_size(axis_name)
+    pieces = jnp.broadcast_to(part[None], (count,) + part.shape)
+    pieces = lax.all_to_all(pieces, axis_name, 0, 0, tiled=False)
+    return pieces.reshape((-1,) + part.shape[1:])
+
+
 def silu_slope(summed):
     sigmoid_value = jax.nn.sigmoid(summed)
     return sigmoid_value * (1.0 + summed * (1.0 - sigmoid_value))
@@ -46,24 +60,19 @@
     forward_terms = block_terms(
         values, col_ids, row_ids, live_count, panel, row_span // block_side, False
     )
-    own_sum = lax.psum_scatter(
-        forward_terms.astype(jnp.bfloat16), "col", scatter_dimension=0, tiled=True
-    ).astype(jnp.float32)
+    own_sum = exchange_sum(forward_terms.astype(jnp.bfloat16), "col")
     output = jax.nn.silu(own_sum).astype(jnp.bfloat16)
     own_upstream = (cotangent.astype(jnp.float32) * silu_slope(own_sum)).astype(jnp.bfloat16)
     upstream = lax.all_gather(own_upstream, "col", axis=0, tiled=True)
     backward_terms = block_terms(
         values, row_ids, col_ids, live_count, upstream, col_span // block_side, True
     )
-    grad_projected = lax.psum_scatter(
-        backward_terms.astype(jnp.bfloat16), "row", scatter_dimension=0, tiled=True
-    )
+    grad_projected = exchange_sum(backward_terms.astype(jnp.bfloat16), "row").astype(jnp.bfloat16)
     weight_term = lax.dot_general(
         features, grad_projected, (((0,), (0,)), ((), ())), preferred_element_type=jnp.float32
     )
-    weight_part = lax.psum_scatter(weight_term, "row", scatter_dimension=0, tiled=True)
-    weight_part = lax.psum(weight_part, "col")
-    grad_weight = lax.all_gather(weight_part, "row", axis=0, tiled=True)
+    weight_part = exchange_sum(exchange_sum(weight_term, "row"), "col")
+    grad_weight = exchange_gather(exchange_gather(weight_part, "col"), "row")
     grad_features = lax.dot_general(
         grad_projected, weight, (((1,), (1,)), ((), ())), preferred_element_type=jnp.float32
     ).astype(jnp.bfloat16)

time: 677 us -> 467 us (0.69)
  waiting for transfers between devices: 543 us -> 129 us
  blocking collectives: 0 us -> 203 us
    all_to_all x0 -> x5, blocking collectives: none -> 203 us  [the longest x4 190 us: exchange_sum(): pieces = lax.all_to_all(pieces, axis_name, 0, 0, tiled=False)]
    psum x1 -> x0, waiting for transfers between devices: 169 us -> none  [shards(): weight_part = lax.psum(weight_part, 'col')]
    reduce_scatter x2 -> x0, waiting for transfers between devices: 163 us -> none  [the longest x1 97.1 us: shards(): lax.psum_scatter(forward_terms.astype(jnp.bfloat16), 'col', scatter_dimen...]
    unnamed x8 -> x2, waiting for transfers between devices: 63.7 us -> 0.03 us
    all_gather x1 -> x0, waiting for transfers between devices: 32.7 us -> none  [shards(): grad_weight = lax.all_gather(weight_part, 'row', axis=0, tiled=True)]
    all_to_all x0 -> x1, waiting for transfers between devices: none -> 12.3 us  [exchange_gather(): pieces = lax.all_to_all(pieces, axis_name, 0, 0, tiled=False)]
  transfers between devices with their start and end apart: 7 -> 3, of which waited for: 7 -> 3; matrix products, arithmetic and copies ran while one was open for 0% -> 1% of each run, Pallas kernels for 0% -> 0%
where the time goes in v2:
time: 467 us; the launch traced here: 462 us
  blocking collectives  203 us (43%)
  waiting for transfers between devices  129 us (28%)
  other arithmetic  51.7 us (11%)
  local copies, waits for them, and re-layouts  39 us (8%)
  matrix products  17.8 us (4%)
  between operations  14.8 us (3%)
  starting transfers between devices  6.75 us (1%)
    all_to_all x4, blocking collectives, exchange_sum(): pieces = lax.all_to_all(pieces, axis_name, 0, 0, tiled=False)  190 us
    all_gather x1, waiting for transfers between devices, shards(): upstream = lax.all_gather(own_upstream, 'col', axis=0, tiled=True)  76.6 us
    all_gather x1, waiting for transfers between devices, shards(): panel = lax.all_gather(projected, 'row', axis=0, tiled=True)  40.6 us
    scatter-add x2, other arithmetic, one_group(): return running.at[target_ids].add(products * alive_mask[:, None, None])  37.1 us
    mul x2, local copies, waits for them, and re-layouts, one_group(): return running.at[target_ids].add(products * alive_mask[:, None, None])  18 us
    all_to_all x1, blocking collectives, exchange_gather(): pieces = lax.all_to_all(pieces, axis_name, 0, 0, tiled=False)  13 us
    all_to_all x1, waiting for transfers between devices, exchange_gather(): pieces = lax.all_to_all(pieces, axis_name, 0, 0, tiled=False)  12.3 us
    gather x2, local copies, waits for them, and re-layouts, one_group(): tiles = jnp.take(source_tiles, source_ids, axis=0)  9.85 us
  transfers between devices with their start and end apart: 3, of which 3 were waited for; matrix products, arithmetic and copies ran while one was open for 1% of the time, Pallas kernels for 0%

profile of v2, /device:TPU:2, one launch (start us, length us, event | category | flops | bytes accessed | tf_op | source)
XLA Modules:
  0.0 462.5 jit_solution(15065479126634602071)
XLA Ops:
  7.2 0.0 copy-start
  7.2 0.0 all-gather.3.cloned.1.call-start
  7.2 2.2 convolution_convert_fusion.1
  9.4 0.0 all-gather.3.cloned.1.call-update
  9.5 0.0 all-gather.5.cloned.1.call-start
  10.2 0.7 compare_select_fusion.1
  10.8 0.7 fusion.14
  11.5 0.7 compare_and_fusion.1
  12.1 40.6 %all-gather.3.cloned.1.call-done = bf16[4096,512]{1,0:T(8,128)(2,1)} async-done(((bf16[256,512]{1,0:T(8,128)(2,1)}), bf16[4096,512]{1,0:T(8,128)(2,1)}) %all-gather.3.cloned.1.call-update) | async-done | bytes 4194320 | tf_op jit(solution)/shard_map/all_gather | solution.py:59
  52.8 4.9 %gather_fusion = bf16[32,128,512]{2,1,0:T(8,128)(2,1)} fusion(bf16[32,128,512]{2,1,0:T(8,128)(2,1)} %bitcast.43, s32[1024]{0:T(1024)S(1)} %pad_clamp_fusion.1), kind=kCustom, calls=%fused_computation.clone | custom fusion | bytes 8388736 | tf_op jit(solution)/shard_map/while/body/eval_jaxpr/jit(_take)/gather | solution.py:16
  57.7 0.0 copy-done
  57.7 7.1 %multiply_bitcast_fusion.1 = f32[32,128,512]{1,2,0:T(8,128)} fusion(f32[32]{0:T(128)S(1)} %get-tuple-element.39, bf16[32,128,512]{2,1,0:T(8,128)(2,1)} %gather_fusion, pred[32]{0:T(512)(128)(4,1)S(1)} %get-tuple-element.38, bf16[1,1,32,128,128]{4,3,2,1,0:T(8,128)(2,1)S(1)} %copy-done), kind=kOutput, calls=%fused_computation.6 | convolution fusion | flops 541065216 | bytes 13631648 | tf_op jit(solution)/shard_map/while/body/eval_jaxpr/kab,kbf->kaf/dot_general | solution.py:20
  64.8 9.0 %copy.21 = f32[32,128,512]{2,1,0:T(8,128)} copy(f32[32,128,512]{1,2,0:T(8,128)} %multiply_bitcast_fusion.1) | data formatting | bytes 16777216 | tf_op jit(solution)/shard_map/while/body/eval_jaxpr/mul | solution.py:22
  73.8 4.3 broadcast.56.clone
  78.1 18.5 %scatter_fusion = f32[32,128,512]{2,1,0:T(8,128)} fusion(f32[32,128,512]{2,1,0:T(8,128)} %broadcast.56.clone, s32[32]{0:T(128)S(1)} %fusion.14, f32[32,128,512]{2,1,0:T(8,128)} %copy.21), kind=kCustom, calls=%fused_computation.2 | custom fusion | flops 2097152 | bytes 25165952 | tf_op jit(solution)/shard_map/while/body/eval_jaxpr/scatter-add | solution.py:22
  96.6 4.0 convert_element_type.46
  100.6 100.2 %all_to_all.30 = bf16[16,256,512]{2,1,0:T(8,128)(2,1)S(1)} all-to-all(bf16[16,256,512]{2,1,0:T(8,128)(2,1)S(1)} %bitcast.41), channel_id=1, replica_groups=mesh['row'=16,'col'=16] {'col'}, dimensions={0} | all-to-all | bytes 8388608 | tf_op jit(solution)/shard_map/all_to_all | solution.py:33
  200.8 0.0 copy-start.4
  200.8 0.6 convert_reduce_fusion
  201.4 0.4 copy-done.4
  201.8 1.0 multiply_convert_fusion
  202.8 0.0 all-gather.5.cloned.1.call-update
  202.8 0.0 copy-done.6
  202.9 0.0 copy-done.5
  202.9 76.6 %all-gather.5.cloned.1.call-done = bf16[4096,512]{1,0:T(8,128)(2,1)} async-done(((bf16[256,512]{1,0:T(8,128)(2,1)}), bf16[4096,512]{1,0:T(8,128)(2,1)}) %all-gather.5.cloned.1.call-update) | async-done | bytes 4194320 | tf_op jit(solution)/shard_map/all_gather | solution.py:66
  279.5 4.9 %gather_fusion.1 = bf16[32,128,512]{2,1,0:T(8,128)(2,1)} fusion(bf16[32,128,512]{2,1,0:T(8,128)(2,1)} %bitcast.44, s32[1024]{0:T(1024)S(1)} %pad_clamp_fusion), kind=kCustom, calls=%fused_computation.1.clone | custom fusion | bytes 8388736 | tf_op jit(solution)/shard_map/while/body/eval_jaxpr/jit(_take)/gather | solution.py:16
  284.4 7.1 %multiply_bitcast_fusion = f32[32,128,512]{1,2,0:T(8,128)} fusion(f32[32]{0:T(128)S(1)} %get-tuple-element.39, bf16[32,128,512]{2,1,0:T(8,128)(2,1)} %gather_fusion.1, pred[32]{0:T(512)(128)(4,1)S(1)} %compare_and_fusion, bf16[1,1,32,128,128]{4,3,2,1,0:T(8,128)(2,1)S(1)} %copy-done), kind=kOutput, calls=%fused_computation.4 | convolution fusion | flops 541065216 | bytes 13631648 | tf_op jit(solution)/shard_map/while/body/eval_jaxpr/kba,kbf->kaf/dot_general | solution.py:18
  291.5 9.0 %copy.23 = f32[32,128,512]{2,1,0:T(8,128)} copy(f32[32,128,512]{1,2,0:T(8,128)} %multiply_bitcast_fusion) | data formatting | bytes 16777216 | tf_op jit(solution)/shard_map/while/body/eval_jaxpr/mul | solution.py:22
  300.5 4.3 broadcast.56
  304.8 18.5 %scatter_fusion.1 = f32[32,128,512]{2,1,0:T(8,128)} fusion(f32[32,128,512]{2,1,0:T(8,128)} %broadcast.56, s32[32]{0:T(128)S(1)} %fusion.15, f32[32,128,512]{2,1,0:T(8,128)} %copy.23), kind=kCustom, calls=%fused_computation.3 | custom fusion | flops 2097152 | bytes 25165952 | tf_op jit(solution)/shard_map/while/body/eval_jaxpr/scatter-add | solution.py:22
  323.4 4.0 convert_element_type.52
  327.4 54.4 %all_to_all.31 = bf16[16,256,512]{2,1,0:T(8,128)(2,1)} all-to-all(bf16[16,256,512]{2,1,0:T(8,128)(2,1)S(1)} %bitcast.42), channel_id=1, replica_groups=mesh['row'=16,'col'=16] {'row'}, dimensions={0} | all-to-all | bytes 8388608 | tf_op jit(solution)/shard_map/all_to_all | solution.py:33
  381.8 2.9 reduce_sum.40
  384.6 0.0 copy-done.3
  384.7 0.0 copy-start.2
  384.7 0.3 fusion.18
  385.0 0.0 copy-start.1
  385.0 19.2 %all_to_all.33 = f32[16,32,512]{2,1,0:T(8,128)S(1)} all-to-all(f32[16,32,512]{2,1,0:T(8,128)S(1)} %bitcast.46), channel_id=1, replica_groups=mesh['row'=16,'col'=16] {'row'}, dimensions={0} | all-to-all | bytes 2097152 | tf_op jit(solution)/shard_map/all_to_all | solution.py:33
  404.2 0.1 reduce_sum.41
  404.4 16.1 %all_to_all.34 = f32[16,2,512]{2,1,0:T(2,128)S(1)} all-to-all(f32[16,2,512]{2,1,0:T(2,128)S(1)} %reshape.100), channel_id=1, replica_groups=mesh['row'=16,'col'=16] {'col'}, dimensions={0} | all-to-all | bytes 131072 | tf_op jit(solution)/shard_map/all_to_all | solution.py:33
  420.5 13.0 %all_to_all.32 = f32[16,2,512]{2,1,0:T(2,128)S(1)} all-to-all(f32[16,2,512]{2,1,0:T(2,128)S(1)} %broadcast_in_dim.30), channel_id=1, replica_groups=mesh['row'=16,'col'=16] {'col'}, dimensions={0} | all-to-all | bytes 131072 | tf_op jit(solution)/shard_map/all_to_all | solution.py:40
  433.6 1.1 broadcast_in_dim.32
  434.7 6.7 %all-to-all-start.5 = ((f32[16,32,512]{2,1,0:T(8,128)}), f32[16,32,512]{2,1,0:T(8,128)S(1)}, u32[]{:S(2)}, u32[]{:S(2)}) async-start(f32[16,32,512]{2,1,0:T(8,128)} %broadcast_in_dim.32), calls=%async_computation.5 | async-start | bytes 2097152 | tf_op jit(solution)/shard_map/all_to_all | solution.py:40
  441.4 0.0 copy-done.2
  441.4 1.0 convolution_convert_fusion
  442.4 12.3 %all-to-all-done.5 = f32[16,32,512]{2,1,0:T(8,128)S(1)} async-done(((f32[16,32,512]{2,1,0:T(8,128)}), f32[16,32,512]{2,1,0:T(8,128)S(1)}, u32[]{:S(2)}, u32[]{:S(2)}) %all-to-all-start.5) | async-done | bytes 1048608 | tf_op jit(solution)/shard_map/all_to_all | solution.py:40
  454.7 1.0 copy.34
  455.7 0.0 copy-done.1
  (12 shorter events, 0.2 us)
Async XLA Ops:
  7.2 50.5 %copy-start = (bf16[1,1,32,128,128]{4,3,2,1,0:T(8,128)(2,1)S(1)}, bf16[1,1,32,128,128]{4,3,2,1,0:T(8,128)(2,1)}, u32[]{:S(2)}) copy-start(bf16[1,1,32,128,128]{4,3,2,1,0:T(8,128)(2,1)} %param.11) | copy-start | bytes 3145732
  7.2 45.6 %all-gather.3.cloned.1.call-start = ((), (), s32[]{:S(2)}) async-start(), calls=%async_computation.6 | async-start | bytes 4456448 | tf_op jit(solution)/shard_map/all_gather | solution.py:59
  9.5 270.0 %all-gather.5.cloned.1.call-start = ((), (), s32[]{:S(2)}) async-start(), calls=%async_computation.7 | async-start | bytes 4456448 | tf_op jit(solution)/shard_map/all_gather | solution.py:66
  200.8 1.0 copy-start.4
  200.8 2.0 copy-start.6
  200.8 2.0 copy-start.5
  381.8 2.9 copy-start.3
  384.7 56.7 %copy-start.2 = (bf16[512,512]{1,0:T(8,128)(2,1)S(1)}, bf16[512,512]{1,0:T(8,128)(2,1)}, u32[]{:S(2)}) copy-start(bf16[512,512]{1,0:T(8,128)(2,1)} %param.10) | copy-start | bytes 1572868
  385.0 70.6 %copy-start.1 = (bf16[1,1,32,128,128]{4,3,2,1,0:T(8,128)(2,1)S(1)}, bf16[1,1,32,128,128]{4,3,2,1,0:T(8,128)(2,1)}, u32[]{:S(2)}) copy-start(bf16[1,1,32,128,128]{4,3,2,1,0:T(8,128)(2,1)} %param.11) | copy-start | bytes 3145732
  434.7 20.0 %all-to-all-start.5 = ((f32[16,32,512]{2,1,0:T(8,128)}), f32[16,32,512]{2,1,0:T(8,128)S(1)}, u32[]{:S(2)}, u32[]{:S(2)}) async-start(f32[16,32,512]{2,1,0:T(8,128)} %broadcast_in_dim.32), calls=%async_computation.5 | async-start | bytes 2097152 | tf_op jit(solution)/shard_map/all_to_all | solution.py:40
Sparse Core Ops, SparseCore 0:
  10.4 42.3 all-gather.2
  203.0 76.4 all-gather.4

commit v3 on v2

--- a/solution.py
+++ b/solution.py
@@ -1,30 +1,67 @@
+import functools
 import jax
 import jax.numpy as jnp
 from jax import lax
+from jax.experimental import pallas as pl
+from jax.experimental.pallas import tpu as pltpu
 from jax.sharding import PartitionSpec as P
 
 
+def block_kernel(source_ids, target_ids, live, values_ref, tile_ref, out_ref, acc_ref, *, transpose):
+    k = pl.program_id(0)
+
+    @pl.when(k == 0)
+    def _():
+        acc_ref[...] = jnp.zeros_like(acc_ref)
+
+    @pl.when(k < live[0])
+    def _():
+        block = values_ref[...]
+        if transpose:
+            term = lax.dot_general(block, tile_ref[...], (((0,), (0,)), ((), ())), preferred_element_type=jnp.float32)
+        else:
+            term = jnp.dot(block, tile_ref[...], preferred_element_type=jnp.float32)
+        target = target_ids[k]
+        acc_ref[target] += term
+
+    @pl.when(k == pl.num_programs(0) - 1)
+    def _():
+        out_ref[...] = acc_ref[...].reshape(out_ref.shape).astype(out_ref.dtype)
+
+
 def block_terms(values, source_ids, target_ids, live_count, source, target_blocks, transpose):
-    entry_total = values.shape[0]
-    block_side = values.shape[1]
+    entry_total, block_side, _ = values.shape
     feature_count = source.shape[1]
-    group_size = min(32, entry_total)
-    source_tiles = source.reshape(-1, block_side, feature_count)
+    live = jnp.reshape(live_count, (1,)).astype(jnp.int32)
 
-    def one_group(group_index, running):
-        first_entry = group_index * group_size
-        tiles = jnp.take(source_tiles, source_ids, axis=0)
-        if transpose:
-            products = jnp.einsum("kba,kbf->kaf", values, tiles, preferred_element_type=jnp.float32)
-        else:
-            products = jnp.einsum("kab,kbf->kaf", values, tiles, preferred_element_type=jnp.float32)
-        alive_mask = (first_entry + jnp.arange(group_size) < live_count).astype(jnp.float32)
-        return running.at[target_ids].add(products * alive_mask[:, None, None])
+    def entry_of(k, live):
+        return jnp.minimum(k, live[0] - 1)
 
-    zero_sum = jnp.zeros((target_blocks, block_side, feature_count), jnp.float32)
-    trip_count = entry_total // group_size
-    running = lax.fori_loop(0, trip_count, one_group, zero_sum)
-    return running.reshape(target_blocks * block_side, feature_count)
+    def values_map(k, source_ids, target_ids, live):
+        return (entry_of(k, live), 0, 0)
+
+    def tile_map(k, source_ids, target_ids, live):
+        return (source_ids[entry_of(k, live)], 0)
+
+    def out_map(k, source_ids, target_ids, live):
+        return (0, 0)
+
+    grid_spec = pltpu.PrefetchScalarGridSpec(
+        num_scalar_prefetch=3,
+        grid=(entry_total,),
+        in_specs=[
+            pl.BlockSpec((None, block_side, block_side), values_map),
+            pl.BlockSpec((block_side, feature_count), tile_map),
+        ],
+        out_specs=pl.BlockSpec((target_blocks * block_side, feature_count), out_map),
+        scratch_shapes=[pltpu.VMEM((target_blocks, block_side, feature_count), jnp.float32)],
+    )
+    return pl.pallas_call(
+        functools.partial(block_kernel, transpose=transpose),
+        grid_spec=grid_spec,
+        out_shape=jax.ShapeDtypeStruct((target_blocks * block_side, feature_count), jnp.bfloat16),
+        compiler_params=pltpu.CompilerParams(dimension_semantics=("arbitrary",)),
+    )(source_ids, target_ids, live, values, source)
 
 
 def exchange_sum(parts, axis_name):

time: 467 us -> 410 us (0.88)
  other arithmetic: 51.7 us -> 4.61 us
  local copies, waits for them, and re-layouts: 39 us -> 3.53 us
  Pallas kernels: 0 us -> 21.2 us
  blocking collectives: 203 us -> 223 us
  matrix products: 17.8 us -> 3.33 us
    scatter-add x2 -> x0, other arithmetic: 37.1 us -> none  [one_group(): return running.at[target_ids].add(products * alive_mask[:, None, None])]
    pallas_call x0 -> x2, Pallas kernels: none -> 21.2 us  [block_terms(): pl.pallas_call(functools.partial(block_kernel, transpose=transpose), grid...]
    all_to_all x4, blocking collectives: 190 us -> 210 us  [exchange_sum(): pieces = lax.all_to_all(pieces, axis_name, 0, 0, tiled=False)]
    mul x2 -> x0, local copies, waits for them, and re-layouts: 18 us -> none  [one_group(): return running.at[target_ids].add(products * alive_mask[:, None, None])]
    dot_general x2 -> x0, matrix products: 14.2 us -> none  [the longest x1 7.12 us: one_group(): jnp.einsum('kba,kbf->kaf', values, tiles, preferred_element_type=jnp.floa...]
    gather x2 -> x0, local copies, waits for them, and re-layouts: 9.85 us -> none  [one_group(): tiles = jnp.take(source_tiles, source_ids, axis=0)]
    another operation x2 -> x0, local copies, waits for them, and re-layouts: 8.57 us -> none
    convert_element_type x2 -> x0, other arithmetic: 7.99 us -> none  [the longest x1 4 us: shards(): own_sum = exchange_sum(forward_terms.astype(jnp.bfloat16), 'col')]
  transfers between devices with their start and end apart: 3 -> 3, of which waited for: 3 -> 3; matrix products, arithmetic and copies ran while one was open for 1% -> 0% of each run, Pallas kernels for 0% -> 0%
where the time goes in v3:
time: 410 us; the launch traced here: 404 us
  blocking collectives  223 us (54%)
  waiting for transfers between devices  126 us (31%)
  Pallas kernels  21.2 us (5%)
  between operations  14.7 us (4%)
  starting transfers between devices  6.75 us (2%)
  other arithmetic  4.61 us (1%)
    all_to_all x4, blocking collectives, exchange_sum(): pieces = lax.all_to_all(pieces, axis_name, 0, 0, tiled=False)  210 us
    all_gather x1, waiting for transfers between devices, shards(): upstream = lax.all_gather(own_upstream, 'col', axis=0, tiled=True)  72.1 us
    all_gather x1, waiting for transfers between devices, shards(): panel = lax.all_gather(projected, 'row', axis=0, tiled=True)  41.9 us
    pallas_call x2, Pallas kernels, block_terms(): pl.pallas_call(functools.partial(block_kernel, transpose=transpose), grid...  21.2 us
    all_to_all x1, blocking collectives, exchange_gather(): pieces = lax.all_to_all(pieces, axis_name, 0, 0, tiled=False)  13 us
    all_to_all x1, waiting for transfers between devices, exchange_gather(): pieces = lax.all_to_all(pieces, axis_name, 0, 0, tiled=False)  12.3 us
  transfers between devices with their start and end apart: 3, of which 3 were waited for; matrix products, arithmetic and copies ran while one was open for 0% of the time, Pallas kernels for 0%

profile of v3, /device:TPU:2, one launch (start us, length us, event | category | flops | bytes accessed | tf_op | source)
XLA Modules:
  0.0 403.6 jit_solution(16291172527712680607)
XLA Ops:
  7.2 0.0 copy-start
  7.2 0.0 all-gather.3.cloned.1.call-start
  7.2 1.0 copy-done
  8.2 2.0 convolution_convert_fusion.1
  10.2 0.0 all-gather.3.cloned.1.call-update
  10.2 0.0 all-gather.5.cloned.1.call-start
  10.9 41.9 %all-gather.3.cloned.1.call-done.tile_ref = bf16[4096,512]{1,0:T(8,128)(2,1)} async-done(((bf16[256,512]{1,0:T(8,128)(2,1)}), bf16[4096,512]{1,0:T(8,128)(2,1)}) %all-gather.3.cloned.1.call-update) | async-done | bytes 4194320 | tf_op jit(solution)/shard_map/all_gather | solution.py:96
  52.8 10.5 %shard_map.94 = bf16[4096,512]{1,0:T(8,128)(2,1)} custom-call(s32[32]{0:T(128)} %bitcast.24, s32[32]{0:T(128)} %bitcast.26, s32[1]{0:T(128)} %bitcast.16.live, bf16[32,128,128]{2,1,0:T(8,128)(2,1)} %bitcast.20, bf16[4096,512]{1,0:T(8,128)(2,1)} %all-gather.3.cloned.1.call-done.tile_ref), custom_call_target="tpu_custom_call" | custom-call | tf_op jit(solution)/shard_map/pallas_call | solution.py:59
  63.3 110.7 %all_to_all.30 = bf16[16,256,512]{2,1,0:T(8,128)(2,1)S(1)} all-to-all(bf16[16,256,512]{2,1,0:T(8,128)(2,1)} %bitcast.19), channel_id=1, replica_groups=mesh['row'=16,'col'=16] {'col'}, dimensions={0} | all-to-all | bytes 8388608 | tf_op jit(solution)/shard_map/all_to_all | solution.py:70
  174.0 0.0 copy-start.2
  174.0 0.6 convert_reduce_fusion
  174.6 0.4 copy-done.2
  174.9 1.0 multiply_convert_fusion
  176.0 0.0 all-gather.5.cloned.1.call-update
  176.0 72.1 %all-gather.5.cloned.1.call-done.tile_ref = bf16[4096,512]{1,0:T(8,128)(2,1)} async-done(((bf16[256,512]{1,0:T(8,128)(2,1)}), bf16[4096,512]{1,0:T(8,128)(2,1)}) %all-gather.5.cloned.1.call-update) | async-done | bytes 4194320 | tf_op jit(solution)/shard_map/all_gather | solution.py:103
  248.1 10.7 %shard_map.95 = bf16[4096,512]{1,0:T(8,128)(2,1)} custom-call(s32[32]{0:T(128)} %bitcast.27, s32[32]{0:T(128)} %bitcast.25, s32[1]{0:T(128)} %bitcast.17.live, bf16[32,128,128]{2,1,0:T(8,128)(2,1)} %bitcast.21, bf16[4096,512]{1,0:T(8,128)(2,1)} %all-gather.5.cloned.1.call-done.tile_ref), custom_call_target="tpu_custom_call" | custom-call | tf_op jit(solution)/shard_map/pallas_call | solution.py:59
  258.8 63.6 %all_to_all.31 = bf16[16,256,512]{2,1,0:T(8,128)(2,1)} all-to-all(bf16[16,256,512]{2,1,0:T(8,128)(2,1)} %bitcast.18), channel_id=1, replica_groups=mesh['row'=16,'col'=16] {'row'}, dimensions={0} | all-to-all | bytes 8388608 | tf_op jit(solution)/shard_map/all_to_all | solution.py:70
  322.4 0.0 copy-start.1
  322.4 2.9 reduce_sum.40
  325.3 0.0 copy-done.1
  325.3 0.3 fusion
  325.6 19.1 %all_to_all.32 = f32[16,32,512]{2,1,0:T(8,128)S(1)} all-to-all(f32[16,32,512]{2,1,0:T(8,128)S(1)} %bitcast.23), channel_id=1, replica_groups=mesh['row'=16,'col'=16] {'row'}, dimensions={0} | all-to-all | bytes 2097152 | tf_op jit(solution)/shard_map/all_to_all | solution.py:70
  344.7 0.1 reduce_sum.41
  344.8 16.7 %all_to_all.33 = f32[16,2,512]{2,1,0:T(2,128)S(1)} all-to-all(f32[16,2,512]{2,1,0:T(2,128)S(1)} %reshape.26), channel_id=1, replica_groups=mesh['row'=16,'col'=16] {'col'}, dimensions={0} | all-to-all | bytes 131072 | tf_op jit(solution)/shard_map/all_to_all | solution.py:70
  361.6 13.0 %all_to_all.34 = f32[16,2,512]{2,1,0:T(2,128)S(1)} all-to-all(f32[16,2,512]{2,1,0:T(2,128)S(1)} %broadcast_in_dim.6), channel_id=1, replica_groups=mesh['row'=16,'col'=16] {'col'}, dimensions={0} | all-to-all | bytes 131072 | tf_op jit(solution)/shard_map/all_to_all | solution.py:77
  374.7 1.1 broadcast_in_dim.15
  375.8 6.7 %all-to-all-start.5 = ((f32[16,32,512]{2,1,0:T(8,128)}), f32[16,32,512]{2,1,0:T(8,128)S(1)}, u32[]{:S(2)}, u32[]{:S(2)}) async-start(f32[16,32,512]{2,1,0:T(8,128)} %broadcast_in_dim.15), calls=%async_computation.5 | async-start | bytes 2097152 | tf_op jit(solution)/shard_map/all_to_all | solution.py:77
  382.5 1.0 convolution_convert_fusion
  383.5 12.3 %all-to-all-done.5 = f32[16,32,512]{2,1,0:T(8,128)S(1)} async-done(((f32[16,32,512]{2,1,0:T(8,128)}), f32[16,32,512]{2,1,0:T(8,128)S(1)}, u32[]{:S(2)}, u32[]{:S(2)}) %all-to-all-start.5) | async-done | bytes 1048608 | tf_op jit(solution)/shard_map/all_to_all | solution.py:77
  395.8 1.0 copy.14
  (4 shorter events, 0.1 us)
Async XLA Ops:
  7.2 1.0 copy-start
  7.2 45.6 %all-gather.3.cloned.1.call-start = ((), (), s32[]{:S(2)}) async-start(), calls=%async_computation.6 | async-start | bytes 4456448 | tf_op jit(solution)/shard_map/all_gather | solution.py:96
  10.2 237.9 %all-gather.5.cloned.1.call-start = ((), (), s32[]{:S(2)}) async-start(), calls=%async_computation.7 | async-start | bytes 4456448 | tf_op jit(solution)/shard_map/all_gather | solution.py:103
  174.0 1.0 copy-start.2
  322.4 2.9 copy-start.1
  375.8 20.0 %all-to-all-start.5 = ((f32[16,32,512]{2,1,0:T(8,128)}), f32[16,32,512]{2,1,0:T(8,128)S(1)}, u32[]{:S(2)}, u32[]{:S(2)}) async-start(f32[16,32,512]{2,1,0:T(8,128)} %broadcast_in_dim.15), calls=%async_computation.5 | async-start | bytes 2097152 | tf_op jit(solution)/shard_map/all_to_all | solution.py:77
Sparse Core Ops, SparseCore 0:
  10.4 42.3 all-gather.2
  176.1 71.9 all-gather.4

commit v4 on v3

--- a/solution.py
+++ b/solution.py
@@ -5,6 +5,8 @@
 from jax.experimental import pallas as pl
 from jax.experimental.pallas import tpu as pltpu
 from jax.sharding import PartitionSpec as P
+
+CHUNKS = 2
 
 
 def block_kernel(source_ids, target_ids, live, values_ref, tile_ref, out_ref, acc_ref, *, transpose):
@@ -92,27 +94,35 @@
     block_side = values.shape[1]
     row_span = lax.axis_size("col") * local_rows
     col_span = lax.axis_size("row") * local_rows
-    projected = jnp.dot(features, weight, preferred_element_type=jnp.float32).astype(jnp.bfloat16)
-    panel = lax.all_gather(projected, "row", axis=0, tiled=True)
-    forward_terms = block_terms(
-        values, col_ids, row_ids, live_count, panel, row_span // block_side, False
-    )
-    own_sum = exchange_sum(forward_terms.astype(jnp.bfloat16), "col")
-    output = jax.nn.silu(own_sum).astype(jnp.bfloat16)
-    own_upstream = (cotangent.astype(jnp.float32) * silu_slope(own_sum)).astype(jnp.bfloat16)
-    upstream = lax.all_gather(own_upstream, "col", axis=0, tiled=True)
-    backward_terms = block_terms(
-        values, row_ids, col_ids, live_count, upstream, col_span // block_side, True
-    )
-    grad_projected = exchange_sum(backward_terms.astype(jnp.bfloat16), "row").astype(jnp.bfloat16)
-    weight_term = lax.dot_general(
-        features, grad_projected, (((0,), (0,)), ((), ())), preferred_element_type=jnp.float32
-    )
+    width = weight.shape[1] // CHUNKS
+    outputs, weight_terms, feature_terms = [], [], []
+    for part in range(CHUNKS):
+        weight_cols = weight[:, part * width:(part + 1) * width]
+        projected = jnp.dot(features, weight_cols, preferred_element_type=jnp.float32).astype(jnp.bfloat16)
+        panel = lax.all_gather(projected, "row", axis=0, tiled=True)
+        forward_terms = block_terms(
+            values, col_ids, row_ids, live_count, panel, row_span // block_side, False
+        )
+        own_sum = exchange_sum(forward_terms, "col")
+        outputs.append(jax.nn.silu(own_sum).astype(jnp.bfloat16))
+        own_cotangent = cotangent[:, part * width:(part + 1) * width].astype(jnp.float32)
+        own_upstream = (own_cotangent * silu_slope(own_sum)).astype(jnp.bfloat16)
+        upstream = lax.all_gather(own_upstream, "col", axis=0, tiled=True)
+        backward_terms = block_terms(
+            values, row_ids, col_ids, live_count, upstream, col_span // block_side, True
+        )
+        grad_projected = exchange_sum(backward_terms, "row").astype(jnp.bfloat16)
+        weight_terms.append(lax.dot_general(
+            features, grad_projected, (((0,), (0,)), ((), ())), preferred_element_type=jnp.float32
+        ))
+        feature_terms.append(lax.dot_general(
+            grad_projected, weight_cols, (((1,), (1,)), ((), ())), preferred_element_type=jnp.float32
+        ))
+    output = jnp.concatenate(outputs, axis=1)
+    weight_term = jnp.concatenate(weight_terms, axis=1)
     weight_part = exchange_sum(exchange_sum(weight_term, "row"), "col")
     grad_weight = exchange_gather(exchange_gather(weight_part, "col"), "row")
-    grad_features = lax.dot_general(
-        grad_projected, weight, (((1,), (1,)), ((), ())), preferred_element_type=jnp.float32
-    ).astype(jnp.bfloat16)
+    grad_features = sum(feature_terms).astype(jnp.bfloat16)
     return (output, grad_features, grad_weight)
 
 

time: 410 us -> 452 us (1.10)
  blocking collectives: 223 us -> 48.9 us
  waiting for transfers between devices: 126 us -> 273 us
  starting transfers between devices: 6.75 us -> 41.5 us
  Pallas kernels: 21.2 us -> 50.5 us
    all_to_all x4 -> x2, blocking collectives: 210 us -> 35.8 us  [exchange_sum(): pieces = lax.all_to_all(pieces, axis_name, 0, 0, tiled=False)]
    all_to_all x0 -> x4, waiting for transfers between devices: none -> 85.2 us  [exchange_sum(): pieces = lax.all_to_all(pieces, axis_name, 0, 0, tiled=False)]
    all_gather x1 -> x2, waiting for transfers between devices: 72.1 us -> 107 us  [shards(): upstream = lax.all_gather(own_upstream, 'col', axis=0, tiled=True)]
    all_to_all x0 -> x4, starting transfers between devices: none -> 34.7 us  [exchange_sum(): pieces = lax.all_to_all(pieces, axis_name, 0, 0, tiled=False)]
    pallas_call x2 -> x4, Pallas kernels: 21.2 us -> 50.5 us  [block_terms(): pl.pallas_call(functools.partial(block_kernel, transpose=transpose), grid...]
    all_gather x1 -> x2, waiting for transfers between devices: 41.9 us -> 68.9 us  [shards(): panel = lax.all_gather(projected, 'row', axis=0, tiled=True)]
  transfers between devices with their start and end apart: 3 -> 9, of which waited for: 3 -> 8; matrix products, arithmetic and copies ran while one was open for 0% -> 1% of each run, Pallas kernels for 0% -> 11%
where the time goes in v4:
time: 452 us; the launch traced here: 444 us
  waiting for transfers between devices  273 us (60%)
  Pallas kernels  50.5 us (11%)
  blocking collectives  48.9 us (11%)
  starting transfers between devices  41.5 us (9%)
  between operations  14.5 us (3%)
  other arithmetic  6.2 us (1%)
  matrix products  5.38 us (1%)
    all_gather x2, waiting for transfers between devices, shards(): upstream = lax.all_gather(own_upstream, 'col', axis=0, tiled=True)  107 us
    all_to_all x4, waiting for transfers between devices, exchange_sum(): pieces = lax.all_to_all(pieces, axis_name, 0, 0, tiled=False)  85.2 us
    all_gather x2, waiting for transfers between devices, shards(): panel = lax.all_gather(projected, 'row', axis=0, tiled=True)  68.9 us
    pallas_call x4, Pallas kernels, block_terms(): pl.pallas_call(functools.partial(block_kernel, transpose=transpose), grid...  50.5 us
    all_to_all x2, blocking collectives, exchange_sum(): pieces = lax.all_to_all(pieces, axis_name, 0, 0, tiled=False)  35.8 us
    all_to_all x4, starting transfers between devices, exchange_sum(): pieces = lax.all_to_all(pieces, axis_name, 0, 0, tiled=False)  34.7 us
    all_to_all x1, blocking collectives, exchange_gather(): pieces = lax.all_to_all(pieces, axis_name, 0, 0, tiled=False)  13.2 us
    all_to_all x1, waiting for transfers between devices, exchange_gather(): pieces = lax.all_to_all(pieces, axis_name, 0, 0, tiled=False)  11.3 us
  transfers between devices with their start and end apart: 9, of which 8 were waited for; matrix products, arithmetic and copies ran while one was open for 1% of the time, Pallas kernels for 11%

profile of v4, /device:TPU:2, one launch (start us, length us, event | category | flops | bytes accessed | tf_op | source)
XLA Modules:
  0.0 443.9 jit_solution(1467629110637690663)
XLA Ops:
  7.2 0.0 copy-start
  7.2 0.0 all-gather.7.cloned.1.call-start
  7.2 0.9 copy-done
  8.1 1.8 convolution_convert_fusion
  10.0 0.0 all-gather.7.cloned.1.call-update
  10.0 0.0 all-gather.5.cloned.1.call-start
  10.0 1.8 convolution_convert_fusion.1
  11.9 0.0 all-gather.5.cloned.1.call-update
  12.5 36.9 %all-gather.7.cloned.1.call-done.tile_ref = bf16[4096,256]{1,0:T(8,128)(2,1)} async-done(((bf16[256,256]{1,0:T(8,128)(2,1)}), bf16[4096,256]{1,0:T(8,128)(2,1)}) %all-gather.7.cloned.1.call-update) | async-done | bytes 2097168 | tf_op jit(solution)/shard_map/all_gather | solution.py:102
  49.5 12.4 %shard_map.95 = bf16[4096,256]{1,0:T(8,128)(2,1)} custom-call(s32[32]{0:T(128)} %bitcast.36, s32[32]{0:T(128)} %bitcast.40, s32[1]{0:T(128)} %bitcast.23.live, bf16[32,128,128]{2,1,0:T(8,128)(2,1)} %bitcast.26, bf16[4096,256]{1,0:T(8,128)(2,1)} %all-gather.7.cloned.1.call-done.tile_ref), custom_call_target="tpu_custom_call" | custom-call | tf_op jit(solution)/shard_map/pallas_call | solution.py:61
  61.9 9.9 %all-to-all-start.1 = ((bf16[16,256,256]{2,1,0:T(8,128)(2,1)}), bf16[16,256,256]{2,1,0:T(8,128)(2,1)S(1)}, u32[]{:S(2)}, u32[]{:S(2)}) async-start(bf16[16,256,256]{2,1,0:T(8,128)(2,1)} %bitcast.33), calls=%async_computation.1 | async-start | bytes 4194304 | tf_op jit(solution)/shard_map/all_to_all | solution.py:72
  71.8 32.0 %all-gather.5.cloned.1.call-done.tile_ref = bf16[4096,256]{1,0:T(8,128)(2,1)} async-done(((bf16[256,256]{1,0:T(8,128)(2,1)}), bf16[4096,256]{1,0:T(8,128)(2,1)}) %all-gather.5.cloned.1.call-update) | async-done | bytes 2097168 | tf_op jit(solution)/shard_map/all_gather | solution.py:102
  103.8 12.4 %shard_map.94 = bf16[4096,256]{1,0:T(8,128)(2,1)} custom-call(s32[32]{0:T(128)} %bitcast.37, s32[32]{0:T(128)} %bitcast.41, s32[1]{0:T(128)} %bitcast.22.live, bf16[32,128,128]{2,1,0:T(8,128)(2,1)} %bitcast.27, bf16[4096,256]{1,0:T(8,128)(2,1)} %all-gather.5.cloned.1.call-done.tile_ref), custom_call_target="tpu_custom_call" | custom-call | tf_op jit(solution)/shard_map/pallas_call | solution.py:61
  116.3 9.5 %all-to-all-done.1 = bf16[16,256,256]{2,1,0:T(8,128)(2,1)S(1)} async-done(((bf16[16,256,256]{2,1,0:T(8,128)(2,1)}), bf16[16,256,256]{2,1,0:T(8,128)(2,1)S(1)}, u32[]{:S(2)}, u32[]{:S(2)}) %all-to-all-start.1) | async-done | bytes 2097184 | tf_op jit(solution)/shard_map/all_to_all | solution.py:72
  125.8 4.4 all-to-all-start
  130.2 0.0 copy-start.2
  130.2 0.0 all-gather.11.cloned.1.call-start
  130.3 0.3 convert_reduce_fusion
  130.6 49.0 %all-to-all-done = bf16[16,256,256]{2,1,0:T(8,128)(2,1)} async-done(((bf16[16,256,256]{2,1,0:T(8,128)(2,1)}), bf16[16,256,256]{2,1,0:T(8,128)(2,1)}, u32[]{:S(2)}, u32[]{:S(2)}) %all-to-all-start) | async-done | bytes 2097184 | tf_op jit(solution)/shard_map/all_to_all | solution.py:72
  179.6 1.9 convert_reduce_fusion.1
  181.5 0.9 multiply_convert_fusion
  182.4 0.0 all-gather.11.cloned.1.call-update
  182.5 0.0 all-gather.9.cloned.1.call-start
  182.5 0.5 all-gather.9.cloned.1.call-update
  183.0 62.0 %all-gather.11.cloned.1.call-done.tile_ref = bf16[4096,256]{1,0:T(8,128)(2,1)} async-done(((bf16[256,256]{1,0:T(8,128)(2,1)}), bf16[4096,256]{1,0:T(8,128)(2,1)}) %all-gather.11.cloned.1.call-update) | async-done | bytes 2097168 | tf_op jit(solution)/shard_map/all_gather | solution.py:110
  245.0 12.8 %shard_map.97 = bf16[4096,256]{1,0:T(8,128)(2,1)} custom-call(s32[32]{0:T(128)} %bitcast.42, s32[32]{0:T(128)} %bitcast.38, s32[1]{0:T(128)} %bitcast.25.live, bf16[32,128,128]{2,1,0:T(8,128)(2,1)} %bitcast.28, bf16[4096,256]{1,0:T(8,128)(2,1)} %all-gather.11.cloned.1.call-done.tile_ref), custom_call_target="tpu_custom_call" | custom-call | tf_op jit(solution)/shard_map/pallas_call | solution.py:61
  257.9 10.2 %all-to-all-start.3 = ((bf16[16,256,256]{2,1,0:T(8,128)(2,1)}), bf16[16,256,256]{2,1,0:T(8,128)(2,1)S(1)}, u32[]{:S(2)}, u32[]{:S(2)}) async-start(bf16[16,256,256]{2,1,0:T(8,128)(2,1)} %bitcast.32), calls=%async_computation.3 | async-start | bytes 4194304 | tf_op jit(solution)/shard_map/all_to_all | solution.py:72
  268.0 45.3 %all-gather.9.cloned.1.call-done.tile_ref = bf16[4096,256]{1,0:T(8,128)(2,1)} async-done(((bf16[256,256]{1,0:T(8,128)(2,1)}), bf16[4096,256]{1,0:T(8,128)(2,1)}) %all-gather.9.cloned.1.call-update) | async-done | bytes 2097168 | tf_op jit(solution)/shard_map/all_gather | solution.py:110
  313.4 12.8 %shard_map.96 = bf16[4096,256]{1,0:T(8,128)(2,1)} custom-call(s32[32]{0:T(128)} %bitcast.43, s32[32]{0:T(128)} %bitcast.39, s32[1]{0:T(128)} %bitcast.24.live, bf16[32,128,128]{2,1,0:T(8,128)(2,1)} %bitcast.29, bf16[4096,256]{1,0:T(8,128)(2,1)} %all-gather.9.cloned.1.call-done.tile_ref), custom_call_target="tpu_custom_call" | custom-call | tf_op jit(solution)/shard_map/pallas_call | solution.py:61
  326.2 10.2 %all-to-all-start.2 = ((bf16[16,256,256]{2,1,0:T(8,128)(2,1)}), bf16[16,256,256]{2,1,0:T(8,128)(2,1)}, u32[]{:S(2)}, u32[]{:S(2)}) async-start(bf16[16,256,256]{2,1,0:T(8,128)(2,1)} %bitcast.31), calls=%async_computation.2 | async-start | bytes 4194304 | tf_op jit(solution)/shard_map/all_to_all | solution.py:72
  336.4 0.3 reduce_sum.63
  336.7 0.2 convolution_bitcast_fusion
  336.9 26.7 %all-to-all-done.2 = bf16[16,256,256]{2,1,0:T(8,128)(2,1)} async-done(((bf16[16,256,256]{2,1,0:T(8,128)(2,1)}), bf16[16,256,256]{2,1,0:T(8,128)(2,1)}, u32[]{:S(2)}, u32[]{:S(2)}) %all-to-all-start.2) | async-done | bytes 2097184 | tf_op jit(solution)/shard_map/all_to_all | solution.py:72
  363.6 1.9 reduce_sum.62
  365.5 0.2 convolution_bitcast_fusion.1
  365.7 0.1 pad_maximum_fusion
  365.8 0.3 copy.12
  366.1 19.4 %all_to_all.40 = f32[16,32,512]{2,1,0:T(8,128)S(1)} all-to-all(f32[16,32,512]{2,1,0:T(8,128)S(1)} %bitcast.35), channel_id=1, replica_groups=mesh['row'=16,'col'=16] {'row'}, dimensions={0} | all-to-all | bytes 2097152 | tf_op jit(solution)/shard_map/all_to_all | solution.py:72
  385.5 0.1 reduce_sum.64
  385.6 16.4 %all_to_all.41 = f32[16,2,512]{2,1,0:T(2,128)S(1)} all-to-all(f32[16,2,512]{2,1,0:T(2,128)S(1)} %reshape.34), channel_id=1, replica_groups=mesh['row'=16,'col'=16] {'col'}, dimensions={0} | all-to-all | bytes 131072 | tf_op jit(solution)/shard_map/all_to_all | solution.py:72
  402.1 13.2 %all_to_all.42 = f32[16,2,512]{2,1,0:T(2,128)S(1)} all-to-all(f32[16,2,512]{2,1,0:T(2,128)S(1)} %broadcast_in_dim.6), channel_id=1, replica_groups=mesh['row'=16,'col'=16] {'col'}, dimensions={0} | all-to-all | bytes 131072 | tf_op jit(solution)/shard_map/all_to_all | solution.py:79
  415.3 1.1 broadcast_in_dim.15
  416.4 6.7 %all-to-all-start.7 = ((f32[16,32,512]{2,1,0:T(8,128)}), f32[16,32,512]{2,1,0:T(8,128)S(1)}, u32[]{:S(2)}, u32[]{:S(2)}) async-start(f32[16,32,512]{2,1,0:T(8,128)} %broadcast_in_dim.15), calls=%async_computation.7 | async-start | bytes 2097152 | tf_op jit(solution)/shard_map/all_to_all | solution.py:79
  423.0 0.7 pad_maximum_fusion.1
  423.8 0.3 fusion.3
  424.0 1.0 fusion
  425.0 11.3 %all-to-all-done.7 = f32[16,32,512]{2,1,0:T(8,128)S(1)} async-done(((f32[16,32,512]{2,1,0:T(8,128)}), f32[16,32,512]{2,1,0:T(8,128)S(1)}, u32[]{:S(2)}, u32[]{:S(2)}) %all-to-all-start.7) | async-done | bytes 1048608 | tf_op jit(solution)/shard_map/all_to_all | solution.py:79
  436.4 1.0 copy.17
  (8 shorter events, 0.2 us)
Async XLA Ops:
  7.2 1.0 copy-start
  7.2 42.3 %all-gather.7.cloned.1.call-start = ((), (), s32[]{:S(2)}) async-start(), calls=%async_computation.9 | async-start | bytes 2228224 | tf_op jit(solution)/shard_map/all_gather | solution.py:102
  10.0 93.9 %all-gather.5.cloned.1.call-start = ((), (), s32[]{:S(2)}) async-start(), calls=%async_computation.8 | async-start | bytes 2228224 | tf_op jit(solution)/shard_map/all_gather | solution.py:102
  61.9 63.9 %all-to-all-start.1 = ((bf16[16,256,256]{2,1,0:T(8,128)(2,1)}), bf16[16,256,256]{2,1,0:T(8,128)(2,1)S(1)}, u32[]{:S(2)}, u32[]{:S(2)}) async-start(bf16[16,256,256]{2,1,0:T(8,128)(2,1)} %bitcast.33), calls=%async_computation.1 | async-start | bytes 4194304 | tf_op jit(solution)/shard_map/all_to_all | solution.py:72
  125.8 53.8 %all-to-all-start = ((bf16[16,256,256]{2,1,0:T(8,128)(2,1)}), bf16[16,256,256]{2,1,0:T(8,128)(2,1)}, u32[]{:S(2)}, u32[]{:S(2)}) async-start(bf16[16,256,256]{2,1,0:T(8,128)(2,1)} %bitcast.30), calls=%async_computation | async-start | bytes 4194304 | tf_op jit(solution)/shard_map/all_to_all | solution.py:72
  130.2 51.3 %copy-start.2 = (bf16[256,512]{1,0:T(8,128)(2,1)S(1)}, bf16[256,512]{1,0:T(8,128)(2,1)}, u32[]{:S(2)}) copy-start(bf16[256,512]{1,0:T(8,128)(2,1)} %param.13) | copy-start | bytes 786436
  130.2 114.8 %all-gather.11.cloned.1.call-start = ((), (), s32[]{:S(2)}) async-start(), calls=%async_computation.11 | async-start | bytes 2228224 | tf_op jit(solution)/shard_map/all_gather | solution.py:110
  182.5 130.9 %all-gather.9.cloned.1.call-start = ((), (), s32[]{:S(2)}) async-start(), calls=%async_computation.10 | async-start | bytes 2228224 | tf_op jit(solution)/shard_map/all_gather | solution.py:110
  257.9 68.3 %all-to-all-start.3 = ((bf16[16,256,256]{2,1,0:T(8,128)(2,1)}), bf16[16,256,256]{2,1,0:T(8,128)(2,1)S(1)}, u32[]{:S(2)}, u32[]{:S(2)}) async-start(bf16[16,256,256]{2,1,0:T(8,128)(2,1)} %bitcast.32), calls=%async_computation.3 | async-start | bytes 4194304 | tf_op jit(solution)/shard_map/all_to_all | solution.py:72
  326.2 37.4 %all-to-all-start.2 = ((bf16[16,256,256]{2,1,0:T(8,128)(2,1)}), bf16[16,256,256]{2,1,0:T(8,128)(2,1)}, u32[]{:S(2)}, u32[]{:S(2)}) async-start(bf16[16,256,256]{2,1,0:T(8,128)(2,1)} %bitcast.31), calls=%async_computation.2 | async-start | bytes 4194304 | tf_op jit(solution)/shard_map/all_to_all | solution.py:72
  402.0 21.8 %copy-start.1 = (bf16[512,512]{1,0:T(8,128)(2,1)S(1)}, bf16[512,512]{1,0:T(8,128)(2,1)}, u32[]{:S(2)}) copy-start(bf16[512,512]{1,0:T(8,128)(2,1)} %param.8) | copy-start | bytes 1572868
  416.4 20.0 %all-to-all-start.7 = ((f32[16,32,512]{2,1,0:T(8,128)}), f32[16,32,512]{2,1,0:T(8,128)S(1)}, u32[]{:S(2)}, u32[]{:S(2)}) async-start(f32[16,32,512]{2,1,0:T(8,128)} %broadcast_in_dim.15), calls=%async_computation.7 | async-start | bytes 2097152 | tf_op jit(solution)/shard_map/all_to_all | solution.py:79
Sparse Core Ops, SparseCore 0:
  10.4 39.0 all-gather.6
  51.9 51.9 all-gather.4
  182.6 62.4 all-gather.10
  247.9 65.4 all-gather.8

commit v5 on v3

--- a/solution.py
+++ b/solution.py
@@ -92,24 +92,24 @@
     block_side = values.shape[1]
     row_span = lax.axis_size("col") * local_rows
     col_span = lax.axis_size("row") * local_rows
-    projected = jnp.dot(features, weight, preferred_element_type=jnp.float32).astype(jnp.bfloat16)
-    panel = lax.all_gather(projected, "row", axis=0, tiled=True)
+    panel = lax.all_gather(features, "row", axis=0, tiled=True)
     forward_terms = block_terms(
         values, col_ids, row_ids, live_count, panel, row_span // block_side, False
     )
-    own_sum = exchange_sum(forward_terms.astype(jnp.bfloat16), "col")
+    own_mixed = exchange_sum(forward_terms, "col").astype(jnp.bfloat16)
+    own_sum = jnp.dot(own_mixed, weight, preferred_element_type=jnp.float32)
     output = jax.nn.silu(own_sum).astype(jnp.bfloat16)
     own_upstream = (cotangent.astype(jnp.float32) * silu_slope(own_sum)).astype(jnp.bfloat16)
+    weight_term = lax.dot_general(
+        own_mixed, own_upstream, (((0,), (0,)), ((), ())), preferred_element_type=jnp.float32
+    )
+    weight_part = exchange_sum(exchange_sum(weight_term, "row"), "col")
+    grad_weight = exchange_gather(exchange_gather(weight_part, "col"), "row")
     upstream = lax.all_gather(own_upstream, "col", axis=0, tiled=True)
     backward_terms = block_terms(
         values, row_ids, col_ids, live_count, upstream, col_span // block_side, True
     )
-    grad_projected = exchange_sum(backward_terms.astype(jnp.bfloat16), "row").astype(jnp.bfloat16)
-    weight_term = lax.dot_general(
-        features, grad_projected, (((0,), (0,)), ((), ())), preferred_element_type=jnp.float32
-    )
-    weight_part = exchange_sum(exchange_sum(weight_term, "row"), "col")
-    grad_weight = exchange_gather(exchange_gather(weight_part, "col"), "row")
+    grad_projected = exchange_sum(backward_terms, "row").astype(jnp.bfloat16)
     grad_features = lax.dot_general(
         grad_projected, weight, (((1,), (1,)), ((), ())), preferred_element_type=jnp.float32
     ).astype(jnp.bfloat16)

time: 410 us -> 363 us (0.89)
  blocking collectives: 223 us -> 168 us
  starting transfers between devices: 6.75 us -> 24.7 us
  waiting for transfers between devices: 126 us -> 118 us
    all_to_all x0 -> x1, waiting for transfers between devices: none -> 60.4 us  [exchange_sum(): pieces = lax.all_to_all(pieces, axis_name, 0, 0, tiled=False)]
    all_gather x1, waiting for transfers between devices: 72.1 us -> 13.7 us  [shards(): upstream = lax.all_gather(own_upstream, 'col', axis=0, tiled=True)]
    all_to_all x4 -> x3, blocking collectives: 210 us -> 154 us  [exchange_sum(): pieces = lax.all_to_all(pieces, axis_name, 0, 0, tiled=False)]
    all_to_all x0 -> x1, starting transfers between devices: none -> 16.4 us  [exchange_sum(): pieces = lax.all_to_all(pieces, axis_name, 0, 0, tiled=False)]
    all_to_all x1, waiting for transfers between devices: 12.3 us -> 0.01 us  [exchange_gather(): pieces = lax.all_to_all(pieces, axis_name, 0, 0, tiled=False)]
  transfers between devices with their start and end apart: 3 -> 4, of which waited for: 3 -> 3; matrix products, arithmetic and copies ran while one was open for 0% -> 1% of each run, Pallas kernels for 0% -> 3%
where the time goes in v5:
time: 363 us; the launch traced here: 357 us
  blocking collectives  168 us (46%)
  waiting for transfers between devices  118 us (33%)
  starting transfers between devices  24.7 us (7%)
  Pallas kernels  19.1 us (5%)
  between operations  14.7 us (4%)
  other arithmetic  5.84 us (2%)
    all_to_all x3, blocking collectives, exchange_sum(): pieces = lax.all_to_all(pieces, axis_name, 0, 0, tiled=False)  154 us
    all_to_all x1, waiting for transfers between devices, exchange_sum(): pieces = lax.all_to_all(pieces, axis_name, 0, 0, tiled=False)  60.4 us
    all_gather x1, waiting for transfers between devices, shards(): panel = lax.all_gather(features, 'row', axis=0, tiled=True)  43.6 us
    pallas_call x2, Pallas kernels, block_terms(): pl.pallas_call(functools.partial(block_kernel, transpose=transpose), grid...  19.1 us
    all_to_all x1, starting transfers between devices, exchange_sum(): pieces = lax.all_to_all(pieces, axis_name, 0, 0, tiled=False)  16.4 us
    all_to_all x1, blocking collectives, exchange_gather(): pieces = lax.all_to_all(pieces, axis_name, 0, 0, tiled=False)  14.4 us
    all_gather x1, waiting for transfers between devices, shards(): upstream = lax.all_gather(own_upstream, 'col', axis=0, tiled=True)  13.7 us
    all_to_all x1, starting transfers between devices, exchange_gather(): pieces = lax.all_to_all(pieces, axis_name, 0, 0, tiled=False)  8.17 us
  transfers between devices with their start and end apart: 4, of which 3 were waited for; matrix products, arithmetic and copies ran while one was open for 1% of the time, Pallas kernels for 3%

profile of v5, /device:TPU:2, one launch (start us, length us, event | category | flops | bytes accessed | tf_op | source)
XLA Modules:
  0.0 356.8 jit_solution(9116934526676792572)
XLA Ops:
  7.2 0.0 copy-start
  7.2 0.0 all-gather.3.cloned.1.call-start
  7.2 0.7 all-gather.3.cloned.1.call-update
  7.9 0.0 all-gather.5.cloned.1.call-start
  8.6 43.6 %all-gather.3.cloned.1.call-done.tile_ref = bf16[4096,512]{1,0:T(8,128)(2,1)} async-done(((bf16[256,512]{1,0:T(8,128)(2,1)}), bf16[4096,512]{1,0:T(8,128)(2,1)}) %all-gather.3.cloned.1.call-update) | async-done | bytes 4194320 | tf_op jit(solution)/shard_map/all_gather | solution.py:95
  52.2 9.5 %shard_map.94 = bf16[4096,512]{1,0:T(8,128)(2,1)} custom-call(s32[32]{0:T(128)} %bitcast.26, s32[32]{0:T(128)} %bitcast.28, s32[1]{0:T(128)} %bitcast.17.live, bf16[32,128,128]{2,1,0:T(8,128)(2,1)} %bitcast.21, bf16[4096,512]{1,0:T(8,128)(2,1)} %all-gather.3.cloned.1.call-done.tile_ref), custom_call_target="tpu_custom_call" | custom-call | tf_op jit(solution)/shard_map/pallas_call | solution.py:59
  61.7 113.9 %all_to_all.30 = bf16[16,256,512]{2,1,0:T(8,128)(2,1)} all-to-all(bf16[16,256,512]{2,1,0:T(8,128)(2,1)} %bitcast.20), channel_id=1, replica_groups=mesh['row'=16,'col'=16] {'col'}, dimensions={0} | all-to-all | bytes 8388608 | tf_op jit(solution)/shard_map/all_to_all | solution.py:70
  175.6 0.0 copy-start.1
  175.6 2.9 reduce_sum.42
  178.5 0.0 copy-done
  178.5 0.0 copy-done.1
  178.5 1.3 multiply_convert_fusion
  179.8 0.0 all-gather.5.cloned.1.call-update
  179.8 0.1 copy.13
  179.9 1.2 fusion
  181.2 26.1 %all_to_all.31 = f32[16,32,512]{2,1,0:T(8,128)S(1)} all-to-all(f32[16,32,512]{2,1,0:T(8,128)S(1)} %fusion), channel_id=1, replica_groups=mesh['row'=16,'col'=16] {'row'}, dimensions={0} | all-to-all | bytes 2097152 | tf_op jit(solution)/shard_map/all_to_all | solution.py:70
  207.3 0.1 reduce_sum.44
  207.4 13.8 %all_to_all.32 = f32[16,2,512]{2,1,0:T(2,128)S(1)} all-to-all(f32[16,2,512]{2,1,0:T(2,128)S(1)} %reshape.24), channel_id=1, replica_groups=mesh['row'=16,'col'=16] {'col'}, dimensions={0} | all-to-all | bytes 131072 | tf_op jit(solution)/shard_map/all_to_all | solution.py:70
  221.2 14.4 %all_to_all.33 = f32[16,2,512]{2,1,0:T(2,128)S(1)} all-to-all(f32[16,2,512]{2,1,0:T(2,128)S(1)} %broadcast_in_dim.6), channel_id=1, replica_groups=mesh['row'=16,'col'=16] {'col'}, dimensions={0} | all-to-all | bytes 131072 | tf_op jit(solution)/shard_map/all_to_all | solution.py:77
  235.7 1.1 broadcast_in_dim.15
  236.8 8.2 %all-to-all-start.5 = ((f32[16,32,512]{2,1,0:T(8,128)}), f32[16,32,512]{2,1,0:T(8,128)S(1)}, u32[]{:S(2)}, u32[]{:S(2)}) async-start(f32[16,32,512]{2,1,0:T(8,128)} %broadcast_in_dim.15), calls=%async_computation.5 | async-start | bytes 2097152 | tf_op jit(solution)/shard_map/all_to_all | solution.py:77
  244.9 13.7 %all-gather.5.cloned.1.call-done.tile_ref = bf16[4096,512]{1,0:T(8,128)(2,1)} async-done(((bf16[256,512]{1,0:T(8,128)(2,1)}), bf16[4096,512]{1,0:T(8,128)(2,1)}) %all-gather.5.cloned.1.call-update) | async-done | bytes 4194320 | tf_op jit(solution)/shard_map/all_gather | solution.py:108
  258.7 9.6 %shard_map.95 = bf16[4096,512]{1,0:T(8,128)(2,1)} custom-call(s32[32]{0:T(128)} %bitcast.29, s32[32]{0:T(128)} %bitcast.27, s32[1]{0:T(128)} %bitcast.18.live, bf16[32,128,128]{2,1,0:T(8,128)(2,1)} %bitcast.22, bf16[4096,512]{1,0:T(8,128)(2,1)} %all-gather.5.cloned.1.call-done.tile_ref), custom_call_target="tpu_custom_call" | custom-call | tf_op jit(solution)/shard_map/pallas_call | solution.py:59
  268.3 0.0 all-to-all-done.5
  268.3 16.4 %all-to-all-start.1 = ((bf16[16,256,512]{2,1,0:T(8,128)(2,1)}), bf16[16,256,512]{2,1,0:T(8,128)(2,1)}, u32[]{:S(2)}, u32[]{:S(2)}) async-start(bf16[16,256,512]{2,1,0:T(8,128)(2,1)} %bitcast.19), calls=%async_computation.1 | async-start | bytes 8388608 | tf_op jit(solution)/shard_map/all_to_all | solution.py:70
  284.7 60.4 %all-to-all-done.1 = bf16[16,256,512]{2,1,0:T(8,128)(2,1)} async-done(((bf16[16,256,512]{2,1,0:T(8,128)(2,1)}), bf16[16,256,512]{2,1,0:T(8,128)(2,1)}, u32[]{:S(2)}, u32[]{:S(2)}) %all-to-all-start.1) | async-done | bytes 4194336 | tf_op jit(solution)/shard_map/all_to_all | solution.py:70
  345.1 2.8 reduce_sum.43
  348.0 1.0 convolution_convert_fusion
  349.0 1.0 copy.18
  (4 shorter events, 0.1 us)
Async XLA Ops:
  7.2 171.3 %copy-start = (bf16[512,512]{1,0:T(8,128)(2,1)S(1)}, bf16[512,512]{1,0:T(8,128)(2,1)}, u32[]{:S(2)}) copy-start(bf16[512,512]{1,0:T(8,128)(2,1)} %param.8) | copy-start | bytes 1572868
  7.2 45.0 %all-gather.3.cloned.1.call-start = ((), (), s32[]{:S(2)}) async-start(), calls=%async_computation.6 | async-start | bytes 4456448 | tf_op jit(solution)/shard_map/all_gather | solution.py:95
  7.9 250.7 %all-gather.5.cloned.1.call-start = ((), (), s32[]{:S(2)}) async-start(), calls=%async_computation.7 | async-start | bytes 4456448 | tf_op jit(solution)/shard_map/all_gather | solution.py:108
  175.6 2.9 copy-start.1
  236.8 31.5 %all-to-all-start.5 = ((f32[16,32,512]{2,1,0:T(8,128)}), f32[16,32,512]{2,1,0:T(8,128)S(1)}, u32[]{:S(2)}, u32[]{:S(2)}) async-start(f32[16,32,512]{2,1,0:T(8,128)} %broadcast_in_dim.15), calls=%async_computation.5 | async-start | bytes 2097152 | tf_op jit(solution)/shard_map/all_to_all | solution.py:77
  268.3 76.8 %all-to-all-start.1 = ((bf16[16,256,512]{2,1,0:T(8,128)(2,1)}), bf16[16,256,512]{2,1,0:T(8,128)(2,1)}, u32[]{:S(2)}, u32[]{:S(2)}) async-start(bf16[16,256,512]{2,1,0:T(8,128)(2,1)} %bitcast.19), calls=%async_computation.1 | async-start | bytes 8388608 | tf_op jit(solution)/shard_map/all_to_all | solution.py:70
Sparse Core Ops, SparseCore 0:
  9.8 42.3 all-gather.2
  179.9 78.6 all-gather.4

commit v6 on v5

--- a/solution.py
+++ b/solution.py
@@ -6,25 +6,31 @@
 from jax.experimental.pallas import tpu as pltpu
 from jax.sharding import PartitionSpec as P
 
+GROUP = 4
 
-def block_kernel(source_ids, target_ids, live, values_ref, tile_ref, out_ref, acc_ref, *, transpose):
-    k = pl.program_id(0)
 
-    @pl.when(k == 0)
+def block_kernel(source_ids, target_ids, live, values_ref, *refs, transpose):
+    tile_refs, out_ref, acc_ref = refs[:-2], refs[-2], refs[-1]
+    step = pl.program_id(0)
+    group = len(tile_refs)
+
+    @pl.when(step == 0)
     def _():
         acc_ref[...] = jnp.zeros_like(acc_ref)
 
-    @pl.when(k < live[0])
-    def _():
-        block = values_ref[...]
-        if transpose:
-            term = lax.dot_general(block, tile_ref[...], (((0,), (0,)), ((), ())), preferred_element_type=jnp.float32)
-        else:
-            term = jnp.dot(block, tile_ref[...], preferred_element_type=jnp.float32)
-        target = target_ids[k]
-        acc_ref[target] += term
+    for slot, tile_ref in enumerate(tile_refs):
+        entry = step * group + slot
 
-    @pl.when(k == pl.num_programs(0) - 1)
+        @pl.when(entry < live[0])
+        def _():
+            block = values_ref[slot]
+            if transpose:
+                term = lax.dot_general(block, tile_ref[...], (((0,), (0,)), ((), ())), preferred_element_type=jnp.float32)
+            else:
+                term = jnp.dot(block, tile_ref[...], preferred_element_type=jnp.float32)
+            acc_ref[target_ids[entry]] += term
+
+    @pl.when(step == pl.num_programs(0) - 1)
     def _():
         out_ref[...] = acc_ref[...].reshape(out_ref.shape).astype(out_ref.dtype)
 
@@ -32,27 +38,25 @@
 def block_terms(values, source_ids, target_ids, live_count, source, target_blocks, transpose):
     entry_total, block_side, _ = values.shape
     feature_count = source.shape[1]
+    group = GROUP
     live = jnp.reshape(live_count, (1,)).astype(jnp.int32)
 
-    def entry_of(k, live):
-        return jnp.minimum(k, live[0] - 1)
+    def values_map(step, source_ids, target_ids, live):
+        return (jnp.minimum(step, (live[0] - 1) // group), 0, 0)
 
-    def values_map(k, source_ids, target_ids, live):
-        return (entry_of(k, live), 0, 0)
+    def tile_map_of(slot):
+        def tile_map(step, source_ids, target_ids, live):
+            return (source_ids[jnp.minimum(step * group + slot, live[0] - 1)], 0)
+        return tile_map
 
-    def tile_map(k, source_ids, target_ids, live):
-        return (source_ids[entry_of(k, live)], 0)
-
-    def out_map(k, source_ids, target_ids, live):
+    def out_map(step, source_ids, target_ids, live):
         return (0, 0)
 
     grid_spec = pltpu.PrefetchScalarGridSpec(
         num_scalar_prefetch=3,
-        grid=(entry_total,),
-        in_specs=[
-            pl.BlockSpec((None, block_side, block_side), values_map),
-            pl.BlockSpec((block_side, feature_count), tile_map),
-        ],
+        grid=(entry_total // group,),
+        in_specs=[pl.BlockSpec((group, block_side, block_side), values_map)]
+        + [pl.BlockSpec((block_side, feature_count), tile_map_of(slot)) for slot in range(group)],
         out_specs=pl.BlockSpec((target_blocks * block_side, feature_count), out_map),
         scratch_shapes=[pltpu.VMEM((target_blocks, block_side, feature_count), jnp.float32)],
     )
@@ -61,7 +65,7 @@
         grid_spec=grid_spec,
         out_shape=jax.ShapeDtypeStruct((target_blocks * block_side, feature_count), jnp.bfloat16),
         compiler_params=pltpu.CompilerParams(dimension_semantics=("arbitrary",)),
-    )(source_ids, target_ids, live, values, source)
+    )(source_ids, target_ids, live, values, *([source] * group))
 
 
 def exchange_sum(parts, axis_name):

time: 363 us -> 348 us (0.959)
  blocking collectives: 168 us -> 161 us
  starting transfers between devices: 24.7 us -> 17.8 us
    all_to_all x3, blocking collectives: 154 us -> 146 us  [exchange_sum(): pieces = lax.all_to_all(pieces, axis_name, 0, 0, tiled=False)]
    all_to_all x1, starting transfers between devices: 16.4 us -> 9.48 us  [exchange_sum(): pieces = lax.all_to_all(pieces, axis_name, 0, 0, tiled=False)]
where the time goes in v6:
time: 348 us; the launch traced here: 344 us
  blocking collectives  161 us (46%)
  waiting for transfers between devices  120 us (34%)
  Pallas kernels  18.8 us (5%)
  starting transfers between devices  17.8 us (5%)
  between operations  14.7 us (4%)
  other arithmetic  5.84 us (2%)
  matrix products  3.55 us (1%)
    all_to_all x3, blocking collectives, exchange_sum(): pieces = lax.all_to_all(pieces, axis_name, 0, 0, tiled=False)  146 us
    all_to_all x1, waiting for transfers between devices, exchange_sum(): pieces = lax.all_to_all(pieces, axis_name, 0, 0, tiled=False)  60.4 us
    all_gather x1, waiting for transfers between devices, shards(): panel = lax.all_gather(features, 'row', axis=0, tiled=True)  43.6 us
    pallas_call x2, Pallas kernels, block_terms(): pl.pallas_call(functools.partial(block_kernel, transpose=transpose), grid...  18.8 us
    all_to_all x1, blocking collectives, exchange_gather(): pieces = lax.all_to_all(pieces, axis_name, 0, 0, tiled=False)  15.3 us
    all_gather x1, waiting for transfers between devices, shards(): upstream = lax.all_gather(own_upstream, 'col', axis=0, tiled=True)  15.1 us
    all_to_all x1, starting transfers between devices, exchange_sum(): pieces = lax.all_to_all(pieces, axis_name, 0, 0, tiled=False)  9.48 us
    all_to_all x1, starting transfers between devices, exchange_gather(): pieces = lax.all_to_all(pieces, axis_name, 0, 0, tiled=False)  8.29 us
  transfers between devices with their start and end apart: 4, of which 3 were waited for; matrix products, arithmetic and copies ran while one was open for 1% of the time, Pallas kernels for 3%

profile of v6, /device:TPU:2, one launch (start us, length us, event | category | flops | bytes accessed | tf_op | source)
XLA Modules:
  0.0 344.3 jit_solution(15105902997760232903)
XLA Ops:
  7.2 0.0 copy-start
  7.2 0.0 all-gather.3.cloned.1.call-start
  7.2 0.7 all-gather.3.cloned.1.call-update
  7.9 0.0 all-gather.5.cloned.1.call-start
  8.6 43.6 %all-gather.3.cloned.1.call-done.refs_0_.refs_1_.refs_2_.refs_3_ = bf16[4096,512]{1,0:T(8,128)(2,1)} async-done(((bf16[256,512]{1,0:T(8,128)(2,1)}), bf16[4096,512]{1,0:T(8,128)(2,1)}) %all-gather.3.cloned.1.call-update) | async-done | bytes 4194320 | tf_op jit(solution)/shard_map/all_gather | solution.py:99
  52.2 9.2 %shard_map.94 = bf16[4096,512]{1,0:T(8,128)(2,1)} custom-call(s32[32]{0:T(128)} %bitcast.26, s32[32]{0:T(128)} %bitcast.28, s32[1]{0:T(128)} %bitcast.17.live, bf16[32,128,128]{2,1,0:T(8,128)(2,1)} %bitcast.21, bf16[4096,512]{1,0:T(8,128)(2,1)} %all-gather.3.cloned.1.call-done.refs_0_.refs_1_.refs_2_.refs_3_, ...), custom_call_target="tpu_custom_call" | custom-call | tf_op jit(solution)/shard_map/pallas_call | solution.py:63
  61.4 107.8 %all_to_all.30 = bf16[16,256,512]{2,1,0:T(8,128)(2,1)} all-to-all(bf16[16,256,512]{2,1,0:T(8,128)(2,1)} %bitcast.20), channel_id=1, replica_groups=mesh['row'=16,'col'=16] {'col'}, dimensions={0} | all-to-all | bytes 8388608 | tf_op jit(solution)/shard_map/all_to_all | solution.py:74
  169.2 0.0 copy-start.1
  169.2 2.9 reduce_sum.42
  172.1 0.0 copy-done
  172.1 0.0 copy-done.1
  172.1 1.3 multiply_convert_fusion
  173.4 0.0 all-gather.5.cloned.1.call-update
  173.4 0.1 copy.13
  173.6 1.2 fusion
  174.8 23.7 %all_to_all.31 = f32[16,32,512]{2,1,0:T(8,128)S(1)} all-to-all(f32[16,32,512]{2,1,0:T(8,128)S(1)} %fusion), channel_id=1, replica_groups=mesh['row'=16,'col'=16] {'row'}, dimensions={0} | all-to-all | bytes 2097152 | tf_op jit(solution)/shard_map/all_to_all | solution.py:74
  198.4 0.1 reduce_sum.44
  198.6 14.6 %all_to_all.32 = f32[16,2,512]{2,1,0:T(2,128)S(1)} all-to-all(f32[16,2,512]{2,1,0:T(2,128)S(1)} %reshape.24), channel_id=1, replica_groups=mesh['row'=16,'col'=16] {'col'}, dimensions={0} | all-to-all | bytes 131072 | tf_op jit(solution)/shard_map/all_to_all | solution.py:74
  213.2 15.3 %all_to_all.33 = f32[16,2,512]{2,1,0:T(2,128)S(1)} all-to-all(f32[16,2,512]{2,1,0:T(2,128)S(1)} %broadcast_in_dim.6), channel_id=1, replica_groups=mesh['row'=16,'col'=16] {'col'}, dimensions={0} | all-to-all | bytes 131072 | tf_op jit(solution)/shard_map/all_to_all | solution.py:81
  228.6 1.1 broadcast_in_dim.15
  229.7 8.3 %all-to-all-start.5 = ((f32[16,32,512]{2,1,0:T(8,128)}), f32[16,32,512]{2,1,0:T(8,128)S(1)}, u32[]{:S(2)}, u32[]{:S(2)}) async-start(f32[16,32,512]{2,1,0:T(8,128)} %broadcast_in_dim.15), calls=%async_computation.5 | async-start | bytes 2097152 | tf_op jit(solution)/shard_map/all_to_all | solution.py:81
  238.0 15.1 %all-gather.5.cloned.1.call-done.refs_0_.refs_1_.refs_2_.refs_3_ = bf16[4096,512]{1,0:T(8,128)(2,1)} async-done(((bf16[256,512]{1,0:T(8,128)(2,1)}), bf16[4096,512]{1,0:T(8,128)(2,1)}) %all-gather.5.cloned.1.call-update) | async-done | bytes 4194320 | tf_op jit(solution)/shard_map/all_gather | solution.py:112
  253.1 9.6 %shard_map.95 = bf16[4096,512]{1,0:T(8,128)(2,1)} custom-call(s32[32]{0:T(128)} %bitcast.29, s32[32]{0:T(128)} %bitcast.27, s32[1]{0:T(128)} %bitcast.18.live, bf16[32,128,128]{2,1,0:T(8,128)(2,1)} %bitcast.22, bf16[4096,512]{1,0:T(8,128)(2,1)} %all-gather.5.cloned.1.call-done.refs_0_.refs_1_.refs_2_.refs_3_, ...), custom_call_target="tpu_custom_call" | custom-call | tf_op jit(solution)/shard_map/pallas_call | solution.py:63
  262.7 0.0 all-to-all-done.5
  262.7 9.5 %all-to-all-start.1 = ((bf16[16,256,512]{2,1,0:T(8,128)(2,1)}), bf16[16,256,512]{2,1,0:T(8,128)(2,1)}, u32[]{:S(2)}, u32[]{:S(2)}) async-start(bf16[16,256,512]{2,1,0:T(8,128)(2,1)} %bitcast.19), calls=%async_computation.1 | async-start | bytes 8388608 | tf_op jit(solution)/shard_map/all_to_all | solution.py:74
  272.2 60.4 %all-to-all-done.1 = bf16[16,256,512]{2,1,0:T(8,128)(2,1)} async-done(((bf16[16,256,512]{2,1,0:T(8,128)(2,1)}), bf16[16,256,512]{2,1,0:T(8,128)(2,1)}, u32[]{:S(2)}, u32[]{:S(2)}) %all-to-all-start.1) | async-done | bytes 4194336 | tf_op jit(solution)/shard_map/all_to_all | solution.py:74
  332.6 2.8 reduce_sum.43
  335.4 1.0 convolution_convert_fusion
  336.5 1.0 copy.18
  (4 shorter events, 0.1 us)
Async XLA Ops:
  7.2 164.9 %copy-start = (bf16[512,512]{1,0:T(8,128)(2,1)S(1)}, bf16[512,512]{1,0:T(8,128)(2,1)}, u32[]{:S(2)}) copy-start(bf16[512,512]{1,0:T(8,128)(2,1)} %param.8) | copy-start | bytes 1572868
  7.2 45.0 %all-gather.3.cloned.1.call-start = ((), (), s32[]{:S(2)}) async-start(), calls=%async_computation.6 | async-start | bytes 4456448 | tf_op jit(solution)/shard_map/all_gather | solution.py:99
  7.9 245.1 %all-gather.5.cloned.1.call-start = ((), (), s32[]{:S(2)}) async-start(), calls=%async_computation.7 | async-start | bytes 4456448 | tf_op jit(solution)/shard_map/all_gather | solution.py:112
  169.2 2.9 copy-start.1
  229.7 33.0 %all-to-all-start.5 = ((f32[16,32,512]{2,1,0:T(8,128)}), f32[16,32,512]{2,1,0:T(8,128)S(1)}, u32[]{:S(2)}, u32[]{:S(2)}) async-start(f32[16,32,512]{2,1,0:T(8,128)} %broadcast_in_dim.15), calls=%async_computation.5 | async-start | bytes 2097152 | tf_op jit(solution)/shard_map/all_to_all | solution.py:81
  262.7 69.9 %all-to-all-start.1 = ((bf16[16,256,512]{2,1,0:T(8,128)(2,1)}), bf16[16,256,512]{2,1,0:T(8,128)(2,1)}, u32[]{:S(2)}, u32[]{:S(2)}) async-start(bf16[16,256,512]{2,1,0:T(8,128)(2,1)} %bitcast.19), calls=%async_computation.1 | async-start | bytes 8388608 | tf_op jit(solution)/shard_map/all_to_all | solution.py:74
Sparse Core Ops, SparseCore 0:
  9.8 42.3 all-gather.2
  173.5 79.4 all-gather.4

commit v7 on v6

--- a/solution.py
+++ b/solution.py
@@ -4,7 +4,7 @@
 from jax import lax
 from jax.experimental import pallas as pl
 from jax.experimental.pallas import tpu as pltpu
-from jax.sharding import PartitionSpec as P
+from jax.sharding import Mesh, PartitionSpec as P
 
 GROUP = 4
 
@@ -68,15 +68,27 @@
     )(source_ids, target_ids, live, values, *([source] * group))
 
 
-def exchange_sum(parts, axis_name):
-    count = lax.axis_size(axis_name)
+ROW = ("zl", "x", "core")
+COL = ("zh", "y")
+
+
+def exchange_sum(parts, axis_name, count):
     pieces = parts.reshape((count, -1) + parts.shape[1:])
     pieces = lax.all_to_all(pieces, axis_name, 0, 0, tiled=False)
     return pieces.astype(jnp.float32).sum(0)
 
 
-def exchange_gather(part, axis_name):
-    count = lax.axis_size(axis_name)
+def staged_sum(parts, axes, sizes):
+    pieces = parts.reshape(tuple(sizes) + (-1,) + parts.shape[1:])
+    for position in reversed(range(len(axes))):
+        pieces = lax.all_to_all(pieces, axes[position], position, position, tiled=False)
+        pieces = pieces.astype(jnp.float32).sum(position)
+        if position > 0:
+            pieces = pieces.astype(jnp.bfloat16)
+    return pieces
+
+
+def exchange_gather(part, axis_name, count):
     pieces = jnp.broadcast_to(part[None], (count,) + part.shape)
     pieces = lax.all_to_all(pieces, axis_name, 0, 0, tiled=False)
     return pieces.reshape((-1,) + part.shape[1:])
@@ -94,26 +106,30 @@
     live_count = entry_counts[0, 0]
     local_rows = features.shape[0]
     block_side = values.shape[1]
-    row_span = lax.axis_size("col") * local_rows
-    col_span = lax.axis_size("row") * local_rows
-    panel = lax.all_gather(features, "row", axis=0, tiled=True)
+    row_sizes = [lax.axis_size(name) for name in ROW]
+    col_sizes = [lax.axis_size(name) for name in COL]
+    row_count = row_sizes[0] * row_sizes[1] * row_sizes[2]
+    col_count = col_sizes[0] * col_sizes[1]
+    row_span = col_count * local_rows
+    col_span = row_count * local_rows
+    panel = lax.all_gather(features, ROW, axis=0, tiled=True)
     forward_terms = block_terms(
         values, col_ids, row_ids, live_count, panel, row_span // block_side, False
     )
-    own_mixed = exchange_sum(forward_terms, "col").astype(jnp.bfloat16)
+    own_mixed = staged_sum(forward_terms, COL, col_sizes).astype(jnp.bfloat16)
     own_sum = jnp.dot(own_mixed, weight, preferred_element_type=jnp.float32)
     output = jax.nn.silu(own_sum).astype(jnp.bfloat16)
     own_upstream = (cotangent.astype(jnp.float32) * silu_slope(own_sum)).astype(jnp.bfloat16)
     weight_term = lax.dot_general(
         own_mixed, own_upstream, (((0,), (0,)), ((), ())), preferred_element_type=jnp.float32
     )
-    weight_part = exchange_sum(exchange_sum(weight_term, "row"), "col")
-    grad_weight = exchange_gather(exchange_gather(weight_part, "col"), "row")
-    upstream = lax.all_gather(own_upstream, "col", axis=0, tiled=True)
+    weight_part = exchange_sum(exchange_sum(weight_term, ROW, row_count), COL, col_count)
+    grad_weight = exchange_gather(exchange_gather(weight_part, COL, col_count), ROW, row_count)
+    upstream = lax.all_gather(own_upstream, COL, axis=0, tiled=True)
     backward_terms = block_terms(
         values, row_ids, col_ids, live_count, upstream, col_span // block_side, True
     )
-    grad_projected = exchange_sum(backward_terms, "row").astype(jnp.bfloat16)
+    grad_projected = staged_sum(backward_terms, ROW, row_sizes).astype(jnp.bfloat16)
     grad_features = lax.dot_general(
         grad_projected, weight, (((1,), (1,)), ((), ())), preferred_element_type=jnp.float32
     ).astype(jnp.bfloat16)
@@ -121,19 +137,22 @@
 
 
 def solution(mesh):
+    row_parts = (2, 4, 2)
+    col_parts = (4, 4)
+    split = Mesh(mesh.devices.reshape(row_parts + col_parts), ROW + COL)
     placed = (
-        P(("col", "row"), None),
+        P(COL + ROW, None),
         P(),
-        P("row", "col", None, None, None),
-        P("row", "col", None),
-        P("row", "col", None),
-        P("row", "col"),
-        P(("row", "col"), None),
+        P(ROW, COL, None, None, None),
+        P(ROW, COL, None),
+        P(ROW, COL, None),
+        P(ROW, COL),
+        P(ROW + COL, None),
     )
     return jax.shard_map(
         shards,
-        mesh=mesh,
+        mesh=split,
         in_specs=placed,
-        out_specs=(P(("row", "col"), None), P(("col", "row"), None), P()),
+        out_specs=(P(ROW + COL, None), P(COL + ROW, None), P()),
         check_vma=False,
     )

time: 348 us -> 342 us (0.983)
  blocking collectives: 161 us -> 135 us
  local copies, waits for them, and re-layouts: 2.32 us -> 11 us
  waiting for transfers between devices: 120 us -> 127 us
  starting transfers between devices: 17.8 us -> 23.7 us
  Pallas kernels: 18.8 us -> 15.1 us
    all_to_all x3 -> x2, blocking collectives: 146 us -> 41.5 us  [exchange_sum(): pieces = lax.all_to_all(pieces, axis_name, 0, 0, tiled=False)]
    all_to_all x1 -> x3, blocking collectives: 15.3 us -> 93.7 us  [staged_sum(): lax.all_to_all(pieces, axes[position], position, position, tiled=False)]
    all_to_all x1 -> x2, waiting for transfers between devices: 60.4 us -> 32.8 us  [staged_sum(): lax.all_to_all(pieces, axes[position], position, position, tiled=False)]
    all_gather x2, waiting for transfers between devices: 58.7 us -> 76.6 us  [the longest x1 43.6 us: shards(): panel = lax.all_gather(features, ROW, axis=0, tiled=True)]
    all_to_all x1 -> x2, waiting for transfers between devices: 0.01 us -> 17.3 us  [exchange_gather(): pieces = lax.all_to_all(pieces, axis_name, 0, 0, tiled=False)]
    reduce_sum x0 -> x5, other arithmetic: none -> 8 us  [staged_sum(): pieces = pieces.astype(jnp.float32).sum(position)]
    all_to_all x1 -> x2, starting transfers between devices: 8.29 us -> 15 us  [exchange_gather(): pieces = lax.all_to_all(pieces, axis_name, 0, 0, tiled=False)]
    reduce_sum x4 -> x2, other arithmetic: 5.84 us -> 0.11 us  [exchange_sum(): return pieces.astype(jnp.float32).sum(0)]
  transfers between devices with their start and end apart: 4 -> 6, of which waited for: 3 -> 6; matrix products, arithmetic and copies ran while one was open for 1% -> 2% of each run, Pallas kernels for 3% -> 0%
where the time goes in v7:
time: 342 us; the launch traced here: 339 us
  blocking collectives  135 us (39%)
  waiting for transfers between devices  127 us (37%)
  starting transfers between devices  23.7 us (7%)
  Pallas kernels  15.1 us (4%)
  between operations  14.8 us (4%)
  local copies, waits for them, and re-layouts  11 us (3%)
  other arithmetic  8.1 us (2%)
  matrix products  3.55 us (1%)
    all_to_all x3, blocking collectives, staged_sum(): lax.all_to_all(pieces, axes[position], position, position, tiled=False)  93.7 us
    all_gather x1, waiting for transfers between devices, shards(): panel = lax.all_gather(features, ROW, axis=0, tiled=True)  43.6 us
    all_to_all x2, blocking collectives, exchange_sum(): pieces = lax.all_to_all(pieces, axis_name, 0, 0, tiled=False)  41.5 us
    all_gather x1, waiting for transfers between devices, shards(): upstream = lax.all_gather(own_upstream, COL, axis=0, tiled=True)  33 us
    all_to_all x2, waiting for transfers between devices, staged_sum(): lax.all_to_all(pieces, axes[position], position, position, tiled=False)  32.8 us
    all_to_all x2, waiting for transfers between devices, exchange_gather(): pieces = lax.all_to_all(pieces, axis_name, 0, 0, tiled=False)  17.3 us
    pallas_call x2, Pallas kernels, block_terms(): pl.pallas_call(functools.partial(block_kernel, transpose=transpose), grid...  15.1 us
    all_to_all x2, starting transfers between devices, exchange_gather(): pieces = lax.all_to_all(pieces, axis_name, 0, 0, tiled=False)  15 us
  transfers between devices with their start and end apart: 6, of which 6 were waited for; matrix products, arithmetic and copies ran while one was open for 2% of the time, Pallas kernels for 0%

profile of v7, /device:TPU:2, one launch (start us, length us, event | category | flops | bytes accessed | tf_op | source)
XLA Modules:
  0.0 338.9 jit_solution(13289653159508865727)
XLA Ops:
  7.2 0.0 copy-start
  7.2 0.0 all-gather.3.cloned.1.call-start
  7.2 0.7 all-gather.3.cloned.1.call-update
  7.9 0.0 all-gather.5.cloned.1.call-start
  8.6 43.6 %all-gather.3.cloned.1.call-done.refs_0_.refs_1_.refs_2_.refs_3_ = bf16[4096,512]{1,0:T(8,128)(2,1)} async-done(((bf16[256,512]{1,0:T(8,128)(2,1)}), bf16[4096,512]{1,0:T(8,128)(2,1)}) %all-gather.3.cloned.1.call-update) | async-done | bytes 4194320 | tf_op jit(solution)/shard_map/all_gather | solution.py:115
  52.2 7.5 %shard_map.94 = bf16[4096,512]{1,0:T(8,128)(2,1)} custom-call(s32[32]{0:T(128)} %bitcast.25, s32[32]{0:T(128)} %bitcast.27, s32[1]{0:T(128)} %bitcast.17.live, bf16[32,128,128]{2,1,0:T(8,128)(2,1)} %bitcast.21, bf16[4096,512]{1,0:T(8,128)(2,1)} %all-gather.3.cloned.1.call-done.refs_0_.refs_1_.refs_2_.refs_3_, ...), custom_call_target="tpu_custom_call" | custom-call | tf_op jit(solution)/shard_map/pallas_call | solution.py:63
  59.7 2.6 copy.19
  62.3 54.7 %all_to_all.45 = bf16[4,4,256,512]{3,2,0,1:T(8,128)(2,1)} all-to-all(bf16[4,4,256,512]{3,2,0,1:T(8,128)(2,1)S(1)} %copy.19), channel_id=1, replica_groups=mesh['zl'=2,'x'=4,'core'=2,'zh'=4,'y'=4] {'y'}, dimensions={1} | all-to-all | bytes 8388608 | tf_op jit(solution)/shard_map/all_to_all | solution.py:84
  117.1 0.0 copy-start.1
  117.1 3.1 reduce_sum.78
  120.1 30.8 %all_to_all.46 = bf16[4,256,512]{2,1,0:T(8,128)(2,1)S(1)} all-to-all(bf16[4,256,512]{2,1,0:T(8,128)(2,1)S(1)} %reduce_sum.78), channel_id=1, replica_groups=mesh['zl'=2,'x'=4,'core'=2,'zh'=4,'y'=4] {'zh'}, dimensions={0} | all-to-all | bytes 2097152 | tf_op jit(solution)/shard_map/all_to_all | solution.py:84
  150.9 0.2 reduce_sum.79
  151.2 0.0 copy-done
  151.2 0.0 copy-done.1
  151.2 1.3 multiply_convert_fusion
  152.4 0.0 all-gather.5.cloned.1.call-update
  152.5 0.1 copy.22
  152.6 1.2 fusion
  153.9 27.5 %all_to_all.47 = f32[16,32,512]{2,1,0:T(8,128)S(1)} all-to-all(f32[16,32,512]{2,1,0:T(8,128)S(1)} %fusion), channel_id=1, replica_groups=mesh['zl'=2,'x'=4,'core'=2,'zh'=4,'y'=4] {'zl','x','core'}, dimensions={0} | all-to-all | bytes 2097152 | tf_op jit(solution)/shard_map/all_to_all | solution.py:77
  181.4 0.1 reduce_sum.83
  181.5 14.0 %all_to_all.48 = f32[16,2,512]{2,1,0:T(2,128)S(1)} all-to-all(f32[16,2,512]{2,1,0:T(2,128)S(1)} %reshape.24), channel_id=1, replica_groups=mesh['zl'=2,'x'=4,'core'=2,'zh'=4,'y'=4] {'zh','y'}, dimensions={0} | all-to-all | bytes 131072 | tf_op jit(solution)/shard_map/all_to_all | solution.py:77
  195.5 33.0 %all-gather.5.cloned.1.call-done.refs_0_.refs_1_.refs_2_.refs_3_ = bf16[4096,512]{1,0:T(8,128)(2,1)} async-done(((bf16[256,512]{1,0:T(8,128)(2,1)}), bf16[4096,512]{1,0:T(8,128)(2,1)}) %all-gather.5.cloned.1.call-update) | async-done | bytes 4194320 | tf_op jit(solution)/shard_map/all_gather | solution.py:128
  228.5 7.6 %shard_map.95 = bf16[4096,512]{1,0:T(8,128)(2,1)} custom-call(s32[32]{0:T(128)} %bitcast.28, s32[32]{0:T(128)} %bitcast.26, s32[1]{0:T(128)} %bitcast.18.live, bf16[32,128,128]{2,1,0:T(8,128)(2,1)} %bitcast.22, bf16[4096,512]{1,0:T(8,128)(2,1)} %all-gather.5.cloned.1.call-done.refs_0_.refs_1_.refs_2_.refs_3_, ...), custom_call_target="tpu_custom_call" | custom-call | tf_op jit(solution)/shard_map/pallas_call | solution.py:63
  236.1 2.6 copy.20
  238.7 8.2 %all_to_all.49 = bf16[2,4,2,256,512]{4,3,1,0,2:T(8,128)(2,1)} all-to-all(bf16[2,4,2,256,512]{4,3,1,0,2:T(8,128)(2,1)S(1)} %copy.20), channel_id=1, replica_groups=mesh['zl'=2,'x'=4,'core'=2,'zh'=4,'y'=4] {'core'}, dimensions={2} | all-to-all | bytes 8388608 | tf_op jit(solution)/shard_map/all_to_all | solution.py:84
  246.9 0.6 broadcast_in_dim.6
  247.5 9.5 %all-to-all-start.7 = ((f32[16,2,512]{2,1,0:T(2,128)}), f32[16,2,512]{2,1,0:T(2,128)S(1)}, u32[]{:S(2)}, u32[]{:S(2)}) async-start(f32[16,2,512]{2,1,0:T(2,128)} %broadcast_in_dim.6), calls=%async_computation.7 | async-start | bytes 131072 | tf_op jit(solution)/shard_map/all_to_all | solution.py:93
  257.0 3.3 reduce_sum.80
  260.3 1.6 copy.21
  261.9 5.2 %all-to-all-done.7 = f32[16,2,512]{2,1,0:T(2,128)S(1)} async-done(((f32[16,2,512]{2,1,0:T(2,128)}), f32[16,2,512]{2,1,0:T(2,128)S(1)}, u32[]{:S(2)}, u32[]{:S(2)}) %all-to-all-start.7) | async-done | bytes 65568 | tf_op jit(solution)/shard_map/all_to_all | solution.py:93
  267.1 5.2 %all-to-all-start.3 = ((bf16[2,4,256,512]{3,2,0,1:T(8,128)(2,1)}), bf16[2,4,256,512]{3,2,0,1:T(8,128)(2,1)S(1)}, u32[]{:S(2)}, u32[]{:S(2)}) async-start(bf16[2,4,256,512]{3,2,0,1:T(8,128)(2,1)} %copy.21), calls=%async_computation.3 | async-start | bytes 4194304 | tf_op jit(solution)/shard_map/all_to_all | solution.py:84
  272.3 24.0 %all-to-all-done.3 = bf16[2,4,256,512]{3,2,0,1:T(8,128)(2,1)S(1)} async-done(((bf16[2,4,256,512]{3,2,0,1:T(8,128)(2,1)}), bf16[2,4,256,512]{3,2,0,1:T(8,128)(2,1)S(1)}, u32[]{:S(2)}, u32[]{:S(2)}) %all-to-all-start.3) | async-done | bytes 2097184 | tf_op jit(solution)/shard_map/all_to_all | solution.py:84
  296.3 1.1 broadcast_in_dim.15
  297.4 5.5 %all-to-all-start.8 = ((f32[16,32,512]{2,1,0:T(8,128)}), f32[16,32,512]{2,1,0:T(8,128)}, u32[]{:S(2)}, u32[]{:S(2)}) async-start(f32[16,32,512]{2,1,0:T(8,128)} %broadcast_in_dim.15), calls=%async_computation.8 | async-start | bytes 2097152 | tf_op jit(solution)/shard_map/all_to_all | solution.py:93
  302.9 1.3 reduce_sum.81
  304.2 12.1 %all-to-all-done.8 = f32[16,32,512]{2,1,0:T(8,128)} async-done(((f32[16,32,512]{2,1,0:T(8,128)}), f32[16,32,512]{2,1,0:T(8,128)}, u32[]{:S(2)}, u32[]{:S(2)}) %all-to-all-start.8) | async-done | bytes 1048608 | tf_op jit(solution)/shard_map/all_to_all | solution.py:93
  316.3 3.5 %all-to-all-start.4 = ((bf16[2,256,512]{2,1,0:T(8,128)(2,1)}), bf16[2,256,512]{2,1,0:T(8,128)(2,1)S(1)}, u32[]{:S(2)}, u32[]{:S(2)}) async-start(bf16[2,256,512]{2,1,0:T(8,128)(2,1)} %reduce_sum.81), calls=%async_computation.4 | async-start | bytes 1048576 | tf_op jit(solution)/shard_map/all_to_all | solution.py:84
  319.8 8.8 %all-to-all-done.4 = bf16[2,256,512]{2,1,0:T(8,128)(2,1)S(1)} async-done(((bf16[2,256,512]{2,1,0:T(8,128)(2,1)}), bf16[2,256,512]{2,1,0:T(8,128)(2,1)S(1)}, u32[]{:S(2)}, u32[]{:S(2)}) %all-to-all-start.4) | async-done | bytes 524320 | tf_op jit(solution)/shard_map/all_to_all | solution.py:84
  328.6 0.1 reduce_sum.82
  328.7 1.0 convolution_convert_fusion
  329.8 2.3 copy.27
  (3 shorter events, 0.1 us)
Async XLA Ops:
  7.2 144.0 %copy-start = (bf16[512,512]{1,0:T(8,128)(2,1)S(1)}, bf16[512,512]{1,0:T(8,128)(2,1)}, u32[]{:S(2)}) copy-start(bf16[512,512]{1,0:T(8,128)(2,1)} %param.8) | copy-start | bytes 1572868
  7.2 45.0 %all-gather.3.cloned.1.call-start = ((), (), s32[]{:S(2)}) async-start(), calls=%async_computation.9 | async-start | bytes 4456448 | tf_op jit(solution)/shard_map/all_gather | solution.py:115
  7.9 220.5 %all-gather.5.cloned.1.call-start = ((), (), s32[]{:S(2)}) async-start(), calls=%async_computation.10 | async-start | bytes 4456448 | tf_op jit(solution)/shard_map/all_gather | solution.py:128
  117.1 34.1 %copy-start.1 = (bf16[256,512]{1,0:T(8,128)(2,1)S(1)}, bf16[256,512]{1,0:T(8,128)(2,1)}, u32[]{:S(2)}) copy-start(bf16[256,512]{1,0:T(8,128)(2,1)} %param.13) | copy-start | bytes 786436
  247.5 19.6 %all-to-all-start.7 = ((f32[16,2,512]{2,1,0:T(2,128)}), f32[16,2,512]{2,1,0:T(2,128)S(1)}, u32[]{:S(2)}, u32[]{:S(2)}) async-start(f32[16,2,512]{2,1,0:T(2,128)} %broadcast_in_dim.6), calls=%async_computation.7 | async-start | bytes 131072 | tf_op jit(solution)/shard_map/all_to_all | solution.py:93
  267.1 29.2 %all-to-all-start.3 = ((bf16[2,4,256,512]{3,2,0,1:T(8,128)(2,1)}), bf16[2,4,256,512]{3,2,0,1:T(8,128)(2,1)S(1)}, u32[]{:S(2)}, u32[]{:S(2)}) async-start(bf16[2,4,256,512]{3,2,0,1:T(8,128)(2,1)} %copy.21), calls=%async_computation.3 | async-start | bytes 4194304 | tf_op jit(solution)/shard_map/all_to_all | solution.py:84
  297.4 18.9 %all-to-all-start.8 = ((f32[16,32,512]{2,1,0:T(8,128)}), f32[16,32,512]{2,1,0:T(8,128)}, u32[]{:S(2)}, u32[]{:S(2)}) async-start(f32[16,32,512]{2,1,0:T(8,128)} %broadcast_in_dim.15), calls=%async_computation.8 | async-start | bytes 2097152 | tf_op jit(solution)/shard_map/all_to_all | solution.py:93
  316.3 12.3 %all-to-all-start.4 = ((bf16[2,256,512]{2,1,0:T(8,128)(2,1)}), bf16[2,256,512]{2,1,0:T(8,128)(2,1)S(1)}, u32[]{:S(2)}, u32[]{:S(2)}) async-start(bf16[2,256,512]{2,1,0:T(8,128)(2,1)} %reduce_sum.81), calls=%async_computation.4 | async-start | bytes 1048576 | tf_op jit(solution)/shard_map/all_to_all | solution.py:84
Sparse Core Ops, SparseCore 0:
  9.8 42.3 all-gather.2
  152.6 75.8 all-gather.4

commit v8 on v7

--- a/solution.py
+++ b/solution.py
@@ -126,6 +126,7 @@
     weight_part = exchange_sum(exchange_sum(weight_term, ROW, row_count), COL, col_count)
     grad_weight = exchange_gather(exchange_gather(weight_part, COL, col_count), ROW, row_count)
     upstream = lax.all_gather(own_upstream, COL, axis=0, tiled=True)
+    upstream, grad_weight = lax.optimization_barrier((upstream, grad_weight))
     backward_terms = block_terms(
         values, row_ids, col_ids, live_count, upstream, col_span // block_side, True
     )

time: 342 us -> 322 us (0.942)
  blocking collectives: 135 us -> 210 us
  waiting for transfers between devices: 127 us -> 52.5 us
  starting transfers between devices: 23.7 us -> 3.67 us
  Pallas kernels: 15.1 us -> 18.6 us
    all_to_all x0 -> x2, blocking collectives: none -> 44.4 us  [exchange_gather(): pieces = lax.all_to_all(pieces, axis_name, 0, 0, tiled=False)]
    all_gather x1, waiting for transfers between devices: 33 us -> 0.01 us  [shards(): upstream = lax.all_gather(own_upstream, COL, axis=0, tiled=True)]
    all_to_all x3 -> x4, blocking collectives: 93.7 us -> 125 us  [staged_sum(): lax.all_to_all(pieces, axes[position], position, position, tiled=False)]
    all_to_all x2 -> x1, waiting for transfers between devices: 32.8 us -> 8.17 us  [staged_sum(): lax.all_to_all(pieces, axes[position], position, position, tiled=False)]
    all_to_all x2 -> x0, waiting for transfers between devices: 17.3 us -> none  [exchange_gather(): pieces = lax.all_to_all(pieces, axis_name, 0, 0, tiled=False)]
    all_to_all x2 -> x0, starting transfers between devices: 15 us -> none  [exchange_gather(): pieces = lax.all_to_all(pieces, axis_name, 0, 0, tiled=False)]
    all_to_all x2 -> x1, starting transfers between devices: 8.65 us -> 3.59 us  [staged_sum(): lax.all_to_all(pieces, axes[position], position, position, tiled=False)]
    pallas_call x2, Pallas kernels: 15.1 us -> 18.6 us  [block_terms(): pl.pallas_call(functools.partial(block_kernel, transpose=transpose), grid...]
  transfers between devices with their start and end apart: 6 -> 3, of which waited for: 6 -> 2; matrix products, arithmetic and copies ran while one was open for 2% -> 1% of each run, Pallas kernels for 0% -> 0%
where the time goes in v8:
time: 322 us; the launch traced here: 319 us
  blocking collectives  210 us (65%)
  waiting for transfers between devices  52.5 us (16%)
  Pallas kernels  18.6 us (6%)
  between operations  14.8 us (5%)
  other arithmetic  8.08 us (3%)
  local copies, waits for them, and re-layouts  8.06 us (3%)
  starting transfers between devices  3.67 us (1%)
  matrix products  3.55 us (1%)
    all_to_all x4, blocking collectives, staged_sum(): lax.all_to_all(pieces, axes[position], position, position, tiled=False)  125 us
    all_to_all x2, blocking collectives, exchange_gather(): pieces = lax.all_to_all(pieces, axis_name, 0, 0, tiled=False)  44.4 us
    all_gather x1, waiting for transfers between devices, shards(): panel = lax.all_gather(features, ROW, axis=0, tiled=True)  43.6 us
    all_to_all x2, blocking collectives, exchange_sum(): pieces = lax.all_to_all(pieces, axis_name, 0, 0, tiled=False)  40.4 us
    pallas_call x2, Pallas kernels, block_terms(): pl.pallas_call(functools.partial(block_kernel, transpose=transpose), grid...  18.6 us
    all_to_all x1, waiting for transfers between devices, staged_sum(): lax.all_to_all(pieces, axes[position], position, position, tiled=False)  8.17 us
    reduce_sum x5, other arithmetic, staged_sum(): pieces = pieces.astype(jnp.float32).sum(position)  7.97 us
  transfers between devices with their start and end apart: 3, of which 2 were waited for; matrix products, arithmetic and copies ran while one was open for 1% of the time, Pallas kernels for 0%

profile of v8, /device:TPU:2, one launch (start us, length us, event | category | flops | bytes accessed | tf_op | source)
XLA Modules:
  0.0 319.3 jit_solution(6653856963867280909)
XLA Ops:
  7.2 0.0 copy-start
  7.2 0.0 all-gather.3.cloned.1.call-start
  7.2 0.7 all-gather.3.cloned.1.call-update
  7.9 0.0 all-gather.5.cloned.1.call-start
  8.6 43.6 %all-gather.3.cloned.1.call-done.refs_0_.refs_1_.refs_2_.refs_3_ = bf16[4096,512]{1,0:T(8,128)(2,1)} async-done(((bf16[256,512]{1,0:T(8,128)(2,1)}), bf16[4096,512]{1,0:T(8,128)(2,1)}) %all-gather.3.cloned.1.call-update) | async-done | bytes 4194320 | tf_op jit(solution)/shard_map/all_gather | solution.py:115
  52.2 9.1 %shard_map.94 = bf16[4096,512]{1,0:T(8,128)(2,1)} custom-call(s32[32]{0:T(128)} %bitcast.26, s32[32]{0:T(128)} %bitcast.28, s32[1]{0:T(128)} %bitcast.17.live, bf16[32,128,128]{2,1,0:T(8,128)(2,1)} %bitcast.21, bf16[4096,512]{1,0:T(8,128)(2,1)} %all-gather.3.cloned.1.call-done.refs_0_.refs_1_.refs_2_.refs_3_, ...), custom_call_target="tpu_custom_call" | custom-call | tf_op jit(solution)/shard_map/pallas_call | solution.py:63
  61.3 2.6 copy.19
  63.9 52.2 %all_to_all.45 = bf16[4,4,256,512]{3,2,0,1:T(8,128)(2,1)} all-to-all(bf16[4,4,256,512]{3,2,0,1:T(8,128)(2,1)S(1)} %copy.19), channel_id=1, replica_groups=mesh['zl'=2,'x'=4,'core'=2,'zh'=4,'y'=4] {'y'}, dimensions={1} | all-to-all | bytes 8388608 | tf_op jit(solution)/shard_map/all_to_all | solution.py:84
  116.2 0.0 copy-start.1
  116.2 3.1 reduce_sum.78
  119.3 33.8 %all_to_all.46 = bf16[4,256,512]{2,1,0:T(8,128)(2,1)S(1)} all-to-all(bf16[4,256,512]{2,1,0:T(8,128)(2,1)S(1)} %reduce_sum.78), channel_id=1, replica_groups=mesh['zl'=2,'x'=4,'core'=2,'zh'=4,'y'=4] {'zh'}, dimensions={0} | all-to-all | bytes 2097152 | tf_op jit(solution)/shard_map/all_to_all | solution.py:84
  153.0 0.2 reduce_sum.79
  153.3 0.0 copy-done
  153.3 0.0 copy-done.1
  153.3 1.3 multiply_convert_fusion
  154.6 0.0 all-gather.5.cloned.1.call-update
  154.6 0.1 copy.20
  154.7 1.2 fusion
  156.0 27.4 %all_to_all.47 = f32[16,32,512]{2,1,0:T(8,128)S(1)} all-to-all(f32[16,32,512]{2,1,0:T(8,128)S(1)} %fusion), channel_id=1, replica_groups=mesh['zl'=2,'x'=4,'core'=2,'zh'=4,'y'=4] {'zl','x','core'}, dimensions={0} | all-to-all | bytes 2097152 | tf_op jit(solution)/shard_map/all_to_all | solution.py:77
  183.4 0.1 reduce_sum.80
  183.5 13.0 %all_to_all.48 = f32[16,2,512]{2,1,0:T(2,128)S(1)} all-to-all(f32[16,2,512]{2,1,0:T(2,128)S(1)} %reshape.23), channel_id=1, replica_groups=mesh['zl'=2,'x'=4,'core'=2,'zh'=4,'y'=4] {'zh','y'}, dimensions={0} | all-to-all | bytes 131072 | tf_op jit(solution)/shard_map/all_to_all | solution.py:77
  196.5 15.0 %all_to_all.49 = f32[16,2,512]{2,1,0:T(2,128)S(1)} all-to-all(f32[16,2,512]{2,1,0:T(2,128)S(1)} %broadcast_in_dim.6), channel_id=1, replica_groups=mesh['zl'=2,'x'=4,'core'=2,'zh'=4,'y'=4] {'zh','y'}, dimensions={0} | all-to-all | bytes 131072 | tf_op jit(solution)/shard_map/all_to_all | solution.py:93
  211.6 0.1 broadcast_in_dim.15
  211.7 29.4 %all_to_all.50 = f32[16,32,512]{2,1,0:T(8,128)} all-to-all(f32[16,32,512]{2,1,0:T(8,128)S(1)} %broadcast_in_dim.15), channel_id=1, replica_groups=mesh['zl'=2,'x'=4,'core'=2,'zh'=4,'y'=4] {'zl','x','core'}, dimensions={0} | all-to-all | bytes 2097152 | tf_op jit(solution)/shard_map/all_to_all | solution.py:93
  241.2 0.0 all-gather.5.cloned.1.call-done.refs_0_.refs_1_.refs_2_.refs_3_
  241.2 9.5 %shard_map.95 = bf16[4096,512]{1,0:T(8,128)(2,1)} custom-call(s32[32]{0:T(128)} %bitcast.29, s32[32]{0:T(128)} %bitcast.27, s32[1]{0:T(128)} %bitcast.18.live, bf16[32,128,128]{2,1,0:T(8,128)(2,1)} %bitcast.22, bf16[4096,512]{1,0:T(8,128)(2,1)} %all-gather.5.cloned.1.call-done.refs_0_.refs_1_.refs_2_.refs_3_, ...), custom_call_target="tpu_custom_call" | custom-call | tf_op jit(solution)/shard_map/pallas_call | solution.py:63
  250.6 2.6 copy.22
  253.2 8.2 %all_to_all.51 = bf16[2,4,2,256,512]{4,3,1,0,2:T(8,128)(2,1)} all-to-all(bf16[2,4,2,256,512]{4,3,1,0,2:T(8,128)(2,1)S(1)} %copy.22), channel_id=1, replica_groups=mesh['zl'=2,'x'=4,'core'=2,'zh'=4,'y'=4] {'core'}, dimensions={2} | all-to-all | bytes 8388608 | tf_op jit(solution)/shard_map/all_to_all | solution.py:84
  261.4 3.3 %reduce_sum.82 = bf16[2,4,256,512]{3,2,1,0:T(8,128)(2,1)S(1)} reduce(bf16[2,4,2,256,512]{4,3,1,0,2:T(8,128)(2,1)} %all_to_all.51, bf16[]{:T(256)} %constant.9.clone.1), dimensions={2}, to_apply=%region_4.5 | reduce | flops 1048576 | bytes 6291458 | tf_op jit(solution)/shard_map/reduce_sum | solution.py:85
  264.8 0.2 copy.23
  265.0 31.1 %all_to_all.52 = bf16[2,4,256,512]{3,2,0,1:T(8,128)(2,1)S(1)} all-to-all(bf16[2,4,256,512]{3,2,0,1:T(8,128)(2,1)S(1)} %copy.23), channel_id=1, replica_groups=mesh['zl'=2,'x'=4,'core'=2,'zh'=4,'y'=4] {'x'}, dimensions={1} | all-to-all | bytes 4194304 | tf_op jit(solution)/shard_map/all_to_all | solution.py:84
  296.1 1.3 reduce_sum.83
  297.3 3.6 %all-to-all-start.8 = ((bf16[2,256,512]{2,1,0:T(8,128)(2,1)}), bf16[2,256,512]{2,1,0:T(8,128)(2,1)S(1)}, u32[]{:S(2)}, u32[]{:S(2)}) async-start(bf16[2,256,512]{2,1,0:T(8,128)(2,1)} %reduce_sum.83), calls=%async_computation.8 | async-start | bytes 1048576 | tf_op jit(solution)/shard_map/all_to_all | solution.py:84
  300.9 8.2 %all-to-all-done.8 = bf16[2,256,512]{2,1,0:T(8,128)(2,1)S(1)} async-done(((bf16[2,256,512]{2,1,0:T(8,128)(2,1)}), bf16[2,256,512]{2,1,0:T(8,128)(2,1)S(1)}, u32[]{:S(2)}, u32[]{:S(2)}) %all-to-all-start.8) | async-done | bytes 524320 | tf_op jit(solution)/shard_map/all_to_all | solution.py:84
  309.1 0.1 reduce_sum.84
  309.2 1.0 convolution_convert_fusion
  310.2 2.3 copy.27
  (4 shorter events, 0.1 us)
Async XLA Ops:
  7.2 146.1 %copy-start = (bf16[512,512]{1,0:T(8,128)(2,1)S(1)}, bf16[512,512]{1,0:T(8,128)(2,1)}, u32[]{:S(2)}) copy-start(bf16[512,512]{1,0:T(8,128)(2,1)} %param.8) | copy-start | bytes 1572868
  7.2 45.0 %all-gather.3.cloned.1.call-start = ((), (), s32[]{:S(2)}) async-start(), calls=%async_computation.9 | async-start | bytes 4456448 | tf_op jit(solution)/shard_map/all_gather | solution.py:115
  7.9 233.2 %all-gather.5.cloned.1.call-start = ((), (), s32[]{:S(2)}) async-start(), calls=%async_computation.10 | async-start | bytes 4456448 | tf_op jit(solution)/shard_map/all_gather | solution.py:128
  116.2 37.1 %copy-start.1 = (bf16[256,512]{1,0:T(8,128)(2,1)S(1)}, bf16[256,512]{1,0:T(8,128)(2,1)}, u32[]{:S(2)}) copy-start(bf16[256,512]{1,0:T(8,128)(2,1)} %param.13) | copy-start | bytes 786436
  297.3 11.8 %all-to-all-start.8 = ((bf16[2,256,512]{2,1,0:T(8,128)(2,1)}), bf16[2,256,512]{2,1,0:T(8,128)(2,1)S(1)}, u32[]{:S(2)}, u32[]{:S(2)}) async-start(bf16[2,256,512]{2,1,0:T(8,128)(2,1)} %reduce_sum.83), calls=%async_computation.8 | async-start | bytes 1048576 | tf_op jit(solution)/shard_map/all_to_all | solution.py:84
Sparse Core Ops, SparseCore 0:
  9.8 42.3 all-gather.2
  154.7 80.9 all-gather.4

commit v9 on v8

--- a/solution.py
+++ b/solution.py
@@ -78,12 +78,21 @@
     return pieces.astype(jnp.float32).sum(0)
 
 
+def reversed_blocks(target_ids, sizes, blocks_per_part):
+    part, half = target_ids // blocks_per_part, target_ids % blocks_per_part
+    flipped, stride = 0, 1
+    for size in reversed(sizes):
+        flipped = flipped * size + part % size
+        part = part // size
+    return flipped * blocks_per_part + half
+
+
 def staged_sum(parts, axes, sizes):
-    pieces = parts.reshape(tuple(sizes) + (-1,) + parts.shape[1:])
-    for position in reversed(range(len(axes))):
-        pieces = lax.all_to_all(pieces, axes[position], position, position, tiled=False)
-        pieces = pieces.astype(jnp.float32).sum(position)
-        if position > 0:
+    pieces = parts.reshape(tuple(reversed(sizes)) + (-1,) + parts.shape[1:])
+    for position, name in enumerate(reversed(axes)):
+        pieces = lax.all_to_all(pieces, name, 0, 0, tiled=False)
+        pieces = pieces.astype(jnp.float32).sum(0)
+        if position < len(axes) - 1:
             pieces = pieces.astype(jnp.bfloat16)
     return pieces
 
@@ -113,8 +122,10 @@
     row_span = col_count * local_rows
     col_span = row_count * local_rows
     panel = lax.all_gather(features, ROW, axis=0, tiled=True)
+    parts_per_device = local_rows // block_side
     forward_terms = block_terms(
-        values, col_ids, row_ids, live_count, panel, row_span // block_side, False
+        values, col_ids, reversed_blocks(row_ids, col_sizes, parts_per_device), live_count,
+        panel, row_span // block_side, False
     )
     own_mixed = staged_sum(forward_terms, COL, col_sizes).astype(jnp.bfloat16)
     own_sum = jnp.dot(own_mixed, weight, preferred_element_type=jnp.float32)
@@ -128,7 +139,8 @@
     upstream = lax.all_gather(own_upstream, COL, axis=0, tiled=True)
     upstream, grad_weight = lax.optimization_barrier((upstream, grad_weight))
     backward_terms = block_terms(
-        values, row_ids, col_ids, live_count, upstream, col_span // block_side, True
+        values, row_ids, reversed_blocks(col_ids, row_sizes, parts_per_device), live_count,
+        upstream, col_span // block_side, True
     )
     grad_projected = staged_sum(backward_terms, ROW, row_sizes).astype(jnp.bfloat16)
     grad_features = lax.dot_general(

time: 322 us -> 323 us (level)
  blocking collectives: 210 us -> 192 us
  waiting for transfers between devices: 52.5 us -> 70 us
  starting transfers between devices: 3.67 us -> 11.2 us
  local copies, waits for them, and re-layouts: 8.06 us -> 2.33 us
  other arithmetic: 8.08 us -> 11.5 us
  Pallas kernels: 18.6 us -> 15.3 us
    all_to_all x2 -> x1, blocking collectives: 44.4 us -> 14.8 us  [exchange_gather(): pieces = lax.all_to_all(pieces, axis_name, 0, 0, tiled=False)]
    all_to_all x1 -> x2, waiting for transfers between devices: 8.17 us -> 27 us  [the longest x1 19.3 us: exchange_gather(): pieces = lax.all_to_all(pieces, axis_name, 0, 0, tiled=False)]
    all_to_all x4, blocking collectives: 125 us -> 139 us  [staged_sum(): pieces = lax.all_to_all(pieces, name, 0, 0, tiled=False)]
    all_to_all x1 -> x2, starting transfers between devices: 3.59 us -> 11.1 us  [the longest x1 7.65 us: exchange_gather(): pieces = lax.all_to_all(pieces, axis_name, 0, 0, tiled=False)]
    reshape x2 -> x0, local copies, waits for them, and re-layouts: 5.21 us -> none  [staged_sum(): pieces = parts.reshape(tuple(sizes) + (-1,) + parts.shape[1:])]
    pallas_call x2, Pallas kernels: 18.6 us -> 15.3 us  [block_terms(): pl.pallas_call(functools.partial(block_kernel, transpose=transpose), grid...]
  transfers between devices with their start and end apart: 3 -> 4, of which waited for: 2 -> 3; matrix products, arithmetic and copies ran while one was open for 1% -> 1% of each run, Pallas kernels for 0% -> 0%
where the time goes in v9:
time: 323 us; the launch traced here: 321 us
  blocking collectives  192 us (59%)
  waiting for transfers between devices  70 us (22%)
  Pallas kernels  15.3 us (5%)
  between operations  14.8 us (5%)
  other arithmetic  11.5 us (4%)
  starting transfers between devices  11.2 us (3%)
  matrix products  3.56 us (1%)
    all_to_all x4, blocking collectives, staged_sum(): pieces = lax.all_to_all(pieces, name, 0, 0, tiled=False)  139 us
    all_gather x1, waiting for transfers between devices, shards(): panel = lax.all_gather(features, ROW, axis=0, tiled=True)  42.4 us
    all_to_all x2, blocking collectives, exchange_sum(): pieces = lax.all_to_all(pieces, axis_name, 0, 0, tiled=False)  38.4 us
    all_to_all x1, waiting for transfers between devices, exchange_gather(): pieces = lax.all_to_all(pieces, axis_name, 0, 0, tiled=False)  19.3 us
    pallas_call x2, Pallas kernels, block_terms(): pl.pallas_call(functools.partial(block_kernel, transpose=transpose), grid...  15.3 us
    all_to_all x1, blocking collectives, exchange_gather(): pieces = lax.all_to_all(pieces, axis_name, 0, 0, tiled=False)  14.8 us
    reduce_sum x5, other arithmetic, staged_sum(): pieces = pieces.astype(jnp.float32).sum(0)  9.65 us
    all_to_all x1, waiting for transfers between devices, staged_sum(): pieces = lax.all_to_all(pieces, name, 0, 0, tiled=False)  7.68 us
  transfers between devices with their start and end apart: 4, of which 3 were waited for; matrix products, arithmetic and copies ran while one was open for 1% of the time, Pallas kernels for 0%

profile of v9, /device:TPU:2, one launch (start us, length us, event | category | flops | bytes accessed | tf_op | source)
XLA Modules:
  0.0 320.7 jit_solution(10308453858659043973)
XLA Ops:
  7.2 0.0 copy-start
  7.2 0.0 all-gather.3.cloned.1.call-start
  7.2 0.7 all-gather.3.cloned.1.call-update
  7.9 0.0 all-gather.5.cloned.1.call-start
  8.6 1.2 fusion.3.target_ids
  9.8 42.4 %all-gather.3.cloned.1.call-done.refs_0_.refs_1_.refs_2_.refs_3_ = bf16[4096,512]{1,0:T(8,128)(2,1)} async-done(((bf16[256,512]{1,0:T(8,128)(2,1)}), bf16[4096,512]{1,0:T(8,128)(2,1)}) %all-gather.3.cloned.1.call-update) | async-done | bytes 4194320 | tf_op jit(solution)/shard_map/all_gather | solution.py:124
  52.2 7.6 %shard_map.94 = bf16[4096,512]{1,0:T(8,128)(2,1)} custom-call(s32[32]{0:T(128)} %bitcast.28, s32[32]{0:T(128)} %fusion.3.target_ids, s32[1]{0:T(128)} %bitcast.19.live, bf16[32,128,128]{2,1,0:T(8,128)(2,1)} %bitcast.23, bf16[4096,512]{1,0:T(8,128)(2,1)} %all-gather.3.cloned.1.call-done.refs_0_.refs_1_.refs_2_.refs_3_, ...), custom_call_target="tpu_custom_call" | custom-call | tf_op jit(solution)/shard_map/pallas_call | solution.py:63
  59.8 55.4 %all_to_all.45 = bf16[4,4,256,512]{3,2,1,0:T(8,128)(2,1)} all-to-all(bf16[4,4,256,512]{3,2,1,0:T(8,128)(2,1)} %bitcast.22), channel_id=1, replica_groups=mesh['zl'=2,'x'=4,'core'=2,'zh'=4,'y'=4] {'y'}, dimensions={0} | all-to-all | bytes 8388608 | tf_op jit(solution)/shard_map/all_to_all | solution.py:93
  115.2 0.0 copy-start.4
  115.2 3.1 reduce_sum.78
  118.3 36.1 %all_to_all.46 = bf16[4,256,512]{2,1,0:T(8,128)(2,1)S(1)} all-to-all(bf16[4,256,512]{2,1,0:T(8,128)(2,1)S(1)} %reduce_sum.78), channel_id=1, replica_groups=mesh['zl'=2,'x'=4,'core'=2,'zh'=4,'y'=4] {'zh'}, dimensions={0} | all-to-all | bytes 2097152 | tf_op jit(solution)/shard_map/all_to_all | solution.py:93
  154.3 0.2 reduce_sum.79
  154.6 0.0 copy-done
  154.6 0.0 copy-done.4
  154.6 1.3 multiply_convert_fusion
  155.9 0.0 all-gather.5.cloned.1.call-update
  155.9 0.1 copy.11
  156.0 0.0 copy-start.3
  156.0 1.2 fusion
  157.3 25.6 %all_to_all.47 = f32[16,32,512]{2,1,0:T(8,128)S(1)} all-to-all(f32[16,32,512]{2,1,0:T(8,128)S(1)} %fusion), channel_id=1, replica_groups=mesh['zl'=2,'x'=4,'core'=2,'zh'=4,'y'=4] {'zl','x','core'}, dimensions={0} | all-to-all | bytes 2097152 | tf_op jit(solution)/shard_map/all_to_all | solution.py:77
  182.8 0.1 reduce_sum.80
  183.0 12.8 %all_to_all.48 = f32[16,2,512]{2,1,0:T(2,128)S(1)} all-to-all(f32[16,2,512]{2,1,0:T(2,128)S(1)} %reshape.23), channel_id=1, replica_groups=mesh['zl'=2,'x'=4,'core'=2,'zh'=4,'y'=4] {'zh','y'}, dimensions={0} | all-to-all | bytes 131072 | tf_op jit(solution)/shard_map/all_to_all | solution.py:77
  195.8 14.8 %all_to_all.49 = f32[16,2,512]{2,1,0:T(2,128)S(1)} all-to-all(f32[16,2,512]{2,1,0:T(2,128)S(1)} %broadcast_in_dim.6), channel_id=1, replica_groups=mesh['zl'=2,'x'=4,'core'=2,'zh'=4,'y'=4] {'zh','y'}, dimensions={0} | all-to-all | bytes 131072 | tf_op jit(solution)/shard_map/all_to_all | solution.py:102
  210.7 1.1 broadcast_in_dim.15
  211.8 7.7 %all-to-all-start.5 = ((f32[16,32,512]{2,1,0:T(8,128)}), f32[16,32,512]{2,1,0:T(8,128)S(1)}, u32[]{:S(2)}, u32[]{:S(2)}) async-start(f32[16,32,512]{2,1,0:T(8,128)} %broadcast_in_dim.15), calls=%async_computation.5 | async-start | bytes 2097152 | tf_op jit(solution)/shard_map/all_to_all | solution.py:102
  219.4 0.0 copy-done.3
  219.4 0.6 fusion.6.target_ids
  220.0 19.3 %all-to-all-done.5 = f32[16,32,512]{2,1,0:T(8,128)S(1)} async-done(((f32[16,32,512]{2,1,0:T(8,128)}), f32[16,32,512]{2,1,0:T(8,128)S(1)}, u32[]{:S(2)}, u32[]{:S(2)}) %all-to-all-start.5) | async-done | bytes 1048608 | tf_op jit(solution)/shard_map/all_to_all | solution.py:102
  239.3 0.0 copy-start.1
  239.3 0.0 all-gather.5.cloned.1.call-done.refs_0_.refs_1_.refs_2_.refs_3_
  239.3 7.7 %shard_map.95 = bf16[4096,512]{1,0:T(8,128)(2,1)} custom-call(s32[32]{0:T(128)} %bitcast.29, s32[32]{0:T(128)} %fusion.6.target_ids, s32[1]{0:T(128)} %bitcast.20.live, bf16[32,128,128]{2,1,0:T(8,128)(2,1)} %bitcast.24, bf16[4096,512]{1,0:T(8,128)(2,1)} %all-gather.5.cloned.1.call-done.refs_0_.refs_1_.refs_2_.refs_3_, ...), custom_call_target="tpu_custom_call" | custom-call | tf_op jit(solution)/shard_map/pallas_call | solution.py:63
  247.0 0.0 copy-done.1
  247.0 11.9 %all_to_all.50 = bf16[2,4,2,256,512]{4,3,2,1,0:T(8,128)(2,1)} all-to-all(bf16[2,4,2,256,512]{4,3,2,1,0:T(8,128)(2,1)} %bitcast.21), channel_id=1, replica_groups=mesh['zl'=2,'x'=4,'core'=2,'zh'=4,'y'=4] {'core'}, dimensions={0} | all-to-all | bytes 8388608 | tf_op jit(solution)/shard_map/all_to_all | solution.py:93
  258.8 3.3 %reduce_sum.82 = bf16[4,2,256,512]{3,2,1,0:T(8,128)(2,1)S(1)} reduce(bf16[2,4,2,256,512]{4,3,2,1,0:T(8,128)(2,1)} %all_to_all.50, bf16[]{:T(256)} %constant.102.clone.1), dimensions={0}, to_apply=%region_4.5 | reduce | flops 1048576 | bytes 6291458 | tf_op jit(solution)/shard_map/reduce_sum | solution.py:94
  262.2 35.4 %all_to_all.51 = bf16[4,2,256,512]{3,2,1,0:T(8,128)(2,1)} all-to-all(bf16[4,2,256,512]{3,2,1,0:T(8,128)(2,1)S(1)} %reduce_sum.82), channel_id=1, replica_groups=mesh['zl'=2,'x'=4,'core'=2,'zh'=4,'y'=4] {'x'}, dimensions={0} | all-to-all | bytes 4194304 | tf_op jit(solution)/shard_map/all_to_all | solution.py:93
  297.6 0.0 copy-start.2
  297.6 2.9 reduce_sum.83
  300.5 3.5 %all-to-all-start.8 = ((bf16[2,256,512]{2,1,0:T(8,128)(2,1)}), bf16[2,256,512]{2,1,0:T(8,128)(2,1)S(1)}, u32[]{:S(2)}, u32[]{:S(2)}) async-start(bf16[2,256,512]{2,1,0:T(8,128)(2,1)} %reduce_sum.83), calls=%async_computation.8 | async-start | bytes 1048576 | tf_op jit(solution)/shard_map/all_to_all | solution.py:93
  304.0 7.7 %all-to-all-done.8 = bf16[2,256,512]{2,1,0:T(8,128)(2,1)S(1)} async-done(((bf16[2,256,512]{2,1,0:T(8,128)(2,1)}), bf16[2,256,512]{2,1,0:T(8,128)(2,1)S(1)}, u32[]{:S(2)}, u32[]{:S(2)}) %all-to-all-start.8) | async-done | bytes 524320 | tf_op jit(solution)/shard_map/all_to_all | solution.py:93
  311.7 0.1 reduce_sum.84
  311.8 1.0 convolution_convert_fusion
  312.9 0.0 copy-done.2
  312.9 1.0 copy.16
  (4 shorter events, 0.1 us)
Async XLA Ops:
  7.2 147.4 %copy-start = (bf16[512,512]{1,0:T(8,128)(2,1)S(1)}, bf16[512,512]{1,0:T(8,128)(2,1)}, u32[]{:S(2)}) copy-start(bf16[512,512]{1,0:T(8,128)(2,1)} %param.8) | copy-start | bytes 1572868
  7.2 45.0 %all-gather.3.cloned.1.call-start = ((), (), s32[]{:S(2)}) async-start(), calls=%async_computation.9 | async-start | bytes 4456448 | tf_op jit(solution)/shard_map/all_gather | solution.py:124
  7.9 231.3 %all-gather.5.cloned.1.call-start = ((), (), s32[]{:S(2)}) async-start(), calls=%async_computation.10 | async-start | bytes 4456448 | tf_op jit(solution)/shard_map/all_gather | solution.py:139
  115.2 39.4 %copy-start.4 = (bf16[256,512]{1,0:T(8,128)(2,1)S(1)}, bf16[256,512]{1,0:T(8,128)(2,1)}, u32[]{:S(2)}) copy-start(bf16[256,512]{1,0:T(8,128)(2,1)} %param.13) | copy-start | bytes 786436
  156.0 63.4 %copy-start.3 = (s32[1,1,32]{2,1,0:T(1,128)S(1)}, s32[1,1,32]{2,1,0:T(1,128)}, u32[]{:S(2)}) copy-start(s32[1,1,32]{2,1,0:T(1,128)} %param.11) | copy-start | bytes 388
  211.8 27.5 %all-to-all-start.5 = ((f32[16,32,512]{2,1,0:T(8,128)}), f32[16,32,512]{2,1,0:T(8,128)S(1)}, u32[]{:S(2)}, u32[]{:S(2)}) async-start(f32[16,32,512]{2,1,0:T(8,128)} %broadcast_in_dim.15), calls=%async_computation.5 | async-start | bytes 2097152 | tf_op jit(solution)/shard_map/all_to_all | solution.py:102
  239.3 7.7 %copy-start.1 = (f32[16,32,512]{2,1,0:T(8,128)}, f32[16,32,512]{2,1,0:T(8,128)S(1)}, u32[]{:S(2)}) copy-start(f32[16,32,512]{2,1,0:T(8,128)S(1)} %all-to-all-done.5) | copy-start | bytes 3145732
  297.6 15.3 %copy-start.2 = (f32[16,32,512]{2,1,0:T(8,128)S(1)}, f32[16,32,512]{2,1,0:T(8,128)}, u32[]{:S(2)}) copy-start(f32[16,32,512]{2,1,0:T(8,128)} %copy-done.1) | copy-start | bytes 3145732
  300.5 11.2 %all-to-all-start.8 = ((bf16[2,256,512]{2,1,0:T(8,128)(2,1)}), bf16[2,256,512]{2,1,0:T(8,128)(2,1)S(1)}, u32[]{:S(2)}, u32[]{:S(2)}) async-start(bf16[2,256,512]{2,1,0:T(8,128)(2,1)} %reduce_sum.83), calls=%async_computation.8 | async-start | bytes 1048576 | tf_op jit(solution)/shard_map/all_to_all | solution.py:93
Sparse Core Ops, SparseCore 0:
  9.8 42.3 all-gather.2
  156.0 79.3 all-gather.4

commit v10 on v9

--- a/solution.py
+++ b/solution.py
@@ -121,7 +121,7 @@
     col_count = col_sizes[0] * col_sizes[1]
     row_span = col_count * local_rows
     col_span = row_count * local_rows
-    panel = lax.all_gather(features, ROW, axis=0, tiled=True)
+    panel = exchange_gather(features, ROW, row_count)
     parts_per_device = local_rows // block_side
     forward_terms = block_terms(
         values, col_ids, reversed_blocks(row_ids, col_sizes, parts_per_device), live_count,
@@ -134,8 +134,9 @@
     weight_term = lax.dot_general(
         own_mixed, own_upstream, (((0,), (0,)), ((), ())), preferred_element_type=jnp.float32
     )
-    weight_part = exchange_sum(exchange_sum(weight_term, ROW, row_count), COL, col_count)
-    grad_weight = exchange_gather(exchange_gather(weight_part, COL, col_count), ROW, row_count)
+    weight_part = exchange_sum(weight_term, ROW, row_count)
+    weight_part = exchange_gather(weight_part[None], COL, col_count).sum(0)
+    grad_weight = exchange_gather(weight_part, ROW, row_count)
     upstream = lax.all_gather(own_upstream, COL, axis=0, tiled=True)
     upstream, grad_weight = lax.optimization_barrier((upstream, grad_weight))
     backward_terms = block_terms(

time: 323 us -> 371 us (1.15)
  blocking collectives: 192 us -> 221 us
  waiting for transfers between devices: 70 us -> 79.1 us
  starting transfers between devices: 11.2 us -> 16.7 us
    all_to_all x1 -> x2, waiting for transfers between devices: 19.3 us -> 71.4 us  [exchange_gather(): pieces = lax.all_to_all(pieces, axis_name, 0, 0, tiled=False)]
    all_gather x1 -> x0, waiting for transfers between devices: 42.4 us -> none  [shards(): panel = lax.all_gather(features, ROW, axis=0, tiled=True)]
    all_to_all x1, blocking collectives: 14.8 us -> 55 us  [exchange_gather(): pieces = lax.all_to_all(pieces, axis_name, 0, 0, tiled=False)]
    all_to_all x2 -> x1, blocking collectives: 38.4 us -> 31.4 us  [exchange_sum(): pieces = lax.all_to_all(pieces, axis_name, 0, 0, tiled=False)]
    all_to_all x1 -> x2, starting transfers between devices: 7.65 us -> 13.1 us  [exchange_gather(): pieces = lax.all_to_all(pieces, axis_name, 0, 0, tiled=False)]
    all_to_all x4, blocking collectives: 139 us -> 134 us  [staged_sum(): pieces = lax.all_to_all(pieces, name, 0, 0, tiled=False)]
where the time goes in v10:
time: 371 us; the launch traced here: 368 us
  blocking collectives  221 us (60%)
  waiting for transfers between devices  79.1 us (21%)
  starting transfers between devices  16.7 us (5%)
  Pallas kernels  16.3 us (4%)
  between operations  14.8 us (4%)
  other arithmetic  10.9 us (3%)
  local copies, waits for them, and re-layouts  5.73 us (2%)
    all_to_all x4, blocking collectives, staged_sum(): pieces = lax.all_to_all(pieces, name, 0, 0, tiled=False)  134 us
    all_to_all x2, waiting for transfers between devices, exchange_gather(): pieces = lax.all_to_all(pieces, axis_name, 0, 0, tiled=False)  71.4 us
    all_to_all x1, blocking collectives, exchange_gather(): pieces = lax.all_to_all(pieces, axis_name, 0, 0, tiled=False)  55 us
    all_to_all x1, blocking collectives, exchange_sum(): pieces = lax.all_to_all(pieces, axis_name, 0, 0, tiled=False)  31.4 us
    pallas_call x2, Pallas kernels, block_terms(): pl.pallas_call(functools.partial(block_kernel, transpose=transpose), grid...  16.3 us
    all_to_all x2, starting transfers between devices, exchange_gather(): pieces = lax.all_to_all(pieces, axis_name, 0, 0, tiled=False)  13.1 us
    reduce_sum x5, other arithmetic, staged_sum(): pieces = pieces.astype(jnp.float32).sum(0)  9.65 us
    all_to_all x1, waiting for transfers between devices, staged_sum(): pieces = lax.all_to_all(pieces, name, 0, 0, tiled=False)  7.68 us
  transfers between devices with their start and end apart: 4, of which 3 were waited for; matrix products, arithmetic and copies ran while one was open for 1% of the time, Pallas kernels for 0%

profile of v10, /device:TPU:2, one launch (start us, length us, event | category | flops | bytes accessed | tf_op | source)
XLA Modules:
  0.0 367.8 jit_solution(13238073922069412067)
XLA Ops:
  7.2 0.0 copy-start
  7.2 3.4 broadcast_in_dim.6
  10.6 0.0 copy-start.4
  10.6 6.6 %all-to-all-start = ((bf16[16,256,512]{2,1,0:T(8,128)(2,1)}), bf16[16,256,512]{2,1,0:T(8,128)(2,1)}, u32[]{:S(2)}, u32[]{:S(2)}) async-start(bf16[16,256,512]{2,1,0:T(8,128)(2,1)} %broadcast_in_dim.6), calls=%async_computation | async-start | bytes 8388608 | tf_op jit(solution)/shard_map/all_to_all | solution.py:102
  17.2 0.0 all-gather.2.cloned.1.call-start
  17.9 0.0 copy-done.4
  17.9 0.5 fusion.3.target_ids
  18.4 58.5 %all-to-all-done = bf16[16,256,512]{2,1,0:T(8,128)(2,1)} async-done(((bf16[16,256,512]{2,1,0:T(8,128)(2,1)}), bf16[16,256,512]{2,1,0:T(8,128)(2,1)}, u32[]{:S(2)}, u32[]{:S(2)}) %all-to-all-start) | async-done | bytes 4194336 | tf_op jit(solution)/shard_map/all_to_all | solution.py:102
  77.0 8.0 %shard_map.94 = bf16[4096,512]{1,0:T(8,128)(2,1)} custom-call(s32[32]{0:T(128)} %bitcast.29, s32[32]{0:T(128)} %fusion.3.target_ids, s32[1]{0:T(128)} %bitcast.20.live, bf16[32,128,128]{2,1,0:T(8,128)(2,1)} %bitcast.24, bf16[4096,512]{1,0:T(8,128)(2,1)} %bitcast.4.refs_0_.refs_1_.refs_2_.refs_3_, bf16[4096,512]{1,0:T(8,128)(2,1)} %bitcast.4.refs_0_.refs_1_.refs_2_.refs_3_, ...), custom_call_target="tpu_custom_call" | custom-call | tf_op jit(solution)/shard_map/pallas_call | solution.py:63
  85.0 55.2 %all_to_all.45 = bf16[4,4,256,512]{3,2,1,0:T(8,128)(2,1)} all-to-all(bf16[4,4,256,512]{3,2,1,0:T(8,128)(2,1)} %bitcast.23), channel_id=1, replica_groups=mesh['zl'=2,'x'=4,'core'=2,'zh'=4,'y'=4] {'y'}, dimensions={0} | all-to-all | bytes 8388608 | tf_op jit(solution)/shard_map/all_to_all | solution.py:93
  140.2 0.0 copy-start.5
  140.2 3.1 reduce_sum.78
  143.3 33.7 %all_to_all.46 = bf16[4,256,512]{2,1,0:T(8,128)(2,1)S(1)} all-to-all(bf16[4,256,512]{2,1,0:T(8,128)(2,1)S(1)} %reduce_sum.78), channel_id=1, replica_groups=mesh['zl'=2,'x'=4,'core'=2,'zh'=4,'y'=4] {'zh'}, dimensions={0} | all-to-all | bytes 2097152 | tf_op jit(solution)/shard_map/all_to_all | solution.py:93
  176.9 0.2 reduce_sum.79
  177.2 0.0 copy-done
  177.2 0.0 copy-done.5
  177.2 1.3 multiply_convert_fusion
  178.5 0.0 all-gather.2.cloned.1.call-update
  178.5 0.1 copy.11
  178.6 1.2 fusion
  179.9 31.4 %all_to_all.47 = f32[16,32,512]{2,1,0:T(8,128)S(1)} all-to-all(f32[16,32,512]{2,1,0:T(8,128)S(1)} %fusion), channel_id=1, replica_groups=mesh['zl'=2,'x'=4,'core'=2,'zh'=4,'y'=4] {'zl','x','core'}, dimensions={0} | all-to-all | bytes 2097152 | tf_op jit(solution)/shard_map/all_to_all | solution.py:77
  211.3 0.0 copy-start.3
  211.3 0.1 reduce_sum.80
  211.4 0.1 broadcast_in_dim.7
  211.5 55.0 %all_to_all.48 = f32[16,1,32,512]{3,2,1,0:T(8,128)S(1)} all-to-all(f32[16,1,32,512]{3,2,1,0:T(8,128)S(1)} %broadcast_in_dim.7), channel_id=1, replica_groups=mesh['zl'=2,'x'=4,'core'=2,'zh'=4,'y'=4] {'zh','y'}, dimensions={0} | all-to-all | bytes 2097152 | tf_op jit(solution)/shard_map/all_to_all | solution.py:102
  266.5 0.1 reduce_sum.81
  266.6 1.1 broadcast_in_dim.8
  267.7 6.5 %all-to-all-start.5 = ((f32[16,32,512]{2,1,0:T(8,128)}), f32[16,32,512]{2,1,0:T(8,128)S(1)}, u32[]{:S(2)}, u32[]{:S(2)}) async-start(f32[16,32,512]{2,1,0:T(8,128)} %broadcast_in_dim.8), calls=%async_computation.5 | async-start | bytes 2097152 | tf_op jit(solution)/shard_map/all_to_all | solution.py:102
  274.2 0.0 copy-done.3
  274.2 0.6 fusion.6.target_ids
  274.7 12.8 %all-to-all-done.5 = f32[16,32,512]{2,1,0:T(8,128)S(1)} async-done(((f32[16,32,512]{2,1,0:T(8,128)}), f32[16,32,512]{2,1,0:T(8,128)S(1)}, u32[]{:S(2)}, u32[]{:S(2)}) %all-to-all-start.5) | async-done | bytes 1048608 | tf_op jit(solution)/shard_map/all_to_all | solution.py:102
  287.6 0.0 copy-start.1
  287.6 0.0 all-gather.2.cloned.1.call-done.refs_0_.refs_1_.refs_2_.refs_3_
  287.6 8.3 %shard_map.95 = bf16[4096,512]{1,0:T(8,128)(2,1)} custom-call(s32[32]{0:T(128)} %bitcast.30, s32[32]{0:T(128)} %fusion.6.target_ids, s32[1]{0:T(128)} %bitcast.21.live, bf16[32,128,128]{2,1,0:T(8,128)(2,1)} %bitcast.25, bf16[4096,512]{1,0:T(8,128)(2,1)} %all-gather.2.cloned.1.call-done.refs_0_.refs_1_.refs_2_.refs_3_, ...), custom_call_target="tpu_custom_call" | custom-call | tf_op jit(solution)/shard_map/pallas_call | solution.py:63
  295.8 0.0 copy-done.1
  295.8 11.9 %all_to_all.49 = bf16[2,4,2,256,512]{4,3,2,1,0:T(8,128)(2,1)} all-to-all(bf16[2,4,2,256,512]{4,3,2,1,0:T(8,128)(2,1)} %bitcast.22), channel_id=1, replica_groups=mesh['zl'=2,'x'=4,'core'=2,'zh'=4,'y'=4] {'core'}, dimensions={0} | all-to-all | bytes 8388608 | tf_op jit(solution)/shard_map/all_to_all | solution.py:93
  307.7 3.3 reduce_sum.82
  311.0 33.7 %all_to_all.50 = bf16[4,2,256,512]{3,2,1,0:T(8,128)(2,1)} all-to-all(bf16[4,2,256,512]{3,2,1,0:T(8,128)(2,1)S(1)} %reduce_sum.82), channel_id=1, replica_groups=mesh['zl'=2,'x'=4,'core'=2,'zh'=4,'y'=4] {'x'}, dimensions={0} | all-to-all | bytes 4194304 | tf_op jit(solution)/shard_map/all_to_all | solution.py:93
  344.7 0.0 copy-start.2
  344.7 2.9 reduce_sum.83
  347.7 3.5 all-to-all-start.8
  351.2 7.7 %all-to-all-done.8 = bf16[2,256,512]{2,1,0:T(8,128)(2,1)S(1)} async-done(((bf16[2,256,512]{2,1,0:T(8,128)(2,1)}), bf16[2,256,512]{2,1,0:T(8,128)(2,1)S(1)}, u32[]{:S(2)}, u32[]{:S(2)}) %all-to-all-start.8) | async-done | bytes 524320 | tf_op jit(solution)/shard_map/all_to_all | solution.py:93
  358.9 0.1 reduce_sum.84
  359.0 1.0 convolution_convert_fusion
  360.0 0.0 copy-done.2
  360.0 1.0 copy.14
Async XLA Ops:
  7.2 170.0 %copy-start = (bf16[512,512]{1,0:T(8,128)(2,1)S(1)}, bf16[512,512]{1,0:T(8,128)(2,1)}, u32[]{:S(2)}) copy-start(bf16[512,512]{1,0:T(8,128)(2,1)} %param.8) | copy-start | bytes 1572868
  10.6 7.3 %copy-start.4 = (s32[1,1,32]{2,1,0:T(1,128)S(1)}, s32[1,1,32]{2,1,0:T(1,128)}, u32[]{:S(2)}) copy-start(s32[1,1,32]{2,1,0:T(1,128)} %param.10) | copy-start | bytes 388
  10.6 66.4 %all-to-all-start = ((bf16[16,256,512]{2,1,0:T(8,128)(2,1)}), bf16[16,256,512]{2,1,0:T(8,128)(2,1)}, u32[]{:S(2)}, u32[]{:S(2)}) async-start(bf16[16,256,512]{2,1,0:T(8,128)(2,1)} %broadcast_in_dim.6), calls=%async_computation | async-start | bytes 8388608 | tf_op jit(solution)/shard_map/all_to_all | solution.py:102
  17.2 270.4 %all-gather.2.cloned.1.call-start = ((), (), s32[]{:S(2)}) async-start(), calls=%async_computation.9 | async-start | bytes 4456448 | tf_op jit(solution)/shard_map/all_gather | solution.py:140
  140.2 37.0 %copy-start.5 = (bf16[256,512]{1,0:T(8,128)(2,1)S(1)}, bf16[256,512]{1,0:T(8,128)(2,1)}, u32[]{:S(2)}) copy-start(bf16[256,512]{1,0:T(8,128)(2,1)} %param.13) | copy-start | bytes 786436
  211.3 62.9 %copy-start.3 = (s32[1,1,32]{2,1,0:T(1,128)S(1)}, s32[1,1,32]{2,1,0:T(1,128)}, u32[]{:S(2)}) copy-start(s32[1,1,32]{2,1,0:T(1,128)} %param.11) | copy-start | bytes 388
  267.7 19.9 %all-to-all-start.5 = ((f32[16,32,512]{2,1,0:T(8,128)}), f32[16,32,512]{2,1,0:T(8,128)S(1)}, u32[]{:S(2)}, u32[]{:S(2)}) async-start(f32[16,32,512]{2,1,0:T(8,128)} %broadcast_in_dim.8), calls=%async_computation.5 | async-start | bytes 2097152 | tf_op jit(solution)/shard_map/all_to_all | solution.py:102
  287.6 8.3 %copy-start.1 = (f32[16,32,512]{2,1,0:T(8,128)}, f32[16,32,512]{2,1,0:T(8,128)S(1)}, u32[]{:S(2)}) copy-start(f32[16,32,512]{2,1,0:T(8,128)S(1)} %all-to-all-done.5) | copy-start | bytes 3145732
  344.7 15.3 %copy-start.2 = (f32[16,32,512]{2,1,0:T(8,128)S(1)}, f32[16,32,512]{2,1,0:T(8,128)}, u32[]{:S(2)}) copy-start(f32[16,32,512]{2,1,0:T(8,128)} %copy-done.1) | copy-start | bytes 3145732
  347.7 11.2 %all-to-all-start.8 = ((bf16[2,256,512]{2,1,0:T(8,128)(2,1)}), bf16[2,256,512]{2,1,0:T(8,128)(2,1)S(1)}, u32[]{:S(2)}, u32[]{:S(2)}) async-start(bf16[2,256,512]{2,1,0:T(8,128)(2,1)} %reduce_sum.83), calls=%async_computation.8 | async-start | bytes 1048576 | tf_op jit(solution)/shard_map/all_to_all | solution.py:93
Sparse Core Ops, SparseCore 0:
  178.6 97.5 all-gather.1

commit v11 on v9

--- a/solution.py
+++ b/solution.py
@@ -6,7 +6,7 @@
 from jax.experimental.pallas import tpu as pltpu
 from jax.sharding import Mesh, PartitionSpec as P
 
-GROUP = 4
+GROUP = 8
 
 
 def block_kernel(source_ids, target_ids, live, values_ref, *refs, transpose):

time: 323 us -> 322 us (level)
  blocking collectives: 192 us -> 186 us
  Pallas kernels: 15.3 us -> 18.8 us
    all_to_all x4, blocking collectives: 139 us -> 133 us  [staged_sum(): pieces = lax.all_to_all(pieces, name, 0, 0, tiled=False)]
    pallas_call x2, Pallas kernels: 15.3 us -> 18.8 us  [block_terms(): pl.pallas_call(functools.partial(block_kernel, transpose=transpose), grid...]
where the time goes in v11:
time: 322 us; the launch traced here: 319 us
  blocking collectives  186 us (58%)
  waiting for transfers between devices  70.4 us (22%)
  Pallas kernels  18.8 us (6%)
  between operations  14.8 us (5%)
  other arithmetic  11.5 us (4%)
  starting transfers between devices  10.6 us (3%)
  matrix products  3.55 us (1%)
    all_to_all x4, blocking collectives, staged_sum(): pieces = lax.all_to_all(pieces, name, 0, 0, tiled=False)  133 us
    all_gather x1, waiting for transfers between devices, shards(): panel = lax.all_gather(features, ROW, axis=0, tiled=True)  42.4 us
    all_to_all x2, blocking collectives, exchange_sum(): pieces = lax.all_to_all(pieces, axis_name, 0, 0, tiled=False)  38.8 us
    all_to_all x1, waiting for transfers between devices, exchange_gather(): pieces = lax.all_to_all(pieces, axis_name, 0, 0, tiled=False)  19.7 us
    pallas_call x2, Pallas kernels, block_terms(): pl.pallas_call(functools.partial(block_kernel, transpose=transpose), grid...  18.8 us
    all_to_all x1, blocking collectives, exchange_gather(): pieces = lax.all_to_all(pieces, axis_name, 0, 0, tiled=False)  14.6 us
    reduce_sum x5, other arithmetic, staged_sum(): pieces = pieces.astype(jnp.float32).sum(0)  9.65 us
    all_to_all x1, waiting for transfers between devices, staged_sum(): pieces = lax.all_to_all(pieces, name, 0, 0, tiled=False)  7.65 us
  transfers between devices with their start and end apart: 4, of which 3 were waited for; matrix products, arithmetic and copies ran while one was open for 1% of the time, Pallas kernels for 0%

profile of v11, /device:TPU:2, one launch (start us, length us, event | category | flops | bytes accessed | tf_op | source)
XLA Modules:
  0.0 318.5 jit_solution(14290961339202663472)
XLA Ops:
  7.2 0.0 copy-start
  7.2 0.0 all-gather.3.cloned.1.call-start
  7.2 0.7 all-gather.3.cloned.1.call-update
  7.9 0.0 all-gather.5.cloned.1.call-start
  8.6 1.2 fusion.3.target_ids
  9.8 42.4 %all-gather.3.cloned.1.call-done.refs_0_.refs_1_.refs_2_.refs_3_.refs_4_.refs_5_.refs_6_.refs_7_ = bf16[4096,512]{1,0:T(8,128)(2,1)} async-done(((bf16[256,512]{1,0:T(8,128)(2,1)}), bf16[4096,512]{1,0:T(8,128)(2,1)}) %all-gather.3.cloned.1.call-update) | async-done | bytes 4194320 | tf_op jit(solution)/shard_map/all_gather | solution.py:124
  52.2 9.0 %shard_map.94 = bf16[4096,512]{1,0:T(8,128)(2,1)} custom-call(s32[32]{0:T(128)} %bitcast.28, s32[32]{0:T(128)} %fusion.3.target_ids, s32[1]{0:T(128)} %bitcast.19.live, bf16[32,128,128]{2,1,0:T(8,128)(2,1)} %bitcast.23, bf16[4096,512]{1,0:T(8,128)(2,1)} %all-gather.3.cloned.1.call-done.refs_0_.refs_1_.refs_2_.refs_3_.refs_4_.refs_5_.refs_6_.refs_7_, ...), custom_call_target="tpu_custom_call" | custom-call | tf_op jit(solution)/shard_map/pallas_call | solution.py:63
  61.2 54.1 %all_to_all.45 = bf16[4,4,256,512]{3,2,1,0:T(8,128)(2,1)} all-to-all(bf16[4,4,256,512]{3,2,1,0:T(8,128)(2,1)} %bitcast.22), channel_id=1, replica_groups=mesh['zl'=2,'x'=4,'core'=2,'zh'=4,'y'=4] {'y'}, dimensions={0} | all-to-all | bytes 8388608 | tf_op jit(solution)/shard_map/all_to_all | solution.py:93
  115.4 0.0 copy-start.4
  115.4 3.1 reduce_sum.78
  118.4 34.9 %all_to_all.46 = bf16[4,256,512]{2,1,0:T(8,128)(2,1)S(1)} all-to-all(bf16[4,256,512]{2,1,0:T(8,128)(2,1)S(1)} %reduce_sum.78), channel_id=1, replica_groups=mesh['zl'=2,'x'=4,'core'=2,'zh'=4,'y'=4] {'zh'}, dimensions={0} | all-to-all | bytes 2097152 | tf_op jit(solution)/shard_map/all_to_all | solution.py:93
  153.3 0.2 reduce_sum.79
  153.6 0.0 copy-done
  153.6 0.0 copy-done.4
  153.6 1.3 multiply_convert_fusion
  154.9 0.0 all-gather.5.cloned.1.call-update
  154.9 0.1 copy.11
  155.0 0.0 copy-start.3
  155.0 1.2 fusion
  156.3 25.0 %all_to_all.47 = f32[16,32,512]{2,1,0:T(8,128)S(1)} all-to-all(f32[16,32,512]{2,1,0:T(8,128)S(1)} %fusion), channel_id=1, replica_groups=mesh['zl'=2,'x'=4,'core'=2,'zh'=4,'y'=4] {'zl','x','core'}, dimensions={0} | all-to-all | bytes 2097152 | tf_op jit(solution)/shard_map/all_to_all | solution.py:77
  181.3 0.1 reduce_sum.80
  181.4 13.8 %all_to_all.48 = f32[16,2,512]{2,1,0:T(2,128)S(1)} all-to-all(f32[16,2,512]{2,1,0:T(2,128)S(1)} %reshape.23), channel_id=1, replica_groups=mesh['zl'=2,'x'=4,'core'=2,'zh'=4,'y'=4] {'zh','y'}, dimensions={0} | all-to-all | bytes 131072 | tf_op jit(solution)/shard_map/all_to_all | solution.py:77
  195.3 14.6 %all_to_all.49 = f32[16,2,512]{2,1,0:T(2,128)S(1)} all-to-all(f32[16,2,512]{2,1,0:T(2,128)S(1)} %broadcast_in_dim.6), channel_id=1, replica_groups=mesh['zl'=2,'x'=4,'core'=2,'zh'=4,'y'=4] {'zh','y'}, dimensions={0} | all-to-all | bytes 131072 | tf_op jit(solution)/shard_map/all_to_all | solution.py:102
  209.9 1.1 broadcast_in_dim.15
  211.0 7.1 %all-to-all-start.5 = ((f32[16,32,512]{2,1,0:T(8,128)}), f32[16,32,512]{2,1,0:T(8,128)S(1)}, u32[]{:S(2)}, u32[]{:S(2)}) async-start(f32[16,32,512]{2,1,0:T(8,128)} %broadcast_in_dim.15), calls=%async_computation.5 | async-start | bytes 2097152 | tf_op jit(solution)/shard_map/all_to_all | solution.py:102
  218.1 0.0 copy-done.3
  218.1 0.6 fusion.6.target_ids
  218.6 19.7 %all-to-all-done.5 = f32[16,32,512]{2,1,0:T(8,128)S(1)} async-done(((f32[16,32,512]{2,1,0:T(8,128)}), f32[16,32,512]{2,1,0:T(8,128)S(1)}, u32[]{:S(2)}, u32[]{:S(2)}) %all-to-all-start.5) | async-done | bytes 1048608 | tf_op jit(solution)/shard_map/all_to_all | solution.py:102
  238.3 0.0 copy-start.1
  238.3 0.0 all-gather.5.cloned.1.call-done.refs_0_.refs_1_.refs_2_.refs_3_.refs_4_.refs_5_.refs_6_.refs_7_
  238.3 9.8 %shard_map.95 = bf16[4096,512]{1,0:T(8,128)(2,1)} custom-call(s32[32]{0:T(128)} %bitcast.29, s32[32]{0:T(128)} %fusion.6.target_ids, s32[1]{0:T(128)} %bitcast.20.live, bf16[32,128,128]{2,1,0:T(8,128)(2,1)} %bitcast.24, bf16[4096,512]{1,0:T(8,128)(2,1)} %all-gather.5.cloned.1.call-done.refs_0_.refs_1_.refs_2_.refs_3_.refs_4_.refs_5_.refs_6_.refs_7_, ...), custom_call_target="tpu_custom_call" | custom-call | tf_op jit(solution)/shard_map/pallas_call | solution.py:63
  248.1 0.0 copy-done.1
  248.1 11.9 %all_to_all.50 = bf16[2,4,2,256,512]{4,3,2,1,0:T(8,128)(2,1)} all-to-all(bf16[2,4,2,256,512]{4,3,2,1,0:T(8,128)(2,1)} %bitcast.21), channel_id=1, replica_groups=mesh['zl'=2,'x'=4,'core'=2,'zh'=4,'y'=4] {'core'}, dimensions={0} | all-to-all | bytes 8388608 | tf_op jit(solution)/shard_map/all_to_all | solution.py:93
  260.0 3.3 %reduce_sum.82 = bf16[4,2,256,512]{3,2,1,0:T(8,128)(2,1)S(1)} reduce(bf16[2,4,2,256,512]{4,3,2,1,0:T(8,128)(2,1)} %all_to_all.50, bf16[]{:T(256)} %constant.102.clone.1), dimensions={0}, to_apply=%region_4.5 | reduce | flops 1048576 | bytes 6291458 | tf_op jit(solution)/shard_map/reduce_sum | solution.py:94
  263.3 32.2 %all_to_all.51 = bf16[4,2,256,512]{3,2,1,0:T(8,128)(2,1)} all-to-all(bf16[4,2,256,512]{3,2,1,0:T(8,128)(2,1)S(1)} %reduce_sum.82), channel_id=1, replica_groups=mesh['zl'=2,'x'=4,'core'=2,'zh'=4,'y'=4] {'x'}, dimensions={0} | all-to-all | bytes 4194304 | tf_op jit(solution)/shard_map/all_to_all | solution.py:93
  295.5 0.0 copy-start.2
  295.5 2.9 reduce_sum.83
  298.4 3.5 %all-to-all-start.8 = ((bf16[2,256,512]{2,1,0:T(8,128)(2,1)}), bf16[2,256,512]{2,1,0:T(8,128)(2,1)S(1)}, u32[]{:S(2)}, u32[]{:S(2)}) async-start(bf16[2,256,512]{2,1,0:T(8,128)(2,1)} %reduce_sum.83), calls=%async_computation.8 | async-start | bytes 1048576 | tf_op jit(solution)/shard_map/all_to_all | solution.py:93
  301.9 7.6 %all-to-all-done.8 = bf16[2,256,512]{2,1,0:T(8,128)(2,1)S(1)} async-done(((bf16[2,256,512]{2,1,0:T(8,128)(2,1)}), bf16[2,256,512]{2,1,0:T(8,128)(2,1)S(1)}, u32[]{:S(2)}, u32[]{:S(2)}) %all-to-all-start.8) | async-done | bytes 524320 | tf_op jit(solution)/shard_map/all_to_all | solution.py:93
  309.6 0.1 reduce_sum.84
  309.7 1.0 convolution_convert_fusion
  310.7 0.0 copy-done.2
  310.7 1.0 copy.16
  (4 shorter events, 0.1 us)
Async XLA Ops:
  7.2 146.4 %copy-start = (bf16[512,512]{1,0:T(8,128)(2,1)S(1)}, bf16[512,512]{1,0:T(8,128)(2,1)}, u32[]{:S(2)}) copy-start(bf16[512,512]{1,0:T(8,128)(2,1)} %param.8) | copy-start | bytes 1572868
  7.2 45.0 %all-gather.3.cloned.1.call-start = ((), (), s32[]{:S(2)}) async-start(), calls=%async_computation.9 | async-start | bytes 4456448 | tf_op jit(solution)/shard_map/all_gather | solution.py:124
  7.9 230.4 %all-gather.5.cloned.1.call-start = ((), (), s32[]{:S(2)}) async-start(), calls=%async_computation.10 | async-start | bytes 4456448 | tf_op jit(solution)/shard_map/all_gather | solution.py:139
  115.4 38.2 %copy-start.4 = (bf16[256,512]{1,0:T(8,128)(2,1)S(1)}, bf16[256,512]{1,0:T(8,128)(2,1)}, u32[]{:S(2)}) copy-start(bf16[256,512]{1,0:T(8,128)(2,1)} %param.13) | copy-start | bytes 786436
  155.0 63.0 %copy-start.3 = (s32[1,1,32]{2,1,0:T(1,128)S(1)}, s32[1,1,32]{2,1,0:T(1,128)}, u32[]{:S(2)}) copy-start(s32[1,1,32]{2,1,0:T(1,128)} %param.11) | copy-start | bytes 388
  211.0 27.3 %all-to-all-start.5 = ((f32[16,32,512]{2,1,0:T(8,128)}), f32[16,32,512]{2,1,0:T(8,128)S(1)}, u32[]{:S(2)}, u32[]{:S(2)}) async-start(f32[16,32,512]{2,1,0:T(8,128)} %broadcast_in_dim.15), calls=%async_computation.5 | async-start | bytes 2097152 | tf_op jit(solution)/shard_map/all_to_all | solution.py:102
  238.3 9.8 %copy-start.1 = (f32[16,32,512]{2,1,0:T(8,128)}, f32[16,32,512]{2,1,0:T(8,128)S(1)}, u32[]{:S(2)}) copy-start(f32[16,32,512]{2,1,0:T(8,128)S(1)} %all-to-all-done.5) | copy-start | bytes 3145732
  295.5 15.2 %copy-start.2 = (f32[16,32,512]{2,1,0:T(8,128)S(1)}, f32[16,32,512]{2,1,0:T(8,128)}, u32[]{:S(2)}) copy-start(f32[16,32,512]{2,1,0:T(8,128)} %copy-done.1) | copy-start | bytes 3145732
  298.4 11.1 %all-to-all-start.8 = ((bf16[2,256,512]{2,1,0:T(8,128)(2,1)}), bf16[2,256,512]{2,1,0:T(8,128)(2,1)S(1)}, u32[]{:S(2)}, u32[]{:S(2)}) async-start(bf16[2,256,512]{2,1,0:T(8,128)(2,1)} %reduce_sum.83), calls=%async_computation.8 | async-start | bytes 1048576 | tf_op jit(solution)/shard_map/all_to_all | solution.py:93
Sparse Core Ops, SparseCore 0:
  9.8 42.3 all-gather.2
  155.0 79.3 all-gather.4

commit v12 on v11

--- a/solution.py
+++ b/solution.py
@@ -10,13 +10,15 @@
 
 
 def block_kernel(source_ids, target_ids, live, values_ref, *refs, transpose):
-    tile_refs, out_ref, acc_ref = refs[:-2], refs[-2], refs[-1]
+    tile_refs, out_ref, acc_ref, seen_ref = refs[:-3], refs[-3], refs[-2], refs[-1]
     step = pl.program_id(0)
     group = len(tile_refs)
+    block_count, block_side, _ = acc_ref.shape
 
     @pl.when(step == 0)
     def _():
-        acc_ref[...] = jnp.zeros_like(acc_ref)
+        for block in range(block_count):
+            seen_ref[block] = 0
 
     for slot, tile_ref in enumerate(tile_refs):
         entry = step * group + slot
@@ -28,11 +30,32 @@
                 term = lax.dot_general(block, tile_ref[...], (((0,), (0,)), ((), ())), preferred_element_type=jnp.float32)
             else:
                 term = jnp.dot(block, tile_ref[...], preferred_element_type=jnp.float32)
-            acc_ref[target_ids[entry]] += term
+            target = target_ids[entry]
+            fresh = seen_ref[target] == 0
+
+            @pl.when(fresh)
+            def _():
+                acc_ref[target] = term
+
+            @pl.when(jnp.logical_not(fresh))
+            def _():
+                acc_ref[target] += term
+
+            seen_ref[target] = 1
 
     @pl.when(step == pl.num_programs(0) - 1)
     def _():
-        out_ref[...] = acc_ref[...].reshape(out_ref.shape).astype(out_ref.dtype)
+        for block in range(block_count):
+            rows = pl.ds(block * block_side, block_side)
+            touched = seen_ref[block] != 0
+
+            @pl.when(touched)
+            def _():
+                out_ref[rows, :] = acc_ref[block].astype(out_ref.dtype)
+
+            @pl.when(jnp.logical_not(touched))
+            def _():
+                out_ref[rows, :] = jnp.zeros((block_side, out_ref.shape[1]), out_ref.dtype)
 
 
 def block_terms(values, source_ids, target_ids, live_count, source, target_blocks, transpose):
@@ -58,7 +81,10 @@
         in_specs=[pl.BlockSpec((group, block_side, block_side), values_map)]
         + [pl.BlockSpec((block_side, feature_count), tile_map_of(slot)) for slot in range(group)],
         out_specs=pl.BlockSpec((target_blocks * block_side, feature_count), out_map),
-        scratch_shapes=[pltpu.VMEM((target_blocks, block_side, feature_count), jnp.float32)],
+        scratch_shapes=[
+            pltpu.VMEM((target_blocks, block_side, feature_count), jnp.float32),
+            pltpu.SMEM((target_blocks,), jnp.int32),
+        ],
     )
     return pl.pallas_call(
         functools.partial(block_kernel, transpose=transpose),

time: 322 us -> 323 us (level)
  blocking collectives: 186 us -> 192 us
  Pallas kernels: 18.8 us -> 15 us
    all_to_all x4, blocking collectives: 133 us -> 138 us  [staged_sum(): pieces = lax.all_to_all(pieces, name, 0, 0, tiled=False)]
    pallas_call x2, Pallas kernels: 18.8 us -> 15 us  [block_terms(): pl.pallas_call(functools.partial(block_kernel, transpose=transpose), grid...]
where the time goes in v12:
time: 323 us; the launch traced here: 319 us
  blocking collectives  192 us (59%)
  waiting for transfers between devices  69.6 us (22%)
  Pallas kernels  15 us (5%)
  between operations  14.8 us (5%)
  other arithmetic  11.5 us (4%)
  starting transfers between devices  10.7 us (3%)
  matrix products  3.55 us (1%)
    all_to_all x4, blocking collectives, staged_sum(): pieces = lax.all_to_all(pieces, name, 0, 0, tiled=False)  138 us
    all_gather x1, waiting for transfers between devices, shards(): panel = lax.all_gather(features, ROW, axis=0, tiled=True)  42.4 us
    all_to_all x2, blocking collectives, exchange_sum(): pieces = lax.all_to_all(pieces, axis_name, 0, 0, tiled=False)  38.3 us
    all_to_all x1, waiting for transfers between devices, exchange_gather(): pieces = lax.all_to_all(pieces, axis_name, 0, 0, tiled=False)  19.4 us
    all_to_all x1, blocking collectives, exchange_gather(): pieces = lax.all_to_all(pieces, axis_name, 0, 0, tiled=False)  15.4 us
    pallas_call x2, Pallas kernels, block_terms(): pl.pallas_call(functools.partial(block_kernel, transpose=transpose), grid...  15 us
    reduce_sum x5, other arithmetic, staged_sum(): pieces = pieces.astype(jnp.float32).sum(0)  9.65 us
    all_to_all x1, waiting for transfers between devices, staged_sum(): pieces = lax.all_to_all(pieces, name, 0, 0, tiled=False)  7.1 us
  transfers between devices with their start and end apart: 4, of which 3 were waited for; matrix products, arithmetic and copies ran while one was open for 1% of the time, Pallas kernels for 0%

profile of v12, /device:TPU:2, one launch (start us, length us, event | category | flops | bytes accessed | tf_op | source)
XLA Modules:
  0.0 319.5 jit_solution(12999491703717035920)
XLA Ops:
  7.2 0.0 copy-start
  7.2 0.0 all-gather.3.cloned.1.call-start
  7.2 0.7 all-gather.3.cloned.1.call-update
  7.9 0.0 all-gather.5.cloned.1.call-start
  8.6 1.2 fusion.3.target_ids
  9.8 42.4 %all-gather.3.cloned.1.call-done.refs_0_.refs_1_.refs_2_.refs_3_.refs_4_.refs_5_.refs_6_.refs_7_ = bf16[4096,512]{1,0:T(8,128)(2,1)} async-done(((bf16[256,512]{1,0:T(8,128)(2,1)}), bf16[4096,512]{1,0:T(8,128)(2,1)}) %all-gather.3.cloned.1.call-update) | async-done | bytes 4194320 | tf_op jit(solution)/shard_map/all_gather | solution.py:150
  52.2 7.3 %shard_map.94 = bf16[4096,512]{1,0:T(8,128)(2,1)} custom-call(s32[32]{0:T(128)} %bitcast.28, s32[32]{0:T(128)} %fusion.3.target_ids, s32[1]{0:T(128)} %bitcast.19.live, bf16[32,128,128]{2,1,0:T(8,128)(2,1)} %bitcast.23, bf16[4096,512]{1,0:T(8,128)(2,1)} %all-gather.3.cloned.1.call-done.refs_0_.refs_1_.refs_2_.refs_3_.refs_4_.refs_5_.refs_6_.refs_7_, ...), custom_call_target="tpu_custom_call" | custom-call | tf_op jit(solution)/shard_map/pallas_call | solution.py:89
  59.5 55.5 %all_to_all.45 = bf16[4,4,256,512]{3,2,1,0:T(8,128)(2,1)} all-to-all(bf16[4,4,256,512]{3,2,1,0:T(8,128)(2,1)} %bitcast.22), channel_id=1, replica_groups=mesh['zl'=2,'x'=4,'core'=2,'zh'=4,'y'=4] {'y'}, dimensions={0} | all-to-all | bytes 8388608 | tf_op jit(solution)/shard_map/all_to_all | solution.py:119
  115.0 0.0 copy-start.4
  115.0 3.1 reduce_sum.78
  118.1 34.5 %all_to_all.46 = bf16[4,256,512]{2,1,0:T(8,128)(2,1)S(1)} all-to-all(bf16[4,256,512]{2,1,0:T(8,128)(2,1)S(1)} %reduce_sum.78), channel_id=1, replica_groups=mesh['zl'=2,'x'=4,'core'=2,'zh'=4,'y'=4] {'zh'}, dimensions={0} | all-to-all | bytes 2097152 | tf_op jit(solution)/shard_map/all_to_all | solution.py:119
  152.6 0.2 reduce_sum.79
  152.8 0.0 copy-done
  152.8 0.0 copy-done.4
  152.8 1.3 multiply_convert_fusion
  154.1 0.0 all-gather.5.cloned.1.call-update
  154.1 0.1 copy.11
  154.3 0.0 copy-start.3
  154.3 1.2 fusion
  155.5 24.5 %all_to_all.47 = f32[16,32,512]{2,1,0:T(8,128)S(1)} all-to-all(f32[16,32,512]{2,1,0:T(8,128)S(1)} %fusion), channel_id=1, replica_groups=mesh['zl'=2,'x'=4,'core'=2,'zh'=4,'y'=4] {'zl','x','core'}, dimensions={0} | all-to-all | bytes 2097152 | tf_op jit(solution)/shard_map/all_to_all | solution.py:103
  180.0 0.1 reduce_sum.80
  180.1 13.8 %all_to_all.48 = f32[16,2,512]{2,1,0:T(2,128)S(1)} all-to-all(f32[16,2,512]{2,1,0:T(2,128)S(1)} %reshape.23), channel_id=1, replica_groups=mesh['zl'=2,'x'=4,'core'=2,'zh'=4,'y'=4] {'zh','y'}, dimensions={0} | all-to-all | bytes 131072 | tf_op jit(solution)/shard_map/all_to_all | solution.py:103
  194.0 15.4 %all_to_all.49 = f32[16,2,512]{2,1,0:T(2,128)S(1)} all-to-all(f32[16,2,512]{2,1,0:T(2,128)S(1)} %broadcast_in_dim.6), channel_id=1, replica_groups=mesh['zl'=2,'x'=4,'core'=2,'zh'=4,'y'=4] {'zh','y'}, dimensions={0} | all-to-all | bytes 131072 | tf_op jit(solution)/shard_map/all_to_all | solution.py:128
  209.4 1.1 broadcast_in_dim.15
  210.5 7.1 %all-to-all-start.5 = ((f32[16,32,512]{2,1,0:T(8,128)}), f32[16,32,512]{2,1,0:T(8,128)S(1)}, u32[]{:S(2)}, u32[]{:S(2)}) async-start(f32[16,32,512]{2,1,0:T(8,128)} %broadcast_in_dim.15), calls=%async_computation.5 | async-start | bytes 2097152 | tf_op jit(solution)/shard_map/all_to_all | solution.py:128
  217.6 0.0 copy-done.3
  217.6 0.6 fusion.6.target_ids
  218.2 19.4 %all-to-all-done.5 = f32[16,32,512]{2,1,0:T(8,128)S(1)} async-done(((f32[16,32,512]{2,1,0:T(8,128)}), f32[16,32,512]{2,1,0:T(8,128)S(1)}, u32[]{:S(2)}, u32[]{:S(2)}) %all-to-all-start.5) | async-done | bytes 1048608 | tf_op jit(solution)/shard_map/all_to_all | solution.py:128
  237.6 0.0 copy-start.1
  237.6 0.0 all-gather.5.cloned.1.call-done.refs_0_.refs_1_.refs_2_.refs_3_.refs_4_.refs_5_.refs_6_.refs_7_
  237.6 7.6 %shard_map.95 = bf16[4096,512]{1,0:T(8,128)(2,1)} custom-call(s32[32]{0:T(128)} %bitcast.29, s32[32]{0:T(128)} %fusion.6.target_ids, s32[1]{0:T(128)} %bitcast.20.live, bf16[32,128,128]{2,1,0:T(8,128)(2,1)} %bitcast.24, bf16[4096,512]{1,0:T(8,128)(2,1)} %all-gather.5.cloned.1.call-done.refs_0_.refs_1_.refs_2_.refs_3_.refs_4_.refs_5_.refs_6_.refs_7_, ...), custom_call_target="tpu_custom_call" | custom-call | tf_op jit(solution)/shard_map/pallas_call | solution.py:89
  245.2 0.0 copy-done.1
  245.2 13.2 %all_to_all.50 = bf16[2,4,2,256,512]{4,3,2,1,0:T(8,128)(2,1)} all-to-all(bf16[2,4,2,256,512]{4,3,2,1,0:T(8,128)(2,1)} %bitcast.21), channel_id=1, replica_groups=mesh['zl'=2,'x'=4,'core'=2,'zh'=4,'y'=4] {'core'}, dimensions={0} | all-to-all | bytes 8388608 | tf_op jit(solution)/shard_map/all_to_all | solution.py:119
  258.5 3.3 %reduce_sum.82 = bf16[4,2,256,512]{3,2,1,0:T(8,128)(2,1)S(1)} reduce(bf16[2,4,2,256,512]{4,3,2,1,0:T(8,128)(2,1)} %all_to_all.50, bf16[]{:T(256)} %constant.102.clone.1), dimensions={0}, to_apply=%region_4.5 | reduce | flops 1048576 | bytes 6291458 | tf_op jit(solution)/shard_map/reduce_sum | solution.py:120
  261.8 35.2 %all_to_all.51 = bf16[4,2,256,512]{3,2,1,0:T(8,128)(2,1)} all-to-all(bf16[4,2,256,512]{3,2,1,0:T(8,128)(2,1)S(1)} %reduce_sum.82), channel_id=1, replica_groups=mesh['zl'=2,'x'=4,'core'=2,'zh'=4,'y'=4] {'x'}, dimensions={0} | all-to-all | bytes 4194304 | tf_op jit(solution)/shard_map/all_to_all | solution.py:119
  297.0 0.0 copy-start.2
  297.0 2.9 reduce_sum.83
  299.9 3.5 %all-to-all-start.8 = ((bf16[2,256,512]{2,1,0:T(8,128)(2,1)}), bf16[2,256,512]{2,1,0:T(8,128)(2,1)S(1)}, u32[]{:S(2)}, u32[]{:S(2)}) async-start(bf16[2,256,512]{2,1,0:T(8,128)(2,1)} %reduce_sum.83), calls=%async_computation.8 | async-start | bytes 1048576 | tf_op jit(solution)/shard_map/all_to_all | solution.py:119
  303.4 7.1 %all-to-all-done.8 = bf16[2,256,512]{2,1,0:T(8,128)(2,1)S(1)} async-done(((bf16[2,256,512]{2,1,0:T(8,128)(2,1)}), bf16[2,256,512]{2,1,0:T(8,128)(2,1)S(1)}, u32[]{:S(2)}, u32[]{:S(2)}) %all-to-all-start.8) | async-done | bytes 524320 | tf_op jit(solution)/shard_map/all_to_all | solution.py:119
  310.5 0.1 reduce_sum.84
  310.6 1.0 convolution_convert_fusion
  311.7 0.0 copy-done.2
  311.7 1.0 copy.16
  (4 shorter events, 0.1 us)
Async XLA Ops:
  7.2 145.6 %copy-start = (bf16[512,512]{1,0:T(8,128)(2,1)S(1)}, bf16[512,512]{1,0:T(8,128)(2,1)}, u32[]{:S(2)}) copy-start(bf16[512,512]{1,0:T(8,128)(2,1)} %param.8) | copy-start | bytes 1572868
  7.2 45.0 %all-gather.3.cloned.1.call-start = ((), (), s32[]{:S(2)}) async-start(), calls=%async_computation.9 | async-start | bytes 4456448 | tf_op jit(solution)/shard_map/all_gather | solution.py:150
  7.9 229.7 %all-gather.5.cloned.1.call-start = ((), (), s32[]{:S(2)}) async-start(), calls=%async_computation.10 | async-start | bytes 4456448 | tf_op jit(solution)/shard_map/all_gather | solution.py:165
  115.0 37.8 %copy-start.4 = (bf16[256,512]{1,0:T(8,128)(2,1)S(1)}, bf16[256,512]{1,0:T(8,128)(2,1)}, u32[]{:S(2)}) copy-start(bf16[256,512]{1,0:T(8,128)(2,1)} %param.13) | copy-start | bytes 786436
  154.3 63.4 %copy-start.3 = (s32[1,1,32]{2,1,0:T(1,128)S(1)}, s32[1,1,32]{2,1,0:T(1,128)}, u32[]{:S(2)}) copy-start(s32[1,1,32]{2,1,0:T(1,128)} %param.11) | copy-start | bytes 388
  210.5 27.1 %all-to-all-start.5 = ((f32[16,32,512]{2,1,0:T(8,128)}), f32[16,32,512]{2,1,0:T(8,128)S(1)}, u32[]{:S(2)}, u32[]{:S(2)}) async-start(f32[16,32,512]{2,1,0:T(8,128)} %broadcast_in_dim.15), calls=%async_computation.5 | async-start | bytes 2097152 | tf_op jit(solution)/shard_map/all_to_all | solution.py:128
  237.6 7.6 %copy-start.1 = (f32[16,32,512]{2,1,0:T(8,128)}, f32[16,32,512]{2,1,0:T(8,128)S(1)}, u32[]{:S(2)}) copy-start(f32[16,32,512]{2,1,0:T(8,128)S(1)} %all-to-all-done.5) | copy-start | bytes 3145732
  297.0 14.7 %copy-start.2 = (f32[16,32,512]{2,1,0:T(8,128)S(1)}, f32[16,32,512]{2,1,0:T(8,128)}, u32[]{:S(2)}) copy-start(f32[16,32,512]{2,1,0:T(8,128)} %copy-done.1) | copy-start | bytes 3145732
  299.9 10.6 %all-to-all-start.8 = ((bf16[2,256,512]{2,1,0:T(8,128)(2,1)}), bf16[2,256,512]{2,1,0:T(8,128)(2,1)S(1)}, u32[]{:S(2)}, u32[]{:S(2)}) async-start(bf16[2,256,512]{2,1,0:T(8,128)(2,1)} %reduce_sum.83), calls=%async_computation.8 | async-start | bytes 1048576 | tf_op jit(solution)/shard_map/all_to_all | solution.py:119
Sparse Core Ops, SparseCore 0:
  9.8 42.3 all-gather.2
  154.2 79.6 all-gather.4

commit v13 on v12

--- a/solution.py
+++ b/solution.py
@@ -160,7 +160,11 @@
     weight_term = lax.dot_general(
         own_mixed, own_upstream, (((0,), (0,)), ((), ())), preferred_element_type=jnp.float32
     )
-    weight_part = exchange_sum(exchange_sum(weight_term, ROW, row_count), COL, col_count)
+    on_chip = weight_term.reshape(tuple(row_sizes) + (-1, weight_term.shape[1]))
+    on_chip = jnp.moveaxis(on_chip, 2, 0)
+    on_chip = lax.all_to_all(on_chip, ROW[2], 0, 0, tiled=False).sum(0)
+    weight_part = exchange_sum(on_chip.reshape((-1, weight_term.shape[1])), ROW[:2], row_count // row_sizes[2])
+    weight_part = exchange_sum(weight_part, COL, col_count)
     grad_weight = exchange_gather(exchange_gather(weight_part, COL, col_count), ROW, row_count)
     upstream = lax.all_gather(own_upstream, COL, axis=0, tiled=True)
     upstream, grad_weight = lax.optimization_barrier((upstream, grad_weight))

time: 323 us -> 322 us (level)
  blocking collectives: 192 us -> 186 us
  Pallas kernels: 15 us -> 20.9 us
    all_to_all x4, blocking collectives: 138 us -> 130 us  [staged_sum(): pieces = lax.all_to_all(pieces, name, 0, 0, tiled=False)]
    pallas_call x2, Pallas kernels: 15 us -> 20.9 us  [block_terms(): pl.pallas_call(functools.partial(block_kernel, transpose=transpose), grid...]
    all_to_all x0 -> x1, blocking collectives: none -> 4.58 us  [shards(): on_chip = lax.all_to_all(on_chip, ROW[2], 0, 0, tiled=False).sum(0)]
where the time goes in v13:
time: 322 us; the launch traced here: 320 us
  blocking collectives  186 us (58%)
  waiting for transfers between devices  72.1 us (22%)
  Pallas kernels  20.9 us (6%)
  between operations  14.8 us (5%)
  other arithmetic  11.6 us (4%)
  starting transfers between devices  8.89 us (3%)
  matrix products  3.56 us (1%)
    all_to_all x4, blocking collectives, staged_sum(): pieces = lax.all_to_all(pieces, name, 0, 0, tiled=False)  130 us
    all_gather x1, waiting for transfers between devices, shards(): panel = lax.all_gather(features, ROW, axis=0, tiled=True)  42.4 us
    all_to_all x2, blocking collectives, exchange_sum(): pieces = lax.all_to_all(pieces, axis_name, 0, 0, tiled=False)  36.5 us
    all_to_all x1, waiting for transfers between devices, exchange_gather(): pieces = lax.all_to_all(pieces, axis_name, 0, 0, tiled=False)  21.9 us
    pallas_call x2, Pallas kernels, block_terms(): pl.pallas_call(functools.partial(block_kernel, transpose=transpose), grid...  20.9 us
    all_to_all x1, blocking collectives, exchange_gather(): pieces = lax.all_to_all(pieces, axis_name, 0, 0, tiled=False)  14.3 us
    reduce_sum x5, other arithmetic, staged_sum(): pieces = pieces.astype(jnp.float32).sum(0)  9.65 us
    all_to_all x1, waiting for transfers between devices, staged_sum(): pieces = lax.all_to_all(pieces, name, 0, 0, tiled=False)  7.1 us
  transfers between devices with their start and end apart: 4, of which 3 were waited for; matrix products, arithmetic and copies ran while one was open for 1% of the time, Pallas kernels for 0%

profile of v13, /device:TPU:2, one launch (start us, length us, event | category | flops | bytes accessed | tf_op | source)
XLA Modules:
  0.0 320.1 jit_solution(18122460603888512549)
XLA Ops:
  7.2 0.0 copy-start
  7.2 0.0 all-gather.3.cloned.1.call-start
  7.2 0.7 all-gather.3.cloned.1.call-update
  7.9 0.0 all-gather.5.cloned.1.call-start
  8.6 1.2 fusion.2.target_ids
  9.8 42.4 %all-gather.3.cloned.1.call-done.refs_0_.refs_1_.refs_2_.refs_3_.refs_4_.refs_5_.refs_6_.refs_7_ = bf16[4096,512]{1,0:T(8,128)(2,1)} async-done(((bf16[256,512]{1,0:T(8,128)(2,1)}), bf16[4096,512]{1,0:T(8,128)(2,1)}) %all-gather.3.cloned.1.call-update) | async-done | bytes 4194320 | tf_op jit(solution)/shard_map/all_gather | solution.py:150
  52.2 10.0 %shard_map.94 = bf16[4096,512]{1,0:T(8,128)(2,1)} custom-call(s32[32]{0:T(128)} %bitcast.34, s32[32]{0:T(128)} %fusion.2.target_ids, s32[1]{0:T(128)} %bitcast.24.live, bf16[32,128,128]{2,1,0:T(8,128)(2,1)} %bitcast.28, bf16[4096,512]{1,0:T(8,128)(2,1)} %all-gather.3.cloned.1.call-done.refs_0_.refs_1_.refs_2_.refs_3_.refs_4_.refs_5_.refs_6_.refs_7_, ...), custom_call_target="tpu_custom_call" | custom-call | tf_op jit(solution)/shard_map/pallas_call | solution.py:89
  62.2 55.6 %all_to_all.50 = bf16[4,4,256,512]{3,2,1,0:T(8,128)(2,1)} all-to-all(bf16[4,4,256,512]{3,2,1,0:T(8,128)(2,1)} %bitcast.27), channel_id=1, replica_groups=mesh['zl'=2,'x'=4,'core'=2,'zh'=4,'y'=4] {'y'}, dimensions={0} | all-to-all | bytes 8388608 | tf_op jit(solution)/shard_map/all_to_all | solution.py:119
  117.8 0.0 copy-start.4
  117.8 3.1 reduce_sum.87
  120.9 29.7 %all_to_all.51 = bf16[4,256,512]{2,1,0:T(8,128)(2,1)S(1)} all-to-all(bf16[4,256,512]{2,1,0:T(8,128)(2,1)S(1)} %reduce_sum.87), channel_id=1, replica_groups=mesh['zl'=2,'x'=4,'core'=2,'zh'=4,'y'=4] {'zh'}, dimensions={0} | all-to-all | bytes 2097152 | tf_op jit(solution)/shard_map/all_to_all | solution.py:119
  150.6 0.2 reduce_sum.88
  150.9 0.0 copy-done
  150.9 0.0 copy-done.4
  150.9 1.3 multiply_convert_fusion
  152.1 0.0 all-gather.5.cloned.1.call-update
  152.2 0.1 copy.17
  152.3 1.2 convolution_bitcast_fusion
  153.6 0.1 copy.18
  153.7 0.0 copy-start.3
  153.7 4.6 %all_to_all.52 = f32[2,2,4,32,512]{4,3,2,1,0:T(8,128)S(1)} all-to-all(f32[2,2,4,32,512]{4,3,2,1,0:T(8,128)S(1)} %copy.18), channel_id=1, replica_groups=mesh['zl'=2,'x'=4,'core'=2,'zh'=4,'y'=4] {'core'}, dimensions={0} | all-to-all | bytes 2097152 | tf_op jit(solution)/shard_map/all_to_all | solution.py:165
  158.2 0.1 reduce_sum.89
  158.4 19.8 %all_to_all.53 = f32[8,32,512]{2,1,0:T(8,128)S(1)} all-to-all(f32[8,32,512]{2,1,0:T(8,128)S(1)} %bitcast.31), channel_id=1, replica_groups=mesh['zl'=2,'x'=4,'core'=2,'zh'=4,'y'=4] {'zl','x'}, dimensions={0} | all-to-all | bytes 1048576 | tf_op jit(solution)/shard_map/all_to_all | solution.py:103
  178.2 16.8 %all_to_all.54 = f32[16,2,512]{2,1,0:T(2,128)S(1)} all-to-all(f32[16,2,512]{2,1,0:T(2,128)S(1)} %reshape.23), channel_id=1, replica_groups=mesh['zl'=2,'x'=4,'core'=2,'zh'=4,'y'=4] {'zh','y'}, dimensions={0} | all-to-all | bytes 131072 | tf_op jit(solution)/shard_map/all_to_all | solution.py:103
  195.1 14.3 %all_to_all.55 = f32[16,2,512]{2,1,0:T(2,128)S(1)} all-to-all(f32[16,2,512]{2,1,0:T(2,128)S(1)} %broadcast_in_dim.6), channel_id=1, replica_groups=mesh['zl'=2,'x'=4,'core'=2,'zh'=4,'y'=4] {'zh','y'}, dimensions={0} | all-to-all | bytes 131072 | tf_op jit(solution)/shard_map/all_to_all | solution.py:128
  209.4 1.1 broadcast_in_dim.15
  210.5 5.3 %all-to-all-start.6 = ((f32[16,32,512]{2,1,0:T(8,128)}), f32[16,32,512]{2,1,0:T(8,128)S(1)}, u32[]{:S(2)}, u32[]{:S(2)}) async-start(f32[16,32,512]{2,1,0:T(8,128)} %broadcast_in_dim.15), calls=%async_computation.6 | async-start | bytes 2097152 | tf_op jit(solution)/shard_map/all_to_all | solution.py:128
  215.8 0.0 copy-done.3
  215.9 0.6 fusion.5.target_ids
  216.4 21.9 %all-to-all-done.6 = f32[16,32,512]{2,1,0:T(8,128)S(1)} async-done(((f32[16,32,512]{2,1,0:T(8,128)}), f32[16,32,512]{2,1,0:T(8,128)S(1)}, u32[]{:S(2)}, u32[]{:S(2)}) %all-to-all-start.6) | async-done | bytes 1048608 | tf_op jit(solution)/shard_map/all_to_all | solution.py:128
  238.4 0.0 copy-start.1
  238.4 0.0 all-gather.5.cloned.1.call-done.refs_0_.refs_1_.refs_2_.refs_3_.refs_4_.refs_5_.refs_6_.refs_7_
  238.4 10.9 %shard_map.95 = bf16[4096,512]{1,0:T(8,128)(2,1)} custom-call(s32[32]{0:T(128)} %bitcast.35, s32[32]{0:T(128)} %fusion.5.target_ids, s32[1]{0:T(128)} %bitcast.25.live, bf16[32,128,128]{2,1,0:T(8,128)(2,1)} %bitcast.29, bf16[4096,512]{1,0:T(8,128)(2,1)} %all-gather.5.cloned.1.call-done.refs_0_.refs_1_.refs_2_.refs_3_.refs_4_.refs_5_.refs_6_.refs_7_, ...), custom_call_target="tpu_custom_call" | custom-call | tf_op jit(solution)/shard_map/pallas_call | solution.py:89
  249.2 0.0 copy-done.1
  249.2 12.7 %all_to_all.56 = bf16[2,4,2,256,512]{4,3,2,1,0:T(8,128)(2,1)} all-to-all(bf16[2,4,2,256,512]{4,3,2,1,0:T(8,128)(2,1)} %bitcast.26), channel_id=1, replica_groups=mesh['zl'=2,'x'=4,'core'=2,'zh'=4,'y'=4] {'core'}, dimensions={0} | all-to-all | bytes 8388608 | tf_op jit(solution)/shard_map/all_to_all | solution.py:119
  261.9 3.3 %reduce_sum.92 = bf16[4,2,256,512]{3,2,1,0:T(8,128)(2,1)S(1)} reduce(bf16[2,4,2,256,512]{4,3,2,1,0:T(8,128)(2,1)} %all_to_all.56, bf16[]{:T(256)} %constant.102.clone.1), dimensions={0}, to_apply=%region_5.6 | reduce | flops 1048576 | bytes 6291458 | tf_op jit(solution)/shard_map/reduce_sum | solution.py:120
  265.2 32.4 %all_to_all.57 = bf16[4,2,256,512]{3,2,1,0:T(8,128)(2,1)} all-to-all(bf16[4,2,256,512]{3,2,1,0:T(8,128)(2,1)S(1)} %reduce_sum.92), channel_id=1, replica_groups=mesh['zl'=2,'x'=4,'core'=2,'zh'=4,'y'=4] {'x'}, dimensions={0} | all-to-all | bytes 4194304 | tf_op jit(solution)/shard_map/all_to_all | solution.py:119
  297.6 0.0 copy-start.2
  297.6 2.9 reduce_sum.93
  300.5 3.5 %all-to-all-start.9 = ((bf16[2,256,512]{2,1,0:T(8,128)(2,1)}), bf16[2,256,512]{2,1,0:T(8,128)(2,1)S(1)}, u32[]{:S(2)}, u32[]{:S(2)}) async-start(bf16[2,256,512]{2,1,0:T(8,128)(2,1)} %reduce_sum.93), calls=%async_computation.9 | async-start | bytes 1048576 | tf_op jit(solution)/shard_map/all_to_all | solution.py:119
  304.0 7.1 %all-to-all-done.9 = bf16[2,256,512]{2,1,0:T(8,128)(2,1)S(1)} async-done(((bf16[2,256,512]{2,1,0:T(8,128)(2,1)}), bf16[2,256,512]{2,1,0:T(8,128)(2,1)S(1)}, u32[]{:S(2)}, u32[]{:S(2)}) %all-to-all-start.9) | async-done | bytes 524320 | tf_op jit(solution)/shard_map/all_to_all | solution.py:119
  311.1 0.1 reduce_sum.94
  311.2 1.0 convolution_convert_fusion
  312.3 0.0 copy-done.2
  312.3 1.0 copy.24
  (5 shorter events, 0.2 us)
Async XLA Ops:
  7.2 143.7 %copy-start = (bf16[512,512]{1,0:T(8,128)(2,1)S(1)}, bf16[512,512]{1,0:T(8,128)(2,1)}, u32[]{:S(2)}) copy-start(bf16[512,512]{1,0:T(8,128)(2,1)} %param.8) | copy-start | bytes 1572868
  7.2 45.0 %all-gather.3.cloned.1.call-start = ((), (), s32[]{:S(2)}) async-start(), calls=%async_computation.10 | async-start | bytes 4456448 | tf_op jit(solution)/shard_map/all_gather | solution.py:150
  7.9 230.4 %all-gather.5.cloned.1.call-start = ((), (), s32[]{:S(2)}) async-start(), calls=%async_computation.11 | async-start | bytes 4456448 | tf_op jit(solution)/shard_map/all_gather | solution.py:169
  117.8 33.0 %copy-start.4 = (bf16[256,512]{1,0:T(8,128)(2,1)S(1)}, bf16[256,512]{1,0:T(8,128)(2,1)}, u32[]{:S(2)}) copy-start(bf16[256,512]{1,0:T(8,128)(2,1)} %param.13) | copy-start | bytes 786436
  153.7 62.2 %copy-start.3 = (s32[1,1,32]{2,1,0:T(1,128)S(1)}, s32[1,1,32]{2,1,0:T(1,128)}, u32[]{:S(2)}) copy-start(s32[1,1,32]{2,1,0:T(1,128)} %param.11) | copy-start | bytes 388
  210.5 27.8 %all-to-all-start.6 = ((f32[16,32,512]{2,1,0:T(8,128)}), f32[16,32,512]{2,1,0:T(8,128)S(1)}, u32[]{:S(2)}, u32[]{:S(2)}) async-start(f32[16,32,512]{2,1,0:T(8,128)} %broadcast_in_dim.15), calls=%async_computation.6 | async-start | bytes 2097152 | tf_op jit(solution)/shard_map/all_to_all | solution.py:128
  238.4 10.9 %copy-start.1 = (f32[16,32,512]{2,1,0:T(8,128)}, f32[16,32,512]{2,1,0:T(8,128)S(1)}, u32[]{:S(2)}) copy-start(f32[16,32,512]{2,1,0:T(8,128)S(1)} %all-to-all-done.6) | copy-start | bytes 3145732
  297.6 14.7 %copy-start.2 = (f32[16,32,512]{2,1,0:T(8,128)S(1)}, f32[16,32,512]{2,1,0:T(8,128)}, u32[]{:S(2)}) copy-start(f32[16,32,512]{2,1,0:T(8,128)} %copy-done.1) | copy-start | bytes 3145732
  300.5 10.6 %all-to-all-start.9 = ((bf16[2,256,512]{2,1,0:T(8,128)(2,1)}), bf16[2,256,512]{2,1,0:T(8,128)(2,1)S(1)}, u32[]{:S(2)}, u32[]{:S(2)}) async-start(bf16[2,256,512]{2,1,0:T(8,128)(2,1)} %reduce_sum.93), calls=%async_computation.9 | async-start | bytes 1048576 | tf_op jit(solution)/shard_map/all_to_all | solution.py:119
Sparse Core Ops, SparseCore 0:
  9.8 42.3 all-gather.2
  152.3 81.9 all-gather.4

commit v14 on v13

--- a/solution.py
+++ b/solution.py
@@ -165,7 +165,11 @@
     on_chip = lax.all_to_all(on_chip, ROW[2], 0, 0, tiled=False).sum(0)
     weight_part = exchange_sum(on_chip.reshape((-1, weight_term.shape[1])), ROW[:2], row_count // row_sizes[2])
     weight_part = exchange_sum(weight_part, COL, col_count)
-    grad_weight = exchange_gather(exchange_gather(weight_part, COL, col_count), ROW, row_count)
+    weight_rows = exchange_gather(weight_part, COL, col_count)
+    chip_rows = exchange_gather(weight_rows, ROW[:2], row_count // row_sizes[2])
+    both_cores = exchange_gather(chip_rows[None], ROW[2], row_sizes[2])
+    both_cores = both_cores.reshape((row_sizes[2], row_sizes[0], row_sizes[1]) + weight_rows.shape)
+    grad_weight = jnp.moveaxis(both_cores, 0, 2).reshape((-1, weight_rows.shape[1]))
     upstream = lax.all_gather(own_upstream, COL, axis=0, tiled=True)
     upstream, grad_weight = lax.optimization_barrier((upstream, grad_weight))
     backward_terms = block_terms(

time: 322 us -> 317 us (0.984)
  waiting for transfers between devices: 72.1 us -> 60.4 us
  blocking collectives: 186 us -> 195 us
  starting transfers between devices: 8.89 us -> 4.73 us
    all_to_all x1 -> x0, waiting for transfers between devices: 7.1 us -> none  [staged_sum(): pieces = lax.all_to_all(pieces, name, 0, 0, tiled=False)]
    all_to_all x4 -> x5, blocking collectives: 130 us -> 137 us  [staged_sum(): pieces = lax.all_to_all(pieces, name, 0, 0, tiled=False)]
    all_to_all x1, waiting for transfers between devices: 21.9 us -> 17.3 us  [exchange_gather(): pieces = lax.all_to_all(pieces, axis_name, 0, 0, tiled=False)]
    all_to_all x1 -> x2, blocking collectives: 14.3 us -> 18.7 us  [exchange_gather(): pieces = lax.all_to_all(pieces, axis_name, 0, 0, tiled=False)]
    all_to_all x1 -> x0, starting transfers between devices: 3.49 us -> none  [staged_sum(): pieces = lax.all_to_all(pieces, name, 0, 0, tiled=False)]
  transfers between devices with their start and end apart: 4 -> 3, of which waited for: 3 -> 2; matrix products, arithmetic and copies ran while one was open for 1% -> 2% of each run, Pallas kernels for 0% -> 0%
where the time goes in v14:
time: 317 us; the launch traced here: 315 us
  blocking collectives  195 us (62%)
  waiting for transfers between devices  60.4 us (19%)
  Pallas kernels  23.2 us (7%)
  between operations  14.8 us (5%)
  other arithmetic  10.7 us (3%)
  starting transfers between devices  4.73 us (1%)
  matrix products  3.55 us (1%)
    all_to_all x5, blocking collectives, staged_sum(): pieces = lax.all_to_all(pieces, name, 0, 0, tiled=False)  137 us
    all_gather x1, waiting for transfers between devices, shards(): panel = lax.all_gather(features, ROW, axis=0, tiled=True)  42.4 us
    all_to_all x2, blocking collectives, exchange_sum(): pieces = lax.all_to_all(pieces, axis_name, 0, 0, tiled=False)  34.9 us
    pallas_call x2, Pallas kernels, block_terms(): pl.pallas_call(functools.partial(block_kernel, transpose=transpose), grid...  23.2 us
    all_to_all x2, blocking collectives, exchange_gather(): pieces = lax.all_to_all(pieces, axis_name, 0, 0, tiled=False)  18.7 us
    all_to_all x1, waiting for transfers between devices, exchange_gather(): pieces = lax.all_to_all(pieces, axis_name, 0, 0, tiled=False)  17.3 us
    reduce_sum x5, other arithmetic, staged_sum(): pieces = pieces.astype(jnp.float32).sum(0)  8.8 us
  transfers between devices with their start and end apart: 3, of which 2 were waited for; matrix products, arithmetic and copies ran while one was open for 2% of the time, Pallas kernels for 0%

profile of v14, /device:TPU:2, one launch (start us, length us, event | category | flops | bytes accessed | tf_op | source)
XLA Modules:
  0.0 314.6 jit_solution(34547415310371628)
XLA Ops:
  7.2 0.0 copy-start
  7.2 0.0 all-gather.3.cloned.1.call-start
  7.2 0.7 all-gather.3.cloned.1.call-update
  7.9 0.0 all-gather.5.cloned.1.call-start
  8.6 1.2 fusion.2.target_ids
  9.8 42.4 %all-gather.3.cloned.1.call-done.refs_0_.refs_1_.refs_2_.refs_3_.refs_4_.refs_5_.refs_6_.refs_7_ = bf16[4096,512]{1,0:T(8,128)(2,1)} async-done(((bf16[256,512]{1,0:T(8,128)(2,1)}), bf16[4096,512]{1,0:T(8,128)(2,1)}) %all-gather.3.cloned.1.call-update) | async-done | bytes 4194320 | tf_op jit(solution)/shard_map/all_gather | solution.py:150
  52.2 11.1 %shard_map.94 = bf16[4096,512]{1,0:T(8,128)(2,1)} custom-call(s32[32]{0:T(128)} %bitcast.40, s32[32]{0:T(128)} %fusion.2.target_ids, s32[1]{0:T(128)} %bitcast.28.live, bf16[32,128,128]{2,1,0:T(8,128)(2,1)} %bitcast.32, bf16[4096,512]{1,0:T(8,128)(2,1)} %all-gather.3.cloned.1.call-done.refs_0_.refs_1_.refs_2_.refs_3_.refs_4_.refs_5_.refs_6_.refs_7_, ...), custom_call_target="tpu_custom_call" | custom-call | tf_op jit(solution)/shard_map/pallas_call | solution.py:89
  63.3 52.1 %all_to_all.55 = bf16[4,4,256,512]{3,2,1,0:T(8,128)(2,1)} all-to-all(bf16[4,4,256,512]{3,2,1,0:T(8,128)(2,1)} %bitcast.31), channel_id=1, replica_groups=mesh['zl'=2,'x'=4,'core'=2,'zh'=4,'y'=4] {'y'}, dimensions={0} | all-to-all | bytes 8388608 | tf_op jit(solution)/shard_map/all_to_all | solution.py:119
  115.4 0.0 copy-start.2
  115.4 3.1 reduce_sum.87
  118.4 33.6 %all_to_all.56 = bf16[4,256,512]{2,1,0:T(8,128)(2,1)S(1)} all-to-all(bf16[4,256,512]{2,1,0:T(8,128)(2,1)S(1)} %reduce_sum.87), channel_id=1, replica_groups=mesh['zl'=2,'x'=4,'core'=2,'zh'=4,'y'=4] {'zh'}, dimensions={0} | all-to-all | bytes 2097152 | tf_op jit(solution)/shard_map/all_to_all | solution.py:119
  152.0 0.2 reduce_sum.88
  152.3 0.0 copy-done
  152.3 0.0 copy-done.2
  152.3 1.3 multiply_convert_fusion
  153.5 0.0 all-gather.5.cloned.1.call-update
  153.6 0.1 copy.21
  153.7 1.2 convolution_bitcast_fusion
  155.0 0.1 copy.22
  155.1 0.0 copy-start.1
  155.1 4.6 %all_to_all.57 = f32[2,2,4,32,512]{4,3,2,1,0:T(8,128)S(1)} all-to-all(f32[2,2,4,32,512]{4,3,2,1,0:T(8,128)S(1)} %copy.22), channel_id=1, replica_groups=mesh['zl'=2,'x'=4,'core'=2,'zh'=4,'y'=4] {'core'}, dimensions={0} | all-to-all | bytes 2097152 | tf_op jit(solution)/shard_map/all_to_all | solution.py:165
  159.6 0.1 reduce_sum.89
  159.8 18.4 %all_to_all.58 = f32[8,32,512]{2,1,0:T(8,128)S(1)} all-to-all(f32[8,32,512]{2,1,0:T(8,128)S(1)} %bitcast.36), channel_id=1, replica_groups=mesh['zl'=2,'x'=4,'core'=2,'zh'=4,'y'=4] {'zl','x'}, dimensions={0} | all-to-all | bytes 1048576 | tf_op jit(solution)/shard_map/all_to_all | solution.py:103
  178.2 16.6 %all_to_all.59 = f32[16,2,512]{2,1,0:T(2,128)S(1)} all-to-all(f32[16,2,512]{2,1,0:T(2,128)S(1)} %reshape.26), channel_id=1, replica_groups=mesh['zl'=2,'x'=4,'core'=2,'zh'=4,'y'=4] {'zh','y'}, dimensions={0} | all-to-all | bytes 131072 | tf_op jit(solution)/shard_map/all_to_all | solution.py:103
  194.9 14.2 %all_to_all.60 = f32[16,2,512]{2,1,0:T(2,128)S(1)} all-to-all(f32[16,2,512]{2,1,0:T(2,128)S(1)} %broadcast_in_dim.20), channel_id=1, replica_groups=mesh['zl'=2,'x'=4,'core'=2,'zh'=4,'y'=4] {'zh','y'}, dimensions={0} | all-to-all | bytes 131072 | tf_op jit(solution)/shard_map/all_to_all | solution.py:128
  209.1 0.9 broadcast_in_dim.22
  209.9 4.7 %all-to-all-start.6 = ((f32[8,32,512]{2,1,0:T(8,128)}), f32[8,32,512]{2,1,0:T(8,128)S(1)}, u32[]{:S(2)}, u32[]{:S(2)}) async-start(f32[8,32,512]{2,1,0:T(8,128)} %broadcast_in_dim.22), calls=%async_computation.6 | async-start | bytes 1048576 | tf_op jit(solution)/shard_map/all_to_all | solution.py:128
  214.6 0.0 copy-done.1
  214.6 0.6 fusion.5.target_ids
  215.1 17.3 %all-to-all-done.6 = f32[8,32,512]{2,1,0:T(8,128)S(1)} async-done(((f32[8,32,512]{2,1,0:T(8,128)}), f32[8,32,512]{2,1,0:T(8,128)S(1)}, u32[]{:S(2)}, u32[]{:S(2)}) %all-to-all-start.6) | async-done | bytes 524320 | tf_op jit(solution)/shard_map/all_to_all | solution.py:128
  232.4 0.1 broadcast_in_dim.24
  232.5 4.6 %all_to_all.61 = f32[2,1,256,512]{3,2,1,0:T(8,128)S(1)} all-to-all(f32[2,1,256,512]{3,2,1,0:T(8,128)S(1)} %broadcast_in_dim.24), channel_id=1, replica_groups=mesh['zl'=2,'x'=4,'core'=2,'zh'=4,'y'=4] {'core'}, dimensions={0} | all-to-all | bytes 2097152 | tf_op jit(solution)/shard_map/all_to_all | solution.py:128
  237.1 1.1 copy.24
  238.2 0.0 all-gather.5.cloned.1.call-done.refs_0_.refs_1_.refs_2_.refs_3_.refs_4_.refs_5_.refs_6_.refs_7_
  238.2 12.2 %shard_map.95 = bf16[4096,512]{1,0:T(8,128)(2,1)} custom-call(s32[32]{0:T(128)} %bitcast.41, s32[32]{0:T(128)} %fusion.5.target_ids, s32[1]{0:T(128)} %bitcast.29.live, bf16[32,128,128]{2,1,0:T(8,128)(2,1)} %bitcast.33, bf16[4096,512]{1,0:T(8,128)(2,1)} %all-gather.5.cloned.1.call-done.refs_0_.refs_1_.refs_2_.refs_3_.refs_4_.refs_5_.refs_6_.refs_7_, ...), custom_call_target="tpu_custom_call" | custom-call | tf_op jit(solution)/shard_map/pallas_call | solution.py:89
  250.4 11.9 %all_to_all.62 = bf16[2,4,2,256,512]{4,3,2,1,0:T(8,128)(2,1)} all-to-all(bf16[2,4,2,256,512]{4,3,2,1,0:T(8,128)(2,1)} %bitcast.30), channel_id=1, replica_groups=mesh['zl'=2,'x'=4,'core'=2,'zh'=4,'y'=4] {'core'}, dimensions={0} | all-to-all | bytes 8388608 | tf_op jit(solution)/shard_map/all_to_all | solution.py:119
  262.2 3.3 %reduce_sum.92 = bf16[4,2,256,512]{3,2,1,0:T(8,128)(2,1)S(1)} reduce(bf16[2,4,2,256,512]{4,3,2,1,0:T(8,128)(2,1)} %all_to_all.62, bf16[]{:T(256)} %constant.102.clone.1), dimensions={0}, to_apply=%region_5.6 | reduce | flops 1048576 | bytes 6291458 | tf_op jit(solution)/shard_map/reduce_sum | solution.py:120
  265.6 29.5 %all_to_all.63 = bf16[4,2,256,512]{3,2,1,0:T(8,128)(2,1)} all-to-all(bf16[4,2,256,512]{3,2,1,0:T(8,128)(2,1)S(1)} %reduce_sum.92), channel_id=1, replica_groups=mesh['zl'=2,'x'=4,'core'=2,'zh'=4,'y'=4] {'x'}, dimensions={0} | all-to-all | bytes 4194304 | tf_op jit(solution)/shard_map/all_to_all | solution.py:119
  295.0 2.1 reduce_sum.93
  297.1 9.5 %all_to_all.64 = bf16[2,256,512]{2,1,0:T(8,128)(2,1)S(1)} all-to-all(bf16[2,256,512]{2,1,0:T(8,128)(2,1)S(1)} %reduce_sum.93), channel_id=1, replica_groups=mesh['zl'=2,'x'=4,'core'=2,'zh'=4,'y'=4] {'zl'}, dimensions={0} | all-to-all | bytes 1048576 | tf_op jit(solution)/shard_map/all_to_all | solution.py:119
  306.6 0.1 reduce_sum.94
  306.7 1.0 convolution_convert_fusion
  (5 shorter events, 0.2 us)
Async XLA Ops:
  7.2 145.1 %copy-start = (bf16[512,512]{1,0:T(8,128)(2,1)S(1)}, bf16[512,512]{1,0:T(8,128)(2,1)}, u32[]{:S(2)}) copy-start(bf16[512,512]{1,0:T(8,128)(2,1)} %param.8) | copy-start | bytes 1572868
  7.2 45.0 %all-gather.3.cloned.1.call-start = ((), (), s32[]{:S(2)}) async-start(), calls=%async_computation.11 | async-start | bytes 4456448 | tf_op jit(solution)/shard_map/all_gather | solution.py:150
  7.9 230.3 %all-gather.5.cloned.1.call-start = ((), (), s32[]{:S(2)}) async-start(), calls=%async_computation.12 | async-start | bytes 4456448 | tf_op jit(solution)/shard_map/all_gather | solution.py:173
  115.4 36.9 %copy-start.2 = (bf16[256,512]{1,0:T(8,128)(2,1)S(1)}, bf16[256,512]{1,0:T(8,128)(2,1)}, u32[]{:S(2)}) copy-start(bf16[256,512]{1,0:T(8,128)(2,1)} %param.13) | copy-start | bytes 786436
  155.1 59.5 %copy-start.1 = (s32[1,1,32]{2,1,0:T(1,128)S(1)}, s32[1,1,32]{2,1,0:T(1,128)}, u32[]{:S(2)}) copy-start(s32[1,1,32]{2,1,0:T(1,128)} %param.11) | copy-start | bytes 388
  209.9 22.5 %all-to-all-start.6 = ((f32[8,32,512]{2,1,0:T(8,128)}), f32[8,32,512]{2,1,0:T(8,128)S(1)}, u32[]{:S(2)}, u32[]{:S(2)}) async-start(f32[8,32,512]{2,1,0:T(8,128)} %broadcast_in_dim.22), calls=%async_computation.6 | async-start | bytes 1048576 | tf_op jit(solution)/shard_map/all_to_all | solution.py:128
Sparse Core Ops, SparseCore 0:
  9.8 42.3 all-gather.2
  153.7 81.3 all-gather.4

commit v15 on v14

--- a/solution.py
+++ b/solution.py
@@ -149,6 +149,7 @@
     col_span = row_count * local_rows
     panel = lax.all_gather(features, ROW, axis=0, tiled=True)
     parts_per_device = local_rows // block_side
+    chip_sizes = [row_sizes[0] * row_sizes[1], row_sizes[2]]
     forward_terms = block_terms(
         values, col_ids, reversed_blocks(row_ids, col_sizes, parts_per_device), live_count,
         panel, row_span // block_side, False
@@ -173,10 +174,10 @@
     upstream = lax.all_gather(own_upstream, COL, axis=0, tiled=True)
     upstream, grad_weight = lax.optimization_barrier((upstream, grad_weight))
     backward_terms = block_terms(
-        values, row_ids, reversed_blocks(col_ids, row_sizes, parts_per_device), live_count,
+        values, row_ids, reversed_blocks(col_ids, chip_sizes, parts_per_device), live_count,
         upstream, col_span // block_side, True
     )
-    grad_projected = staged_sum(backward_terms, ROW, row_sizes).astype(jnp.bfloat16)
+    grad_projected = staged_sum(backward_terms, (ROW[:2], ROW[2]), chip_sizes).astype(jnp.bfloat16)
     grad_features = lax.dot_general(
         grad_projected, weight, (((1,), (1,)), ((), ())), preferred_element_type=jnp.float32
     ).astype(jnp.bfloat16)

time: 317 us -> 308 us (0.972)
  blocking collectives: 195 us -> 188 us
    all_to_all x5 -> x4, blocking collectives: 137 us -> 129 us  [staged_sum(): pieces = lax.all_to_all(pieces, name, 0, 0, tiled=False)]
    reduce_sum x5 -> x4, other arithmetic: 8.8 us -> 8.59 us  [staged_sum(): pieces = pieces.astype(jnp.float32).sum(0)]
where the time goes in v15:
time: 308 us; the launch traced here: 305 us
  blocking collectives  188 us (61%)
  waiting for transfers between devices  60.3 us (20%)
  Pallas kernels  20.9 us (7%)
  between operations  14.8 us (5%)
  other arithmetic  10.5 us (3%)
  starting transfers between devices  4.89 us (2%)
  matrix products  3.55 us (1%)
    all_to_all x4, blocking collectives, staged_sum(): pieces = lax.all_to_all(pieces, name, 0, 0, tiled=False)  129 us
    all_gather x1, waiting for transfers between devices, shards(): panel = lax.all_gather(features, ROW, axis=0, tiled=True)  42.4 us
    all_to_all x2, blocking collectives, exchange_sum(): pieces = lax.all_to_all(pieces, axis_name, 0, 0, tiled=False)  35.3 us
    pallas_call x2, Pallas kernels, block_terms(): pl.pallas_call(functools.partial(block_kernel, transpose=transpose), grid...  20.9 us
    all_to_all x2, blocking collectives, exchange_gather(): pieces = lax.all_to_all(pieces, axis_name, 0, 0, tiled=False)  19 us
    all_to_all x1, waiting for transfers between devices, exchange_gather(): pieces = lax.all_to_all(pieces, axis_name, 0, 0, tiled=False)  17.2 us
    reduce_sum x4, other arithmetic, staged_sum(): pieces = pieces.astype(jnp.float32).sum(0)  8.59 us
  transfers between devices with their start and end apart: 3, of which 2 were waited for; matrix products, arithmetic and copies ran while one was open for 2% of the time, Pallas kernels for 0%

profile of v15, /device:TPU:2, one launch (start us, length us, event | category | flops | bytes accessed | tf_op | source)
XLA Modules:
  0.0 304.9 jit_solution(2563445002255950129)
XLA Ops:
  7.2 0.0 copy-start
  7.2 0.0 all-gather.3.cloned.1.call-start
  7.2 0.7 all-gather.3.cloned.1.call-update
  7.9 0.0 all-gather.5.cloned.1.call-start
  8.6 1.2 fusion.2.target_ids
  9.8 42.4 %all-gather.3.cloned.1.call-done.refs_0_.refs_1_.refs_2_.refs_3_.refs_4_.refs_5_.refs_6_.refs_7_ = bf16[4096,512]{1,0:T(8,128)(2,1)} async-done(((bf16[256,512]{1,0:T(8,128)(2,1)}), bf16[4096,512]{1,0:T(8,128)(2,1)}) %all-gather.3.cloned.1.call-update) | async-done | bytes 4194320 | tf_op jit(solution)/shard_map/all_gather | solution.py:150
  52.2 9.9 %shard_map.94 = bf16[4096,512]{1,0:T(8,128)(2,1)} custom-call(s32[32]{0:T(128)} %bitcast.40, s32[32]{0:T(128)} %fusion.2.target_ids, s32[1]{0:T(128)} %bitcast.28.live, bf16[32,128,128]{2,1,0:T(8,128)(2,1)} %bitcast.32, bf16[4096,512]{1,0:T(8,128)(2,1)} %all-gather.3.cloned.1.call-done.refs_0_.refs_1_.refs_2_.refs_3_.refs_4_.refs_5_.refs_6_.refs_7_, ...), custom_call_target="tpu_custom_call" | custom-call | tf_op jit(solution)/shard_map/pallas_call | solution.py:89
  62.1 52.4 %all_to_all.50 = bf16[4,4,256,512]{3,2,1,0:T(8,128)(2,1)} all-to-all(bf16[4,4,256,512]{3,2,1,0:T(8,128)(2,1)} %bitcast.31), channel_id=1, replica_groups=mesh['zl'=2,'x'=4,'core'=2,'zh'=4,'y'=4] {'y'}, dimensions={0} | all-to-all | bytes 8388608 | tf_op jit(solution)/shard_map/all_to_all | solution.py:119
  114.5 0.0 copy-start.2
  114.5 3.1 %reduce_sum.75 = bf16[4,256,512]{2,1,0:T(8,128)(2,1)S(1)} reduce(bf16[4,4,256,512]{3,2,1,0:T(8,128)(2,1)} %all_to_all.50, bf16[]{:T(256)} %constant.94.clone.1), dimensions={0}, to_apply=%region_0.1 | reduce | flops 1572864 | bytes 5242882 | tf_op jit(solution)/shard_map/reduce_sum | solution.py:120
  117.6 33.8 %all_to_all.51 = bf16[4,256,512]{2,1,0:T(8,128)(2,1)S(1)} all-to-all(bf16[4,256,512]{2,1,0:T(8,128)(2,1)S(1)} %reduce_sum.75), channel_id=1, replica_groups=mesh['zl'=2,'x'=4,'core'=2,'zh'=4,'y'=4] {'zh'}, dimensions={0} | all-to-all | bytes 2097152 | tf_op jit(solution)/shard_map/all_to_all | solution.py:119
  151.4 0.2 reduce_sum.76
  151.6 0.0 copy-done
  151.6 0.0 copy-done.2
  151.6 1.3 multiply_convert_fusion
  152.9 0.0 all-gather.5.cloned.1.call-update
  152.9 0.1 copy.21
  153.1 1.2 convolution_bitcast_fusion
  154.3 0.1 copy.22
  154.4 0.0 copy-start.1
  154.4 4.6 %all_to_all.52 = f32[2,2,4,32,512]{4,3,2,1,0:T(8,128)S(1)} all-to-all(f32[2,2,4,32,512]{4,3,2,1,0:T(8,128)S(1)} %copy.22), channel_id=1, replica_groups=mesh['zl'=2,'x'=4,'core'=2,'zh'=4,'y'=4] {'core'}, dimensions={0} | all-to-all | bytes 2097152 | tf_op jit(solution)/shard_map/all_to_all | solution.py:166
  159.0 0.1 reduce_sum.77
  159.1 17.7 %all_to_all.53 = f32[8,32,512]{2,1,0:T(8,128)S(1)} all-to-all(f32[8,32,512]{2,1,0:T(8,128)S(1)} %bitcast.36), channel_id=1, replica_groups=mesh['zl'=2,'x'=4,'core'=2,'zh'=4,'y'=4] {'zl','x'}, dimensions={0} | all-to-all | bytes 1048576 | tf_op jit(solution)/shard_map/all_to_all | solution.py:103
  176.9 17.6 %all_to_all.54 = f32[16,2,512]{2,1,0:T(2,128)S(1)} all-to-all(f32[16,2,512]{2,1,0:T(2,128)S(1)} %reshape.26), channel_id=1, replica_groups=mesh['zl'=2,'x'=4,'core'=2,'zh'=4,'y'=4] {'zh','y'}, dimensions={0} | all-to-all | bytes 131072 | tf_op jit(solution)/shard_map/all_to_all | solution.py:103
  194.6 14.5 %all_to_all.55 = f32[16,2,512]{2,1,0:T(2,128)S(1)} all-to-all(f32[16,2,512]{2,1,0:T(2,128)S(1)} %broadcast_in_dim.20), channel_id=1, replica_groups=mesh['zl'=2,'x'=4,'core'=2,'zh'=4,'y'=4] {'zh','y'}, dimensions={0} | all-to-all | bytes 131072 | tf_op jit(solution)/shard_map/all_to_all | solution.py:128
  209.1 0.9 broadcast_in_dim.22
  210.0 4.8 %all-to-all-start.6 = ((f32[8,32,512]{2,1,0:T(8,128)}), f32[8,32,512]{2,1,0:T(8,128)S(1)}, u32[]{:S(2)}, u32[]{:S(2)}) async-start(f32[8,32,512]{2,1,0:T(8,128)} %broadcast_in_dim.22), calls=%async_computation.6 | async-start | bytes 1048576 | tf_op jit(solution)/shard_map/all_to_all | solution.py:128
  214.8 0.0 copy-done.1
  214.8 0.6 fusion.4.target_ids
  215.3 17.2 %all-to-all-done.6 = f32[8,32,512]{2,1,0:T(8,128)S(1)} async-done(((f32[8,32,512]{2,1,0:T(8,128)}), f32[8,32,512]{2,1,0:T(8,128)S(1)}, u32[]{:S(2)}, u32[]{:S(2)}) %all-to-all-start.6) | async-done | bytes 524320 | tf_op jit(solution)/shard_map/all_to_all | solution.py:128
  232.5 0.1 broadcast_in_dim.24
  232.6 4.6 %all_to_all.56 = f32[2,1,256,512]{3,2,1,0:T(8,128)S(1)} all-to-all(f32[2,1,256,512]{3,2,1,0:T(8,128)S(1)} %broadcast_in_dim.24), channel_id=1, replica_groups=mesh['zl'=2,'x'=4,'core'=2,'zh'=4,'y'=4] {'core'}, dimensions={0} | all-to-all | bytes 2097152 | tf_op jit(solution)/shard_map/all_to_all | solution.py:128
  237.2 1.1 copy.24
  238.3 0.0 all-gather.5.cloned.1.call-done.refs_0_.refs_1_.refs_2_.refs_3_.refs_4_.refs_5_.refs_6_.refs_7_
  238.3 10.9 %shard_map.95 = bf16[4096,512]{1,0:T(8,128)(2,1)} custom-call(s32[32]{0:T(128)} %bitcast.41, s32[32]{0:T(128)} %fusion.4.target_ids, s32[1]{0:T(128)} %bitcast.29.live, bf16[32,128,128]{2,1,0:T(8,128)(2,1)} %bitcast.33, bf16[4096,512]{1,0:T(8,128)(2,1)} %all-gather.5.cloned.1.call-done.refs_0_.refs_1_.refs_2_.refs_3_.refs_4_.refs_5_.refs_6_.refs_7_, ...), custom_call_target="tpu_custom_call" | custom-call | tf_op jit(solution)/shard_map/pallas_call | solution.py:89
  249.2 11.9 %all_to_all.57 = bf16[2,8,256,512]{3,2,1,0:T(8,128)(2,1)} all-to-all(bf16[2,8,256,512]{3,2,1,0:T(8,128)(2,1)} %bitcast.30), channel_id=1, replica_groups=mesh['zl'=2,'x'=4,'core'=2,'zh'=4,'y'=4] {'core'}, dimensions={0} | all-to-all | bytes 8388608 | tf_op jit(solution)/shard_map/all_to_all | solution.py:119
  261.1 3.3 %reduce_sum.80 = bf16[8,256,512]{2,1,0:T(8,128)(2,1)S(1)} reduce(bf16[2,8,256,512]{3,2,1,0:T(8,128)(2,1)} %all_to_all.57, bf16[]{:T(256)} %constant.94.clone.1), dimensions={0}, to_apply=%region_5.6 | reduce | flops 1048576 | bytes 6291458 | tf_op jit(solution)/shard_map/reduce_sum | solution.py:120
  264.4 30.6 %all_to_all.58 = bf16[8,256,512]{2,1,0:T(8,128)(2,1)} all-to-all(bf16[8,256,512]{2,1,0:T(8,128)(2,1)S(1)} %reduce_sum.80), channel_id=1, replica_groups=mesh['zl'=2,'x'=4,'core'=2,'zh'=4,'y'=4] {'zl','x'}, dimensions={0} | all-to-all | bytes 4194304 | tf_op jit(solution)/shard_map/all_to_all | solution.py:119
  295.0 2.0 reduce_sum.81
  297.0 1.0 convolution_convert_fusion
  (5 shorter events, 0.2 us)
Async XLA Ops:
  7.2 144.4 %copy-start = (bf16[512,512]{1,0:T(8,128)(2,1)S(1)}, bf16[512,512]{1,0:T(8,128)(2,1)}, u32[]{:S(2)}) copy-start(bf16[512,512]{1,0:T(8,128)(2,1)} %param.8) | copy-start | bytes 1572868
  7.2 45.0 %all-gather.3.cloned.1.call-start = ((), (), s32[]{:S(2)}) async-start(), calls=%async_computation.10 | async-start | bytes 4456448 | tf_op jit(solution)/shard_map/all_gather | solution.py:150
  7.9 230.4 %all-gather.5.cloned.1.call-start = ((), (), s32[]{:S(2)}) async-start(), calls=%async_computation.11 | async-start | bytes 4456448 | tf_op jit(solution)/shard_map/all_gather | solution.py:174
  114.5 37.1 %copy-start.2 = (bf16[256,512]{1,0:T(8,128)(2,1)S(1)}, bf16[256,512]{1,0:T(8,128)(2,1)}, u32[]{:S(2)}) copy-start(bf16[256,512]{1,0:T(8,128)(2,1)} %param.13) | copy-start | bytes 786436
  154.4 60.4 %copy-start.1 = (s32[1,1,32]{2,1,0:T(1,128)S(1)}, s32[1,1,32]{2,1,0:T(1,128)}, u32[]{:S(2)}) copy-start(s32[1,1,32]{2,1,0:T(1,128)} %param.11) | copy-start | bytes 388
  210.0 22.5 %all-to-all-start.6 = ((f32[8,32,512]{2,1,0:T(8,128)}), f32[8,32,512]{2,1,0:T(8,128)S(1)}, u32[]{:S(2)}, u32[]{:S(2)}) async-start(f32[8,32,512]{2,1,0:T(8,128)} %broadcast_in_dim.22), calls=%async_computation.6 | async-start | bytes 1048576 | tf_op jit(solution)/shard_map/all_to_all | solution.py:128
Sparse Core Ops, SparseCore 0:
  9.8 42.3 all-gather.2
  153.0 82.6 all-gather.4
